TPU v7x, 32 devices: a whole 2x2x4 slice. The times are simulated.
32 devices in a mesh: outer: 4 (over z), inner: 8 (over y, x, core).
Axes of the slice: x: 2, y: 2, z: 4, core: 2. Of those that a mesh axis runs over, the one named last changes fastest.
Arguments:
- observations: float32 [2048, 128], P(('outer', 'inner')), may hold values from -18 to 18
- gains: float32 [2048, 128, 128], P(('outer', 'inner')), may hold values from -0.2 to 0.7, as said below
- smoother_gains: float32 [2048, 128, 128], P(('outer', 'inner')), may hold values from -0.2 to 1.05, as said below
- transition: float32 [128, 128], replicated, may hold values from -0.2 to 1.05, as said below
- observation_map: float32 [128, 128], replicated, may hold values from -0.25 to 1.25, as said below
- initial_mean: float32 [128], replicated, may hold values from -12 to 12
Outputs:
- filtered: float32 [2048, 128], P(('outer', 'inner'))
- smoothed: float32 [2048, 128], P(('outer', 'inner'))
Inputs may be any that keep to these rules, and one draw needn't show every extreme that they name: `gains`: each frame's gain is a dense 128 by 128 matrix with entries in this range; nothing else about its structure is promised. `smoother_gains`: each frame's smoother gain is a dense 128 by 128 matrix with entries in this range; nothing else about its structure is promised. `transition`: a dense 128 by 128 matrix. `observation_map`: a dense 128 by 128 matrix.
All inputs are finite; a program needn't handle non-finite values.
Results may differ from a plain program's by a relative error of at most 0.0003.
Values sent between devices are 32-bit elements; how exact they have to be, the bound alone decides.
No kernel may reach another device: no remote copies, remote signals or barrier semaphores. Data moves between devices by JAX's collectives and lax.ppermute only.
A program may use at most 128 MiB of HBM per device.

v0:
```python
import jax
import jax.numpy as jnp
from jax import lax
from jax.sharding import PartitionSpec as P

exact = lax.Precision.HIGHEST
AXES = ("outer", "inner")


def mm(a, b):
    return jnp.matmul(a, b, precision=exact, preferred_element_type=jnp.float32)


def mv(a, v):
    return jnp.einsum("...ij,...j->...i", a, v, precision=exact, preferred_element_type=jnp.float32)


def mv_whole(a, v):
    return jnp.sum(a * v[..., None, :], axis=-1)


def local_pair(mats, vecs, backward):
    count, width = mats.shape[0], mats.shape[-1]
    pm = mats.reshape(count // 2, 2, width, width)
    pv = vecs.reshape(count // 2, 2, width)
    first, second = (1, 0) if backward else (0, 1)
    joined = mm(pm[:, second], pm[:, first])
    partner = jnp.stack((pv[:, 1], pv[:, 0]), axis=1).reshape(count, width)
    crossed = mv_whole(mats, partner).reshape(count // 2, 2, width)
    return joined, crossed[:, second] + pv[:, second]


def pair_up(mats, vecs, backward):
    shape = mats.shape
    pm = mats.reshape(shape[:-3] + (shape[-3] // 2, 2) + shape[-2:])
    pv = vecs.reshape(vecs.shape[:-2] + (vecs.shape[-2] // 2, 2, vecs.shape[-1]))
    first, second = (1, 0) if backward else (0, 1)
    m1, m2 = pm[..., first, :, :], pm[..., second, :, :]
    v1, v2 = pv[..., first, :], pv[..., second, :]
    return mm(m2, m1), mv(m2, v1) + v2


def local_tiers(mats, vecs, backward):
    tiers = [(mats, vecs)]
    while tiers[-1][0].shape[0] > 1:
        tiers.append(local_pair(tiers[-1][0], tiers[-1][1], backward))
    return tiers


def spread(tiers, entry, backward):
    width = entry.shape[0]
    states = entry[None, :]
    for height in reversed(range(len(tiers) - 1)):
        mats, vecs = tiers[height]
        half = mats.shape[0] // 2
        pv = vecs.reshape(half, 2, width)
        both = jnp.broadcast_to(states[:, None, :], (half, 2, width)).reshape(-1, width)
        applied = mv_whole(mats, both).reshape(half, 2, width)
        if backward:
            other = applied[:, 1] + pv[:, 1]
            states = jnp.stack((other, states), axis=1)
        else:
            other = applied[:, 0] + pv[:, 0]
            states = jnp.stack((states, other), axis=1)
        states = states.reshape(-1, width)
    return mv_whole(tiers[0][0], states) + tiers[0][1]


def pad_pow2(mats, vecs):
    count = mats.shape[-3]
    size = 1
    while size < count:
        size *= 2
    if size > count:
        width = mats.shape[-1]
        eye = jnp.broadcast_to(
            jnp.eye(width, dtype=mats.dtype), mats.shape[:-3] + (size - count, width, width)
        )
        mats = jnp.concatenate((mats, eye), axis=-3)
        zero = jnp.zeros(vecs.shape[:-2] + (size - count, width), vecs.dtype)
        vecs = jnp.concatenate((vecs, zero), axis=-2)
    return mats, vecs


def reduce_maps(mats, vecs, backward):
    mats, vecs = pad_pow2(mats, vecs)
    while mats.shape[-3] > 1:
        mats, vecs = pair_up(mats, vecs, backward)
    return mats[..., 0, :, :], vecs[..., 0, :]


def keep_only(mats, vecs, keep):
    eye = jnp.eye(mats.shape[-1], dtype=jnp.float32)
    mats = jnp.where(keep[:, None, None], mats, eye)
    vecs = jnp.where(keep[:, None], vecs, 0.0)
    return mats, vecs


def pack(mat, vec):
    return jnp.concatenate((mat, vec[None, :]), axis=0)


def group_level(mat, vec, axis, backward):
    gathered = lax.all_gather(pack(mat, vec), axis)
    mats, vecs = gathered[:, :-1], gathered[:, -1]
    me = lax.axis_index(axis)
    index = jnp.arange(mats.shape[0])
    keep = index > me if backward else index < me
    pm, pv = keep_only(mats, vecs, keep)
    both_m = jnp.stack((pm, mats), axis=0)
    both_v = jnp.stack((pv, vecs), axis=0)
    rm, rv = reduce_maps(both_m, both_v, backward)
    return (rm[0], rv[0]), (rm[1], rv[1])


def across(mat, vec, backward):
    (pm, pv), (gm, gv) = group_level(mat, vec, "inner", backward)
    gathered = lax.all_gather(pack(gm, gv), "outer")
    mats, vecs = gathered[:, :-1], gathered[:, -1]
    me = lax.axis_index("outer")
    index = jnp.arange(mats.shape[0])
    keep = index > me if backward else index < me
    om, ov = reduce_maps(*keep_only(mats, vecs, keep), backward)
    return mm(pm, om), mv(pm, ov) + pv


def on_device(observations, gains, smoother_gains, transition, observation_map, initial_mean):
    me = lax.axis_index(AXES)
    devices = lax.axis_size(AXES)
    mapped = mm(observation_map, transition)
    forward_maps = transition[None] - jnp.einsum(
        "tij,jk->tik", gains, mapped, precision=exact, preferred_element_type=jnp.float32
    )
    forward_inputs = mv_whole(gains, observations)
    forward = local_tiers(forward_maps, forward_inputs, False)
    fm, fv = forward[-1][0][0], forward[-1][1][0]
    before_m, before_v = across(fm, fv, False)
    entry_state = mv(before_m, initial_mean) + before_v
    filtered = spread(forward, entry_state, False)

    predicted_all = jnp.dot(
        filtered, transition.T, precision=exact, preferred_element_type=jnp.float32
    )
    offsets = filtered - mv_whole(smoother_gains, predicted_all)
    backward = local_tiers(smoother_gains, offsets, True)
    bm, bv = backward[-1][0][0], backward[-1][1][0]
    last = me == devices - 1
    extra = jnp.where(last, predicted_all[-1], 0.0)
    bv = bv + mv(bm, extra)
    after_m, after_v = across(bm, bv, True)
    after_state = after_v + extra
    smoothed = spread(backward, after_state, True)
    return (filtered, smoothed)


def solution(mesh):
    in_specs = (
        P(AXES, None),
        P(AXES, None, None),
        P(AXES, None, None),
        P(),
        P(),
        P(),
    )
    out_specs = (P(AXES, None), P(AXES, None))
    return jax.shard_map(
        on_device, mesh=mesh, in_specs=in_specs, out_specs=out_specs, check_vma=False
    )
```

profile of v0, /device:TPU:0, one launch (start us, length us, event | category | flops | bytes accessed | tf_op | source)
XLA Modules:
  0.0 116.3 jit_solution(18187284907825696353)
XLA Ops:
  0.7 3.4 %multiply_reduce_fusion.7 = f32[64,128]{1,0:T(8,128)S(1)} fusion(f32[64,128,128]{2,1,0:T(8,128)} %param.7, f32[64,128]{1,0:T(8,128)} %param.6), kind=kLoop, calls=%fused_computation.8 | loop fusion | flops 2088960 | bytes 4259840 | tf_op jit(solution)/shard_map/reduce_sum | solution.py:19
  4.5 5.9 %multiply_reduce_fusion.6 = (f32[64,128]{1,0:T(8,128)S(1)}, f32[64,128,128]{1,2,0:T(8,128)S(1)}) fusion(f32[64,128]{1,0:T(8,128)S(1)} %bitcast.638, f32[128,128,1]{0,1,2:T(8,128)S(1)} %convolution_bitcast_fusion.4, f32[64,128,128]{2,1,0:T(8,128)} %param.7, f32[128,128]{0,1:T(8,128)S(1)} %copy.373), kind=kOutput, calls=%fused_computation.7 | convolution fusion | flops 1613750272 | bytes 8585216 | tf_op jit(solution)/shard_map/tij,jk->tik/dot_general | solution.py:131
  10.6 2.3 %multiply_reduce_fusion.11 = (f32[32,128]{1,0:T(8,128)S(1)}, f32[32,128,128]{1,2,0:T(8,128)S(1)}) fusion(f32[32,128]{1,0:T(8,128)S(1)} %bitcast.658, f32[32,2,128,128]{2,3,1,0:T(8,128)S(1)} %bitcast.592), kind=kOutput, calls=%fused_computation.18 | convolution fusion | flops 806350848 | bytes 6324224 | tf_op jit(solution)/shard_map/dot_general | solution.py:11
  13.0 1.2 multiply_reduce_fusion.15
  17.1 11.4 %all-gather.4 = f32[8,129,128]{2,1,0:T(8,128)S(1)} all-gather(f32[1,129,128]{2,1,0:T(8,128)S(1)} %maximum_bitcast_fusion), channel_id=2, replica_groups=mesh['outer'=4,'inner'=8] {'inner'}, dimensions={0}, use_global_device_ids=true | all-gather | bytes 594432 | tf_op jit(solution)/shard_map/all_gather | solution.py:104
  28.5 0.8 copy-done.8
  29.4 1.2 fusion.85
  30.6 0.9 fusion.45
  35.0 15.0 %all-gather.5 = f32[4,129,128]{2,1,0:T(8,128)} all-gather(f32[1,129,128]{2,1,0:T(8,128)S(1)} %maximum_bitcast_fusion.1), channel_id=3, replica_groups=mesh['outer'=4,'inner'=8] {'outer'}, dimensions={0}, use_global_device_ids=true | all-gather | bytes 330240 | tf_op jit(solution)/shard_map/all_gather | solution.py:118
  50.0 1.2 %slice_select_fusion.1 = f32[4,128,128]{2,1,0:T(8,128)S(1)} fusion(f32[4,129,128]{2,1,0:T(8,128)} %all-gather.5, f32[128,128]{1,0:T(8,128)S(1)} %fusion.43, pred[4]{0:T(512)(128)(4,1)S(1)} %iota_compare_fusion.3), kind=kLoop, calls=%fused_computation.82 | loop fusion | flops 65536 | bytes 589828 | tf_op jit(solution)/shard_map/jit(_where)/select_n | solution.py:94
  52.8 1.1 fusion.7
  54.1 1.0 fusion.44
  55.1 0.8 fusion.10
  56.0 1.0 multiply_reduce_fusion.26
  58.6 1.3 %multiply_reduce_fusion.18 = f32[8,128]{1,0:T(8,128)S(1)} fusion(f32[8,128,128]{1,2,0:T(8,128)} %copy-done.5, f32[8,128]{1,0:T(8,128)S(1)} %bitcast.696), kind=kLoop, calls=%fused_computation.74 | loop fusion | flops 261120 | bytes 532480 | tf_op jit(solution)/shard_map/reduce_sum | solution.py:19
  61.6 0.9 multiply_reduce_fusion.10
  62.6 1.5 %multiply_reduce_fusion.5 = f32[64,128]{1,0:T(8,128)S(1)} fusion(f32[64,128,128]{1,2,0:T(8,128)S(1)} %copy-done.4, f32[64,128]{1,0:T(8,128)S(1)} %bitcast.642), kind=kLoop, calls=%fused_computation.6 | loop fusion | flops 2088960 | bytes 4259840 | tf_op jit(solution)/shard_map/reduce_sum | solution.py:19
  64.2 1.5 %multiply_reduce_fusion.4 = f32[64,128]{1,0:T(8,128)S(1)} fusion(f32[64,128,128]{1,2,0:T(8,128)S(1)} %copy-done.4, f32[64,128]{1,0:T(8,128)S(1)} %bitcast.639), kind=kLoop, calls=%fused_computation.5 | loop fusion | flops 2088960 | bytes 4259840 | tf_op jit(solution)/shard_map/reduce_sum | solution.py:19
  66.6 1.2 multiply_reduce_fusion.3
  67.9 1.2 multiply_reduce_fusion.2
  69.1 3.9 %multiply_reduce_fusion.9 = (f32[32,128]{1,0:T(8,128)S(1)}, f32[32,128,128]{1,2,0:T(8,128)S(1)}) fusion(f32[32,128]{1,0:T(8,128)S(1)} %bitcast.659, f32[32,2,128,128]{3,2,1,0:T(8,128)S(1)} %bitcast.591), kind=kOutput, calls=%fused_computation.16 | convolution fusion | flops 806350848 | bytes 6324224 | tf_op jit(solution)/shard_map/dot_general | solution.py:11
  73.1 1.2 multiply_reduce_fusion.13
  76.8 0.8 multiply_reduce_fusion.25
  78.2 0.9 fusion.40
  79.1 1.0 fusion.6
  80.2 0.9 maximum_bitcast_fusion.2
  81.1 10.2 %all-gather.6 = f32[8,129,128]{2,1,0:T(8,128)S(1)} all-gather(f32[1,129,128]{2,1,0:T(8,128)S(1)} %maximum_bitcast_fusion.2), channel_id=4, replica_groups=mesh['outer'=4,'inner'=8] {'inner'}, dimensions={0}, use_global_device_ids=true | all-gather | bytes 594432 | tf_op jit(solution)/shard_map/all_gather | solution.py:104
  91.5 0.9 fusion.48
  94.7 14.7 %all-gather.7 = f32[4,129,128]{2,1,0:T(8,128)S(1)} all-gather(f32[1,129,128]{2,1,0:T(8,128)S(1)} %maximum_bitcast_fusion.3), channel_id=5, replica_groups=mesh['outer'=4,'inner'=8] {'outer'}, dimensions={0}, use_global_device_ids=true | all-gather | bytes 330240 | tf_op jit(solution)/shard_map/all_gather | solution.py:118
  110.4 0.9 fusion.11
  113.2 1.2 multiply_reduce_fusion.1
  114.5 1.2 multiply_reduce_fusion
  (225 shorter events, 22.0 us)
Async XLA Ops:
  0.6 3.5 %copy-start = (f32[128,128]{1,0:T(8,128)S(1)}, f32[128,128]{1,0:T(8,128)}, u32[]{:S(2)}) copy-start(f32[128,128]{1,0:T(8,128)} %param.10) | copy-start | bytes 196612
  0.6 3.5 %copy-start.15 = (f32[128,128]{1,0:T(8,128)S(1)}, f32[128,128]{1,0:T(8,128)}, u32[]{:S(2)}) copy-start(f32[128,128]{1,0:T(8,128)} %param.9) | copy-start | bytes 196612
  4.0 6.4 %copy-start.12 = (f32[64,128]{1,0:T(8,128)}, f32[64,128]{1,0:T(8,128)S(1)}, u32[]{:S(2)}) copy-start(f32[64,128]{1,0:T(8,128)S(1)} %multiply_reduce_fusion.7) | copy-start | bytes 98308
  10.5 3.7 %copy-start.3 = (f32[64,128,128]{1,2,0:T(8,128)}, f32[64,128,128]{1,2,0:T(8,128)S(1)}, u32[]{:S(2)}) copy-start(f32[64,128,128]{1,2,0:T(8,128)S(1)} %get-tuple-element.39) | copy-start | bytes 12582916
  12.9 3.5 %copy-start.24 = (f32[16,1,128]{2,1,0:T(1,128)}, f32[16,1,128]{2,1,0:T(1,128)S(1)}, u32[]{:S(2)}) copy-start(f32[16,1,128]{2,1,0:T(1,128)S(1)} %slice_add_fusion.7) | copy-start | bytes 24580
  14.2 2.3 %copy-start.27 = (f32[8,1,128]{2,1,0:T(1,128)}, f32[8,1,128]{2,1,0:T(1,128)S(1)}, u32[]{:S(2)}) copy-start(f32[8,1,128]{2,1,0:T(1,128)S(1)} %slice_add_fusion.11) | copy-start | bytes 12292
  14.9 0.8 copy-start.5
  14.9 1.6 %copy-start.30 = (f32[4,1,128]{2,1,0:T(1,128)}, f32[4,1,128]{2,1,0:T(1,128)S(1)}, u32[]{:S(2)}) copy-start(f32[4,1,128]{2,1,0:T(1,128)S(1)} %slice_add_fusion.15) | copy-start | bytes 6148
  16.4 0.6 copy-start.9
  28.5 0.8 copy-start.8
  34.3 0.7 copy-start.14
  50.0 12.6 %copy-start.4 = (f32[64,128,128]{1,2,0:T(8,128)S(1)}, f32[64,128,128]{1,2,0:T(8,128)}, u32[]{:S(2)}) copy-start(f32[64,128,128]{1,2,0:T(8,128)} %copy-done.3) | copy-start | bytes 12582916
  57.7 6.4 %copy-start.13 = (f32[64,128]{1,0:T(8,128)S(1)}, f32[64,128]{1,0:T(8,128)}, u32[]{:S(2)}) copy-start(f32[64,128]{1,0:T(8,128)} %copy-done.12) | copy-start | bytes 98308
  62.6 3.7 %copy-start.16 = (f32[128,128]{1,0:T(8,128)S(1)}, f32[128,128]{1,0:T(8,128)}, u32[]{:S(2)}) copy-start(f32[128,128]{1,0:T(8,128)} %param.9) | copy-start | bytes 196612
  62.6 3.9 %copy-start.1 = (f32[64,128,128]{2,1,0:T(8,128)S(1)}, f32[64,128,128]{2,1,0:T(8,128)}, u32[]{:S(2)}) copy-start(f32[64,128,128]{2,1,0:T(8,128)} %param.8) | copy-start | bytes 12582916
  66.6 1.2 %copy-start.23 = (f32[64,128]{1,0:T(8,128)}, f32[64,128]{1,0:T(8,128)S(1)}, u32[]{:S(2)}) copy-start(f32[64,128]{1,0:T(8,128)S(1)} %fusion.100) | copy-start | bytes 98308
  67.7 5.3 %copy-start.17 = (f32[64,128]{1,0:T(8,128)}, f32[64,128]{1,0:T(8,128)S(1)}, u32[]{:S(2)}) copy-start(f32[64,128]{1,0:T(8,128)S(1)} %multiply_reduce_fusion.3) | copy-start | bytes 98308
  67.8 5.3 %copy-start.19 = (f32[8,8,128]{2,1,0:T(8,128)}, f32[8,8,128]{2,1,0:T(8,128)S(1)}, u32[]{:S(2)}) copy-start(f32[8,8,128]{2,1,0:T(8,128)S(1)} %add_subtract_fusion) | copy-start | bytes 98308
  73.1 2.0 %copy-start.25 = (f32[16,1,128]{2,1,0:T(1,128)}, f32[16,1,128]{2,1,0:T(1,128)S(1)}, u32[]{:S(2)}) copy-start(f32[16,1,128]{2,1,0:T(1,128)S(1)} %slice_add_fusion.5) | copy-start | bytes 24580
  74.3 0.8 copy-start.28
  75.0 0.8 copy-start.6
  77.6 0.7 copy-start.10
  91.4 19.9 %copy-start.11 = (f32[2,128,128]{1,2,0:T(8,128)S(1)}, f32[2,128,128]{1,2,0:T(8,128)}, u32[]{:S(2)}) copy-start(f32[2,128,128]{1,2,0:T(8,128)} %copy-done.10) | copy-start | bytes 393220
  91.4 20.1 %copy-start.32 = (f32[2,1,128]{2,1,0:T(1,128)S(1)}, f32[2,1,128]{2,1,0:T(1,128)}, u32[]{:S(2)}) copy-start(f32[2,1,128]{2,1,0:T(1,128)} %copy-done.31) | copy-start | bytes 3076
  91.5 20.2 %copy-start.34 = (f32[2,1,128]{2,1,0:T(1,128)S(1)}, f32[2,1,128]{2,1,0:T(1,128)}, u32[]{:S(2)}) copy-start(f32[2,1,128]{2,1,0:T(1,128)} %copy-done.33) | copy-start | bytes 3076
  91.5 20.2 %copy-start.7 = (f32[8,128,128]{1,2,0:T(8,128)S(1)}, f32[8,128,128]{1,2,0:T(8,128)}, u32[]{:S(2)}) copy-start(f32[8,128,128]{1,2,0:T(8,128)} %copy-done.6) | copy-start | bytes 1572868
  91.5 20.4 %copy-start.29 = (f32[8,1,128]{2,1,0:T(1,128)S(1)}, f32[8,1,128]{2,1,0:T(1,128)}, u32[]{:S(2)}) copy-start(f32[8,1,128]{2,1,0:T(1,128)} %copy-done.28) | copy-start | bytes 12292
  92.4 19.9 %copy-start.26 = (f32[16,1,128]{2,1,0:T(1,128)S(1)}, f32[16,1,128]{2,1,0:T(1,128)}, u32[]{:S(2)}) copy-start(f32[16,1,128]{2,1,0:T(1,128)} %copy-done.25) | copy-start | bytes 24580
  93.1 20.1 %copy-start.2 = (f32[64,128,128]{2,1,0:T(8,128)S(1)}, f32[64,128,128]{2,1,0:T(8,128)}, u32[]{:S(2)}) copy-start(f32[64,128,128]{2,1,0:T(8,128)} %param.8) | copy-start | bytes 12582916
  111.5 2.9 %copy-start.20 = (f32[8,8,128]{2,1,0:T(8,128)S(1)}, f32[8,8,128]{2,1,0:T(8,128)}, u32[]{:S(2)}) copy-start(f32[8,8,128]{2,1,0:T(8,128)} %copy-done.19) | copy-start | bytes 98308
  113.2 2.4 %copy-start.18 = (f32[64,128]{1,0:T(8,128)S(1)}, f32[64,128]{1,0:T(8,128)}, u32[]{:S(2)}) copy-start(f32[64,128]{1,0:T(8,128)} %copy-done.17) | copy-start | bytes 98308
  113.2 2.4 %copy-start.22 = (f32[64,128]{1,0:T(8,128)S(1)}, f32[64,128]{1,0:T(8,128)}, u32[]{:S(2)}) copy-start(f32[64,128]{1,0:T(8,128)} %copy-done.21) | copy-start | bytes 98308
  (5 other events, 3.0 us)
where the time goes:
time: 117 us; the launch traced here: 116 us
  blocking collectives  51.2 us (44%)
  matrix products  32.2 us (28%)
  other arithmetic  24.1 us (21%)
  local copies, waits for them, and re-layouts  6.83 us (6%)
  between operations  1.96 us (2%)
    all_gather x2, blocking collectives, across(): gathered = lax.all_gather(pack(gm, gv), 'outer')  29.6 us
    all_gather x2, blocking collectives, group_level(): gathered = lax.all_gather(pack(mat, vec), axis)  21.6 us
    dot_general x23, matrix products, mm(): return jnp.matmul(a, b, precision=exact, preferred_element_type=jnp.float32)  17.7 us
    reduce_sum x17, other arithmetic, mv_whole(): return jnp.sum(a * v[..., None, :], axis=-1)  16.2 us
    dot_general x14, matrix products, mv(): jnp.einsum('...ij,...j->...i', a, v, precision=exact, preferred_element_t...  8.29 us
    dot_general x1, matrix products, on_device(): jnp.einsum('tij,jk->tik', gains, mapped, precision=exact, preferred_eleme...  5.92 us
    unnamed x75, local copies, waits for them, and re-layouts  5.82 us
    add x6, other arithmetic, spread(): other = applied[:, 0] + pv[:, 0]  2.78 us

commit v1 on v0

--- a/solution.py
+++ b/solution.py
@@ -113,14 +113,28 @@
     return (rm[0], rv[0]), (rm[1], rv[1])
 
 
+def from_other_groups(packed, backward):
+    count = lax.axis_size("outer")
+    me = lax.axis_index("outer")
+    received = []
+    keep = []
+    for shift in reversed(range(1, count)):
+        step = -shift if backward else shift
+        pairs = [(i, (i + step) % count) for i in range(count)]
+        received.append(lax.ppermute(packed, "outer", pairs))
+        keep.append(me + shift <= count - 1 if backward else me - shift >= 0)
+    if not received:
+        return None
+    maps = jnp.stack(received)
+    return keep_only(maps[:, :-1], maps[:, -1], jnp.stack(keep))
+
+
 def across(mat, vec, backward):
     (pm, pv), (gm, gv) = group_level(mat, vec, "inner", backward)
-    gathered = lax.all_gather(pack(gm, gv), "outer")
-    mats, vecs = gathered[:, :-1], gathered[:, -1]
-    me = lax.axis_index("outer")
-    index = jnp.arange(mats.shape[0])
-    keep = index > me if backward else index < me
-    om, ov = reduce_maps(*keep_only(mats, vecs, keep), backward)
+    others = from_other_groups(pack(gm, gv), backward)
+    if others is None:
+        return pm, pv
+    om, ov = reduce_maps(others[0], others[1], False)
     return mm(pm, om), mv(pm, ov) + pv
 
 

time: 117 us -> 99.8 us (0.85)
  blocking collectives: 51.2 us -> 21.6 us
  waiting for transfers between devices: 0 us -> 9.11 us
  starting transfers between devices: 0 us -> 9 us
  local copies, waits for them, and re-layouts: 6.83 us -> 2.55 us
  matrix products: 32.2 us -> 29.5 us
  other arithmetic: 24.1 us -> 25.5 us
    all_gather x2 -> x0, blocking collectives: 29.6 us -> none  [across(): gathered = lax.all_gather(pack(gm, gv), 'outer')]
    ppermute x0 -> x6, waiting for transfers between devices: none -> 9.11 us  [from_other_groups(): received.append(lax.ppermute(packed, 'outer', pairs))]
    ppermute x0 -> x6, starting transfers between devices: none -> 9 us  [from_other_groups(): received.append(lax.ppermute(packed, 'outer', pairs))]
    unnamed x75 -> x51, local copies, waits for them, and re-layouts: 5.82 us -> 1.63 us
    add x6, other arithmetic: 2.78 us -> 0.72 us  [spread(): other = applied[:, 0] + pv[:, 0]]
    concatenate x0 -> x4, other arithmetic: none -> 1.73 us  [the longest x2 1.09 us: pad_pow2(): mats = jnp.concatenate((mats, eye), axis=-3)]
    dot_general x14, matrix products: 8.29 us -> 6.71 us  [mv(): jnp.einsum('...ij,...j->...i', a, v, precision=exact, preferred_element_t...]
    another operation x0 -> x4, other arithmetic: none -> 1.3 us  [the longest x2 1.14 us: from_other_groups(): maps = jnp.stack(received)]
  transfers between devices with their start and end apart: 0 -> 6, of which waited for: 0 -> 3; matrix products, arithmetic and copies ran while one was open for 0% -> 2% of each run, Pallas kernels for 0% -> 0%
where the time goes in v1:
time: 99.8 us; the launch traced here: 99.3 us
  matrix products  29.5 us (30%)
  other arithmetic  25.5 us (26%)
  blocking collectives  21.6 us (22%)
  waiting for transfers between devices  9.11 us (9%)
  starting transfers between devices  9 us (9%)
  local copies, waits for them, and re-layouts  2.55 us (3%)
  between operations  1.98 us (2%)
    all_gather x2, blocking collectives, group_level(): gathered = lax.all_gather(pack(mat, vec), axis)  21.6 us
    dot_general x23, matrix products, mm(): return jnp.matmul(a, b, precision=exact, preferred_element_type=jnp.float32)  16.6 us
    reduce_sum x17, other arithmetic, mv_whole(): return jnp.sum(a * v[..., None, :], axis=-1)  16 us
    ppermute x6, waiting for transfers between devices, from_other_groups(): received.append(lax.ppermute(packed, 'outer', pairs))  9.11 us
    ppermute x6, starting transfers between devices, from_other_groups(): received.append(lax.ppermute(packed, 'outer', pairs))  9 us
    dot_general x14, matrix products, mv(): jnp.einsum('...ij,...j->...i', a, v, precision=exact, preferred_element_t...  6.71 us
    dot_general x1, matrix products, on_device(): jnp.einsum('tij,jk->tik', gains, mapped, precision=exact, preferred_eleme...  5.92 us
  transfers between devices with their start and end apart: 6, of which 3 were waited for; matrix products, arithmetic and copies ran while one was open for 2% of the time, Pallas kernels for 0%

profile of v1, /device:TPU:0, one launch (start us, length us, event | category | flops | bytes accessed | tf_op | source)
XLA Modules:
  0.0 99.3 jit_solution(2409089224011392366)
XLA Ops:
  1.9 3.3 %multiply_reduce_fusion.7 = f32[64,128]{1,0:T(8,128)S(1)} fusion(f32[64,128,128]{2,1,0:T(8,128)} %param.7, f32[64,128]{1,0:T(8,128)} %param.6), kind=kLoop, calls=%fused_computation.8 | loop fusion | flops 2088960 | bytes 4259840 | tf_op jit(solution)/shard_map/reduce_sum | solution.py:19
  5.7 5.9 %multiply_reduce_fusion.6 = (f32[64,128]{1,0:T(8,128)S(1)}, f32[64,128,128]{1,2,0:T(8,128)S(1)}) fusion(f32[64,128]{1,0:T(8,128)S(1)} %bitcast.637, f32[128,128,1]{0,1,2:T(8,128)S(1)} %convolution_bitcast_fusion.4, f32[64,128,128]{2,1,0:T(8,128)} %param.7, f32[128,128]{0,1:T(8,128)S(1)} %copy.398), kind=kOutput, calls=%fused_computation.7 | convolution fusion | flops 1613750272 | bytes 8585216 | tf_op jit(solution)/shard_map/tij,jk->tik/dot_general | solution.py:145
  11.8 2.3 %multiply_reduce_fusion.11 = (f32[32,128]{1,0:T(8,128)S(1)}, f32[32,128,128]{1,2,0:T(8,128)S(1)}) fusion(f32[32,128]{1,0:T(8,128)S(1)} %bitcast.659, f32[32,2,128,128]{2,3,1,0:T(8,128)S(1)} %bitcast.593), kind=kOutput, calls=%fused_computation.18 | convolution fusion | flops 806350848 | bytes 6324224 | tf_op jit(solution)/shard_map/dot_general | solution.py:11
  14.2 1.2 %multiply_reduce_fusion.15 = (f32[16,128]{1,0:T(8,128)S(1)}, f32[16,128,128]{1,2,0:T(8,128)S(1)}) fusion(f32[16,128]{1,0:T(8,128)S(1)} %bitcast.677, f32[16,2,128,128]{2,3,1,0:T(8,128)S(1)} %bitcast.594), kind=kOutput, calls=%fused_computation.53 | convolution fusion | flops 403175424 | bytes 3162112 | tf_op jit(solution)/shard_map/dot_general | solution.py:11
  18.1 11.4 %all-gather.2 = f32[8,129,128]{2,1,0:T(8,128)S(1)} all-gather(f32[1,129,128]{2,1,0:T(8,128)S(1)} %maximum_bitcast_fusion), channel_id=2, replica_groups=mesh['outer'=4,'inner'=8] {'inner'}, dimensions={0}, use_global_device_ids=true | all-gather | bytes 594432 | tf_op jit(solution)/shard_map/all_gather | solution.py:104
  30.4 0.9 fusion.45
  34.1 1.6 %collective-permute-start.2 = (f32[129,128]{1,0:T(8,128)}, f32[129,128]{1,0:T(8,128)}, u32[]{:S(2)}, u32[]{:S(2)}) collective-permute-start(f32[129,128]{1,0:T(8,128)} %pad_maximum_fusion.6), channel_id=1, source_target_pairs={{0,8},{8,16},{16,24},{24,0},{1,9},{9,17},{17,25},{25,1},{2,10},{10... | collective-permute-start | bytes 198152 | tf_op jit(solution)/shard_map/ppermute | solution.py:124
  35.7 2.6 %collective-permute-start.1 = (f32[129,128]{1,0:T(8,128)}, f32[129,128]{1,0:T(8,128)}, u32[]{:S(2)}, u32[]{:S(2)}) collective-permute-start(f32[129,128]{1,0:T(8,128)} %pad_maximum_fusion.6), channel_id=1, source_target_pairs={{0,16},{8,24},{16,0},{24,8},{1,17},{9,25},{17,1},{25,9},{2,18},{10... | collective-permute-start | bytes 198152 | tf_op jit(solution)/shard_map/ppermute | solution.py:124
  38.3 1.3 %collective-permute-start = (f32[129,128]{1,0:T(8,128)}, f32[129,128]{1,0:T(8,128)}, u32[]{:S(2)}, u32[]{:S(2)}) collective-permute-start(f32[129,128]{1,0:T(8,128)} %pad_maximum_fusion.6), channel_id=1, source_target_pairs={{0,24},{8,0},{16,8},{24,16},{1,25},{9,1},{17,9},{25,17},{2,26},{10... | collective-permute-start | bytes 198152 | tf_op jit(solution)/shard_map/ppermute | solution.py:124
  41.5 2.3 %collective-permute-done.1 = f32[129,128]{1,0:T(8,128)} collective-permute-done((f32[129,128]{1,0:T(8,128)}, f32[129,128]{1,0:T(8,128)}, u32[]{:S(2)}, u32[]{:S(2)}) %collective-permute-start.1) | collective-permute-done | bytes 66080 | tf_op jit(solution)/shard_map/ppermute | solution.py:124
  44.1 1.0 pad_maximum_fusion.5
  45.1 0.7 pad_maximum_fusion.30
  46.0 1.0 pad_maximum_fusion.3
  48.2 1.1 %fusion.7 = f32[128]{0:T(128)S(1)} fusion(f32[128,1]{0,1:T(1,128)S(1)} %fusion.9, f32[2,128,128]{2,1,0:T(8,128)} %copy-done.8, f32[2,128]{1,0:T(2,128)} %copy-done.19), kind=kOutput, calls=%fused_computation.33 | convolution fusion | flops 196736 | bytes 67072 | tf_op jit(solution)/shard_map/...ij,...j->...i/dot_general | solution.py:15
  49.3 1.1 %fusion.44 = f32[128,128]{1,0:T(8,128)S(1)} fusion(f32[128,128]{1,0:T(8,128)S(1)} %fusion.41, f32[2,128,128]{2,1,0:T(8,128)} %copy-done.8), kind=kOutput, calls=%fused_computation.145 | convolution fusion | flops 25165824 | bytes 196608 | tf_op jit(solution)/shard_map/dot_general | solution.py:11
  50.4 0.8 fusion.10
  51.2 1.0 %multiply_reduce_fusion.26 = f32[2,128]{1,0:T(2,128)S(1)} fusion(f32[2,128,128]{1,2,0:T(8,128)} %copy-done.5, f32[128]{0:T(128)S(1)} %fusion.10), kind=kLoop, calls=%fused_computation.119 | loop fusion | flops 65280 | bytes 132608 | tf_op jit(solution)/shard_map/reduce_sum | solution.py:19
  53.2 1.3 %multiply_reduce_fusion.18 = f32[8,128]{1,0:T(8,128)S(1)} fusion(f32[8,128,128]{1,2,0:T(8,128)} %copy-done.4, f32[8,128]{1,0:T(8,128)S(1)} %bitcast.697), kind=kLoop, calls=%fused_computation.74 | loop fusion | flops 261120 | bytes 532480 | tf_op jit(solution)/shard_map/reduce_sum | solution.py:19
  54.9 0.7 multiply_reduce_fusion.10
  55.7 1.5 %multiply_reduce_fusion.5 = f32[64,128]{1,0:T(8,128)S(1)} fusion(f32[64,128,128]{1,2,0:T(8,128)S(1)} %copy-done.3, f32[64,128]{1,0:T(8,128)S(1)} %bitcast.641), kind=kLoop, calls=%fused_computation.6 | loop fusion | flops 2088960 | bytes 4259840 | tf_op jit(solution)/shard_map/reduce_sum | solution.py:19
  57.3 1.5 %multiply_reduce_fusion.4 = f32[64,128]{1,0:T(8,128)S(1)} fusion(f32[64,128,128]{1,2,0:T(8,128)S(1)} %copy-done.3, f32[64,128]{1,0:T(8,128)S(1)} %bitcast.638), kind=kLoop, calls=%fused_computation.5 | loop fusion | flops 2088960 | bytes 4259840 | tf_op jit(solution)/shard_map/reduce_sum | solution.py:19
  59.0 1.2 %multiply_reduce_fusion.3 = f32[64,128]{1,0:T(8,128)S(1)} fusion(f32[64,128,128]{2,1,0:T(8,128)S(1)} %copy-done.1, f32[64,128]{1,0:T(8,128)S(1)} %fusion.97), kind=kLoop, calls=%fused_computation.4 | loop fusion | flops 2088960 | bytes 4259840 | tf_op jit(solution)/shard_map/reduce_sum | solution.py:19
  60.3 1.2 %multiply_reduce_fusion.2 = f32[64,128]{1,0:T(8,128)S(1)} fusion(f32[64,128,128]{2,1,0:T(8,128)S(1)} %copy-done.1, f32[64,128]{1,0:T(8,128)S(1)} %bitcast.639), kind=kLoop, calls=%fused_computation.3 | loop fusion | flops 2088960 | bytes 4259840 | tf_op jit(solution)/shard_map/reduce_sum | solution.py:19
  61.5 3.9 %multiply_reduce_fusion.9 = (f32[32,128]{1,0:T(8,128)S(1)}, f32[32,128,128]{1,2,0:T(8,128)S(1)}) fusion(f32[32,128]{1,0:T(8,128)S(1)} %bitcast.660, f32[32,2,128,128]{3,2,1,0:T(8,128)S(1)} %bitcast.592), kind=kOutput, calls=%fused_computation.16 | convolution fusion | flops 806350848 | bytes 6324224 | tf_op jit(solution)/shard_map/dot_general | solution.py:11
  65.5 1.2 %multiply_reduce_fusion.13 = (f32[16,128]{1,0:T(8,128)S(1)}, f32[16,128,128]{1,2,0:T(8,128)S(1)}) fusion(f32[16,128]{1,0:T(8,128)S(1)} %bitcast.678, f32[16,2,128,128]{2,3,1,0:T(8,128)S(1)} %bitcast.595), kind=kOutput, calls=%fused_computation.51 | convolution fusion | flops 403175424 | bytes 3162112 | tf_op jit(solution)/shard_map/dot_general | solution.py:11
  68.7 10.2 %all-gather.3 = f32[8,129,128]{2,1,0:T(8,128)S(1)} all-gather(f32[1,129,128]{2,1,0:T(8,128)S(1)} %maximum_bitcast_fusion.1), channel_id=3, replica_groups=mesh['outer'=4,'inner'=8] {'inner'}, dimensions={0}, use_global_device_ids=true | all-gather | bytes 594432 | tf_op jit(solution)/shard_map/all_gather | solution.py:104
  79.8 0.9 fusion.48
  82.3 2.8 %collective-permute-start.5 = (f32[129,128]{1,0:T(8,128)S(1)}, f32[129,128]{1,0:T(8,128)S(1)}, u32[]{:S(2)}, u32[]{:S(2)}) collective-permute-start(f32[129,128]{1,0:T(8,128)S(1)} %pad_maximum_fusion.7), channel_id=1, source_target_pairs={{0,24},{8,0},{16,8},{24,16},{1,25},{9,1},{17,9},{25,17},{2,26},{10... | collective-permute-start | bytes 198152 | tf_op jit(solution)/shard_map/ppermute | solution.py:124
  85.9 6.6 %collective-permute-done.4 = f32[129,128]{1,0:T(8,128)S(1)} collective-permute-done((f32[129,128]{1,0:T(8,128)S(1)}, f32[129,128]{1,0:T(8,128)S(1)}, u32[]{:S(2)}, u32[]{:S(2)}) %collective-permute-start.4) | collective-permute-done | bytes 66080 | tf_op jit(solution)/shard_map/ppermute | solution.py:124
  95.5 0.7 multiply_reduce_fusion.8
  96.3 1.2 %multiply_reduce_fusion.1 = f32[64,128]{1,0:T(8,128)S(1)} fusion(f32[64,128,128]{2,1,0:T(8,128)S(1)} %copy-done.1, f32[64,128]{1,0:T(8,128)S(1)} %bitcast.642), kind=kLoop, calls=%fused_computation.2 | loop fusion | flops 2088960 | bytes 4259840 | tf_op jit(solution)/shard_map/reduce_sum | solution.py:19
  97.5 1.2 %multiply_reduce_fusion = f32[64,128]{1,0:T(8,128)S(1)} fusion(f32[64,128,128]{2,1,0:T(8,128)S(1)} %copy-done.1, f32[64,128]{1,0:T(8,128)S(1)} %bitcast.640), kind=kLoop, calls=%fused_computation.1 | loop fusion | flops 2088960 | bytes 4259840 | tf_op jit(solution)/shard_map/reduce_sum | solution.py:19
  (221 shorter events, 21.9 us)
Async XLA Ops:
  0.6 4.7 %copy-start = (f32[128,128]{1,0:T(8,128)S(1)}, f32[128,128]{1,0:T(8,128)}, u32[]{:S(2)}) copy-start(f32[128,128]{1,0:T(8,128)} %param.10) | copy-start | bytes 196612
  0.6 4.6 %copy-start.10 = (f32[128,128]{1,0:T(8,128)S(1)}, f32[128,128]{1,0:T(8,128)}, u32[]{:S(2)}) copy-start(f32[128,128]{1,0:T(8,128)} %param.9) | copy-start | bytes 196612
  5.2 6.4 %copy-start.6 = (f32[64,128]{1,0:T(8,128)}, f32[64,128]{1,0:T(8,128)S(1)}, u32[]{:S(2)}) copy-start(f32[64,128]{1,0:T(8,128)S(1)} %multiply_reduce_fusion.7) | copy-start | bytes 98308
  11.6 3.7 %copy-start.2 = (f32[64,128,128]{1,2,0:T(8,128)}, f32[64,128,128]{1,2,0:T(8,128)S(1)}, u32[]{:S(2)}) copy-start(f32[64,128,128]{1,2,0:T(8,128)S(1)} %get-tuple-element.43) | copy-start | bytes 12582916
  14.1 15.4 %copy-start.24 = (pred[4,2]{0,1:T(4,128)(4,1)S(1)}, pred[4,2]{0,1:T(4,128)(4,1)}, u32[]{:S(2)}) copy-start(pred[4,2]{0,1:T(4,128)(4,1)} %fusion.65) | copy-start | bytes 28
  14.1 15.5 %copy-start.22 = (pred[8]{0:T(512)(128)(4,1)S(1)}, pred[8]{0:T(512)(128)(4,1)}, u32[]{:S(2)}) copy-start(pred[8]{0:T(512)(128)(4,1)} %iota_compare_fusion.2) | copy-start | bytes 28
  14.1 2.0 %copy-start.13 = (f32[16,1,128]{2,1,0:T(1,128)}, f32[16,1,128]{2,1,0:T(1,128)S(1)}, u32[]{:S(2)}) copy-start(f32[16,1,128]{2,1,0:T(1,128)S(1)} %slice_add_fusion.7) | copy-start | bytes 24580
  15.4 0.8 copy-start.15
  16.1 13.5 %copy-start.4 = (f32[8,128,128]{1,2,0:T(8,128)}, f32[8,128,128]{1,2,0:T(8,128)S(1)}, u32[]{:S(2)}) copy-start(f32[8,128,128]{1,2,0:T(8,128)S(1)} %get-tuple-element.49) | copy-start | bytes 1572868
  16.1 0.7 copy-start.17
  17.2 0.6 copy-start.20
  17.5 12.1 %copy-start.5 = (f32[2,128,128]{1,2,0:T(8,128)}, f32[2,128,128]{1,2,0:T(8,128)S(1)}, u32[]{:S(2)}) copy-start(f32[2,128,128]{1,2,0:T(8,128)S(1)} %get-tuple-element.53) | copy-start | bytes 393220
  32.6 0.9 copy-start.8
  32.9 0.6 copy-start.19
  34.1 7.4 %collective-permute-start.2 = (f32[129,128]{1,0:T(8,128)}, f32[129,128]{1,0:T(8,128)}, u32[]{:S(2)}, u32[]{:S(2)}) collective-permute-start(f32[129,128]{1,0:T(8,128)} %pad_maximum_fusion.6), channel_id=1, source_target_pairs={{0,8},{8,16},{16,24},{24,0},{1,9},{9,17},{17,25},{25,1},{2,10},{10... | collective-permute-start | bytes 198152 | tf_op jit(solution)/shard_map/ppermute | solution.py:124
  35.7 8.1 %collective-permute-start.1 = (f32[129,128]{1,0:T(8,128)}, f32[129,128]{1,0:T(8,128)}, u32[]{:S(2)}, u32[]{:S(2)}) collective-permute-start(f32[129,128]{1,0:T(8,128)} %pad_maximum_fusion.6), channel_id=1, source_target_pairs={{0,16},{8,24},{16,0},{24,8},{1,17},{9,25},{17,1},{25,9},{2,18},{10... | collective-permute-start | bytes 198152 | tf_op jit(solution)/shard_map/ppermute | solution.py:124
  38.3 5.8 %collective-permute-start = (f32[129,128]{1,0:T(8,128)}, f32[129,128]{1,0:T(8,128)}, u32[]{:S(2)}, u32[]{:S(2)}) collective-permute-start(f32[129,128]{1,0:T(8,128)} %pad_maximum_fusion.6), channel_id=1, source_target_pairs={{0,24},{8,0},{16,8},{24,16},{1,25},{9,1},{17,9},{25,17},{2,26},{10... | collective-permute-start | bytes 198152 | tf_op jit(solution)/shard_map/ppermute | solution.py:124
  41.5 11.7 %copy-start.18 = (f32[4,1,128]{2,1,0:T(1,128)S(1)}, f32[4,1,128]{2,1,0:T(1,128)}, u32[]{:S(2)}) copy-start(f32[4,1,128]{2,1,0:T(1,128)} %copy-done.17) | copy-start | bytes 6148
  41.5 13.0 %copy-start.16 = (f32[8,1,128]{2,1,0:T(1,128)S(1)}, f32[8,1,128]{2,1,0:T(1,128)}, u32[]{:S(2)}) copy-start(f32[8,1,128]{2,1,0:T(1,128)} %copy-done.15) | copy-start | bytes 12292
  41.5 13.4 %copy-start.14 = (f32[16,1,128]{2,1,0:T(1,128)S(1)}, f32[16,1,128]{2,1,0:T(1,128)}, u32[]{:S(2)}) copy-start(f32[16,1,128]{2,1,0:T(1,128)} %copy-done.13) | copy-start | bytes 24580
  41.5 14.2 %copy-start.3 = (f32[64,128,128]{1,2,0:T(8,128)S(1)}, f32[64,128,128]{1,2,0:T(8,128)}, u32[]{:S(2)}) copy-start(f32[64,128,128]{1,2,0:T(8,128)} %copy-done.2) | copy-start | bytes 12582916
  52.9 4.2 %copy-start.7 = (f32[64,128]{1,0:T(8,128)S(1)}, f32[64,128]{1,0:T(8,128)}, u32[]{:S(2)}) copy-start(f32[64,128]{1,0:T(8,128)} %copy-done.6) | copy-start | bytes 98308
  55.7 3.1 %copy-start.11 = (f32[128,128]{1,0:T(8,128)S(1)}, f32[128,128]{1,0:T(8,128)}, u32[]{:S(2)}) copy-start(f32[128,128]{1,0:T(8,128)} %param.9) | copy-start | bytes 196612
  55.7 3.3 %copy-start.1 = (f32[64,128,128]{2,1,0:T(8,128)S(1)}, f32[64,128,128]{2,1,0:T(8,128)}, u32[]{:S(2)}) copy-start(f32[64,128,128]{2,1,0:T(8,128)} %param.8) | copy-start | bytes 12582916
  58.8 39.9 %copy-start.12 = (f32[64,128]{1,0:T(8,128)}, f32[64,128]{1,0:T(8,128)S(1)}, u32[]{:S(2)}) copy-start(f32[64,128]{1,0:T(8,128)S(1)} %add.261) | copy-start | bytes 98308
  65.5 13.5 %copy-start.21 = (pred[8]{0:T(512)(128)(4,1)S(1)}, pred[8]{0:T(512)(128)(4,1)}, u32[]{:S(2)}) copy-start(pred[8]{0:T(512)(128)(4,1)} %iota_compare_fusion.1) | copy-start | bytes 28
  65.5 13.5 %copy-start.23 = (pred[4,2]{0,1:T(4,128)(4,1)S(1)}, pred[4,2]{0,1:T(4,128)(4,1)}, u32[]{:S(2)}) copy-start(pred[4,2]{0,1:T(4,128)(4,1)} %fusion.64) | copy-start | bytes 28
  78.9 14.1 %copy-start.9 = (f32[1,128,128]{2,0,1:T(1,128)S(1)}, f32[1,128,128]{2,0,1:T(1,128)}, u32[]{:S(2)}) copy-start(f32[1,128,128]{2,0,1:T(1,128)} %compare_convert_fusion) | copy-start | bytes 196612
  82.3 10.3 %collective-permute-start.5 = (f32[129,128]{1,0:T(8,128)S(1)}, f32[129,128]{1,0:T(8,128)S(1)}, u32[]{:S(2)}, u32[]{:S(2)}) collective-permute-start(f32[129,128]{1,0:T(8,128)S(1)} %pad_maximum_fusion.7), channel_id=1, source_target_pairs={{0,24},{8,0},{16,8},{24,16},{1,25},{9,1},{17,9},{25,17},{2,26},{10... | collective-permute-start | bytes 198152 | tf_op jit(solution)/shard_map/ppermute | solution.py:124
  85.2 7.3 %collective-permute-start.4 = (f32[129,128]{1,0:T(8,128)S(1)}, f32[129,128]{1,0:T(8,128)S(1)}, u32[]{:S(2)}, u32[]{:S(2)}) collective-permute-start(f32[129,128]{1,0:T(8,128)S(1)} %pad_maximum_fusion.7), channel_id=1, source_target_pairs={{0,16},{8,24},{16,0},{24,8},{1,17},{9,25},{17,1},{25,9},{2,18},{10... | collective-permute-start | bytes 198152 | tf_op jit(solution)/shard_map/ppermute | solution.py:124
  85.6 7.0 %collective-permute-start.3 = (f32[129,128]{1,0:T(8,128)S(1)}, f32[129,128]{1,0:T(8,128)S(1)}, u32[]{:S(2)}, u32[]{:S(2)}) collective-permute-start(f32[129,128]{1,0:T(8,128)S(1)} %pad_maximum_fusion.7), channel_id=1, source_target_pairs={{0,8},{8,16},{16,24},{24,0},{1,9},{9,17},{17,25},{25,1},{2,10},{10... | collective-permute-start | bytes 198152 | tf_op jit(solution)/shard_map/ppermute | solution.py:124

commit v2 on v1

--- a/solution.py
+++ b/solution.py
@@ -44,6 +44,31 @@
     tiers = [(mats, vecs)]
     while tiers[-1][0].shape[0] > 1:
         tiers.append(local_pair(tiers[-1][0], tiers[-1][1], backward))
+    return tiers
+
+
+def matrix_tiers(mats, backward):
+    tiers = [mats]
+    width = mats.shape[-1]
+    while tiers[-1].shape[0] > 1:
+        below = tiers[-1]
+        pm = below.reshape(below.shape[0] // 2, 2, width, width)
+        first, second = (1, 0) if backward else (0, 1)
+        tiers.append(mm(pm[:, second], pm[:, first]))
+    return tiers
+
+
+def vector_tiers(mats_tiers, vecs, backward):
+    tiers = [(mats_tiers[0], vecs)]
+    width = vecs.shape[-1]
+    first, second = (1, 0) if backward else (0, 1)
+    for mats, joined in zip(mats_tiers[:-1], mats_tiers[1:]):
+        below = tiers[-1][1]
+        count = below.shape[0]
+        pv = below.reshape(count // 2, 2, width)
+        partner = jnp.stack((pv[:, 1], pv[:, 0]), axis=1).reshape(count, width)
+        crossed = mv_whole(mats, partner).reshape(count // 2, 2, width)
+        tiers.append((joined, crossed[:, second] + pv[:, second]))
     return tiers
 
 
@@ -141,6 +166,7 @@
 def on_device(observations, gains, smoother_gains, transition, observation_map, initial_mean):
     me = lax.axis_index(AXES)
     devices = lax.axis_size(AXES)
+    back_mats = lax.optimization_barrier(matrix_tiers(smoother_gains, True))
     mapped = mm(observation_map, transition)
     forward_maps = transition[None] - jnp.einsum(
         "tij,jk->tik", gains, mapped, precision=exact, preferred_element_type=jnp.float32
@@ -156,7 +182,7 @@
         filtered, transition.T, precision=exact, preferred_element_type=jnp.float32
     )
     offsets = filtered - mv_whole(smoother_gains, predicted_all)
-    backward = local_tiers(smoother_gains, offsets, True)
+    backward = vector_tiers(back_mats, offsets, True)
     bm, bv = backward[-1][0][0], backward[-1][1][0]
     last = me == devices - 1
     extra = jnp.where(last, predicted_all[-1], 0.0)

time: 99.8 us -> 103 us (1.032)
  other arithmetic: 25.5 us -> 30.8 us
  waiting for transfers between devices: 9.11 us -> 6.58 us
  starting transfers between devices: 9 us -> 7.94 us
    reduce_sum x17 -> x22, other arithmetic: 16 us -> 20.9 us  [mv_whole(): return jnp.sum(a * v[..., None, :], axis=-1)]
    ppermute x6, waiting for transfers between devices: 9.11 us -> 6.58 us  [from_other_groups(): received.append(lax.ppermute(packed, 'outer', pairs))]
    ppermute x6, starting transfers between devices: 9 us -> 7.94 us  [from_other_groups(): received.append(lax.ppermute(packed, 'outer', pairs))]
    unnamed x51 -> x67, local copies, waits for them, and re-layouts: 1.63 us -> 2.62 us
  transfers between devices with their start and end apart: 6 -> 6, of which waited for: 3 -> 1; matrix products, arithmetic and copies ran while one was open for 2% -> 10% of each run, Pallas kernels for 0% -> 0%
where the time goes in v2:
time: 103 us
  other arithmetic  30.8 us (30%)
  matrix products  30.4 us (30%)
  blocking collectives  21.4 us (21%)
  starting transfers between devices  7.94 us (8%)
  waiting for transfers between devices  6.58 us (6%)
  local copies, waits for them, and re-layouts  3.52 us (3%)
  between operations  2.14 us (2%)
    all_gather x2, blocking collectives, group_level(): gathered = lax.all_gather(pack(mat, vec), axis)  21.4 us
    reduce_sum x22, other arithmetic, mv_whole(): return jnp.sum(a * v[..., None, :], axis=-1)  20.9 us
    dot_general x23, matrix products, mm(): return jnp.matmul(a, b, precision=exact, preferred_element_type=jnp.float32)  17.5 us
    ppermute x6, starting transfers between devices, from_other_groups(): received.append(lax.ppermute(packed, 'outer', pairs))  7.94 us
    dot_general x14, matrix products, mv(): jnp.einsum('...ij,...j->...i', a, v, precision=exact, preferred_element_t...  6.71 us
    ppermute x6, waiting for transfers between devices, from_other_groups(): received.append(lax.ppermute(packed, 'outer', pairs))  6.58 us
    dot_general x1, matrix products, on_device(): jnp.einsum('tij,jk->tik', gains, mapped, precision=exact, preferred_eleme...  5.93 us
    unnamed x67, local copies, waits for them, and re-layouts  2.62 us
  transfers between devices with their start and end apart: 6, of which 1 were waited for; matrix products, arithmetic and copies ran while one was open for 10% of the time, Pallas kernels for 0%

profile of v2, /device:TPU:0, one launch (start us, length us, event | category | flops | bytes accessed | tf_op | source)
XLA Modules:
  0.0 102.8 jit_solution(8051317525204941120)
XLA Ops:
  1.8 3.3 %multiply_reduce_fusion.7 = f32[64,128]{1,0:T(8,128)S(1)} fusion(f32[64,128,128]{2,1,0:T(8,128)} %param.7, f32[64,128]{1,0:T(8,128)} %param.6), kind=kLoop, calls=%fused_computation.8 | loop fusion | flops 2088960 | bytes 4259840 | tf_op jit(solution)/shard_map/reduce_sum | solution.py:19
  5.6 5.9 %multiply_reduce_fusion.6 = (f32[64,128]{1,0:T(8,128)S(1)}, f32[64,128,128]{1,2,0:T(8,128)S(1)}) fusion(f32[64,128]{1,0:T(8,128)S(1)} %bitcast.627, f32[128,128,1]{0,1,2:T(8,128)S(1)} %convolution_bitcast_fusion.5, f32[64,128,128]{2,1,0:T(8,128)} %param.7, f32[128,128]{0,1:T(8,128)S(1)} %copy.397), kind=kOutput, calls=%fused_computation.7 | convolution fusion | flops 1613750272 | bytes 8585216 | tf_op jit(solution)/shard_map/tij,jk->tik/dot_general | solution.py:171
  11.7 2.3 %multiply_reduce_fusion.11 = (f32[32,128]{1,0:T(8,128)S(1)}, f32[32,128,128]{1,2,0:T(8,128)S(1)}) fusion(f32[32,128]{1,0:T(8,128)S(1)} %bitcast.649, f32[32,2,128,128]{2,3,1,0:T(8,128)S(1)} %bitcast.582), kind=kOutput, calls=%fused_computation.18 | convolution fusion | flops 806350848 | bytes 6324224 | tf_op jit(solution)/shard_map/dot_general | solution.py:11
  14.1 1.2 %multiply_reduce_fusion.15 = (f32[16,128]{1,0:T(8,128)S(1)}, f32[16,128,128]{1,2,0:T(8,128)S(1)}) fusion(f32[16,128]{1,0:T(8,128)S(1)} %bitcast.667, f32[16,2,128,128]{2,3,1,0:T(8,128)S(1)} %bitcast.584), kind=kOutput, calls=%fused_computation.54 | convolution fusion | flops 403175424 | bytes 3162112 | tf_op jit(solution)/shard_map/dot_general | solution.py:11
  17.5 11.4 %all-gather.2 = f32[8,129,128]{2,1,0:T(8,128)S(1)} all-gather(f32[1,129,128]{2,1,0:T(8,128)S(1)} %maximum_bitcast_fusion), channel_id=2, replica_groups=mesh['outer'=4,'inner'=8] {'inner'}, dimensions={0}, use_global_device_ids=true | all-gather | bytes 594432 | tf_op jit(solution)/shard_map/all_gather | solution.py:129
  29.9 0.9 fusion.44
  33.6 1.6 %collective-permute-start.2 = (f32[129,128]{1,0:T(8,128)}, f32[129,128]{1,0:T(8,128)}, u32[]{:S(2)}, u32[]{:S(2)}) collective-permute-start(f32[129,128]{1,0:T(8,128)} %pad_maximum_fusion.6), channel_id=1, source_target_pairs={{0,8},{8,16},{16,24},{24,0},{1,9},{9,17},{17,25},{25,1},{2,10},{10... | collective-permute-start | bytes 198152 | tf_op jit(solution)/shard_map/ppermute | solution.py:149
  35.2 2.6 %collective-permute-start.1 = (f32[129,128]{1,0:T(8,128)}, f32[129,128]{1,0:T(8,128)}, u32[]{:S(2)}, u32[]{:S(2)}) collective-permute-start(f32[129,128]{1,0:T(8,128)} %pad_maximum_fusion.6), channel_id=1, source_target_pairs={{0,16},{8,24},{16,0},{24,8},{1,17},{9,25},{17,1},{25,9},{2,18},{10... | collective-permute-start | bytes 198152 | tf_op jit(solution)/shard_map/ppermute | solution.py:149
  37.8 1.3 %collective-permute-start = (f32[129,128]{1,0:T(8,128)}, f32[129,128]{1,0:T(8,128)}, u32[]{:S(2)}, u32[]{:S(2)}) collective-permute-start(f32[129,128]{1,0:T(8,128)} %pad_maximum_fusion.6), channel_id=1, source_target_pairs={{0,24},{8,0},{16,8},{24,16},{1,25},{9,1},{17,9},{25,17},{2,26},{10... | collective-permute-start | bytes 198152 | tf_op jit(solution)/shard_map/ppermute | solution.py:149
  41.0 4.4 %fusion = f32[32,128,128]{2,1,0:T(8,128)S(1)} fusion(f32[32,2,128,128]{3,2,1,0:T(8,128)} %bitcast.581), kind=kOutput, calls=%fused_computation.10 | convolution fusion | flops 805306368 | bytes 6291456 | tf_op jit(solution)/shard_map/dot_general | solution.py:11
  45.3 1.1 %fusion.12 = f32[16,128,128]{2,1,0:T(8,128)S(1)} fusion(f32[16,2,128,128]{3,2,1,0:T(8,128)S(1)} %bitcast.583), kind=kOutput, calls=%fused_computation.42 | convolution fusion | flops 402653184 | bytes 3145728 | tf_op jit(solution)/shard_map/dot_general | solution.py:11
  50.2 1.1 %pad_maximum_fusion.5 = f32[3,129,128]{2,1,0:T(8,128)S(1)} fusion(f32[1,129,128]{2,1,0:T(8,128)} %bitcast.78, f32[1,129,128]{2,1,0:T(8,128)} %bitcast.77, f32[1,129,128]{2,1,0:T(8,128)} %bitcast.76), kind=kLoop, calls=%fused_computation.101 | loop fusion | flops 99072 | bytes 396288 | tf_op jit(solution)/shard_map/stack | solution.py:153
  51.4 0.8 pad_maximum_fusion.30
  52.4 1.0 pad_maximum_fusion.3
  54.6 1.1 %fusion.7 = f32[128]{0:T(128)S(1)} fusion(f32[128,1]{0,1:T(1,128)S(1)} %fusion.9, f32[2,128,128]{2,1,0:T(8,128)} %copy-done.15, f32[2,128]{1,0:T(2,128)} %copy-done.27), kind=kOutput, calls=%fused_computation.34 | convolution fusion | flops 196736 | bytes 67072 | tf_op jit(solution)/shard_map/...ij,...j->...i/dot_general | solution.py:15
  55.7 1.1 %fusion.43 = f32[128,128]{1,0:T(8,128)S(1)} fusion(f32[128,128]{1,0:T(8,128)S(1)} %fusion.40, f32[2,128,128]{2,1,0:T(8,128)} %copy-done.15), kind=kOutput, calls=%fused_computation.145 | convolution fusion | flops 25165824 | bytes 196608 | tf_op jit(solution)/shard_map/dot_general | solution.py:11
  56.8 0.8 fusion.10
  57.6 1.0 %multiply_reduce_fusion.26 = f32[2,128]{1,0:T(2,128)S(1)} fusion(f32[2,128,128]{1,2,0:T(8,128)} %copy-done.12, f32[128]{0:T(128)S(1)} %fusion.10), kind=kLoop, calls=%fused_computation.120 | loop fusion | flops 65280 | bytes 132608 | tf_op jit(solution)/shard_map/reduce_sum | solution.py:19
  59.4 1.1 %multiply_reduce_fusion.22 = f32[4,128]{1,0:T(4,128)S(1)} fusion(f32[4,128,128]{1,2,0:T(8,128)} %copy-done.9, f32[4,128]{1,0:T(4,128)S(1)} %bitcast.713), kind=kLoop, calls=%fused_computation.94 | loop fusion | flops 130560 | bytes 266240 | tf_op jit(solution)/shard_map/reduce_sum | solution.py:19
  60.6 1.3 %multiply_reduce_fusion.18 = f32[8,128]{1,0:T(8,128)S(1)} fusion(f32[8,128,128]{1,2,0:T(8,128)} %copy-done.8, f32[8,128]{1,0:T(8,128)S(1)} %bitcast.687), kind=kLoop, calls=%fused_computation.75 | loop fusion | flops 261120 | bytes 532480 | tf_op jit(solution)/shard_map/reduce_sum | solution.py:19
  61.9 1.6 %multiply_reduce_fusion.14 = f32[16,128]{1,0:T(8,128)S(1)} fusion(f32[16,128,128]{1,2,0:T(8,128)} %copy-done.5, f32[16,128]{1,0:T(8,128)S(1)} %bitcast.669), kind=kLoop, calls=%fused_computation.53 | loop fusion | flops 522240 | bytes 1064960 | tf_op jit(solution)/shard_map/reduce_sum | solution.py:19
  63.5 2.1 %multiply_reduce_fusion.10 = f32[32,128]{1,0:T(8,128)S(1)} fusion(f32[32,128,128]{1,2,0:T(8,128)} %copy-done.4, f32[32,128]{1,0:T(8,128)S(1)} %bitcast.651), kind=kLoop, calls=%fused_computation.17 | loop fusion | flops 1044480 | bytes 2129920 | tf_op jit(solution)/shard_map/reduce_sum | solution.py:19
  65.8 1.5 %multiply_reduce_fusion.5 = f32[64,128]{1,0:T(8,128)S(1)} fusion(f32[64,128,128]{1,2,0:T(8,128)S(1)} %copy-done.3, f32[64,128]{1,0:T(8,128)S(1)} %bitcast.631), kind=kLoop, calls=%fused_computation.6 | loop fusion | flops 2088960 | bytes 4259840 | tf_op jit(solution)/shard_map/reduce_sum | solution.py:19
  67.3 1.5 %multiply_reduce_fusion.4 = f32[64,128]{1,0:T(8,128)S(1)} fusion(f32[64,128,128]{1,2,0:T(8,128)S(1)} %copy-done.3, f32[64,128]{1,0:T(8,128)S(1)} %bitcast.628), kind=kLoop, calls=%fused_computation.5 | loop fusion | flops 2088960 | bytes 4259840 | tf_op jit(solution)/shard_map/reduce_sum | solution.py:19
  69.1 1.2 %multiply_reduce_fusion.3 = f32[64,128]{1,0:T(8,128)S(1)} fusion(f32[64,128,128]{2,1,0:T(8,128)S(1)} %copy-done.1, f32[64,128]{1,0:T(8,128)S(1)} %fusion.97), kind=kLoop, calls=%fused_computation.4 | loop fusion | flops 2088960 | bytes 4259840 | tf_op jit(solution)/shard_map/reduce_sum | solution.py:19
  70.4 1.2 %multiply_reduce_fusion.2 = f32[64,128]{1,0:T(8,128)S(1)} fusion(f32[64,128,128]{2,1,0:T(8,128)S(1)} %copy-done.1, f32[64,128]{1,0:T(8,128)S(1)} %bitcast.629), kind=kLoop, calls=%fused_computation.3 | loop fusion | flops 2088960 | bytes 4259840 | tf_op jit(solution)/shard_map/reduce_sum | solution.py:19
  73.6 10.0 %all-gather.3 = f32[8,129,128]{2,1,0:T(8,128)S(1)} all-gather(f32[1,129,128]{2,1,0:T(8,128)S(1)} %maximum_bitcast_fusion.1), channel_id=3, replica_groups=mesh['outer'=4,'inner'=8] {'inner'}, dimensions={0}, use_global_device_ids=true | all-gather | bytes 594432 | tf_op jit(solution)/shard_map/all_gather | solution.py:129
  84.4 0.9 fusion.47
  87.4 1.7 %collective-permute-start.4 = (f32[129,128]{1,0:T(8,128)S(1)}, f32[129,128]{1,0:T(8,128)S(1)}, u32[]{:S(2)}, u32[]{:S(2)}) collective-permute-start(f32[129,128]{1,0:T(8,128)S(1)} %pad_maximum_fusion.7), channel_id=1, source_target_pairs={{0,16},{8,24},{16,0},{24,8},{1,17},{9,25},{17,1},{25,9},{2,18},{10... | collective-permute-start | bytes 198152 | tf_op jit(solution)/shard_map/ppermute | solution.py:149
  89.4 6.6 %collective-permute-done.4 = f32[129,128]{1,0:T(8,128)S(1)} collective-permute-done((f32[129,128]{1,0:T(8,128)S(1)}, f32[129,128]{1,0:T(8,128)S(1)}, u32[]{:S(2)}, u32[]{:S(2)}) %collective-permute-start.4) | collective-permute-done | bytes 66080 | tf_op jit(solution)/shard_map/ppermute | solution.py:149
  99.8 1.2 %multiply_reduce_fusion.1 = f32[64,128]{1,0:T(8,128)S(1)} fusion(f32[64,128,128]{2,1,0:T(8,128)S(1)} %copy-done.1, f32[64,128]{1,0:T(8,128)S(1)} %bitcast.632), kind=kLoop, calls=%fused_computation.2 | loop fusion | flops 2088960 | bytes 4259840 | tf_op jit(solution)/shard_map/reduce_sum | solution.py:19
  101.0 1.2 %multiply_reduce_fusion = f32[64,128]{1,0:T(8,128)S(1)} fusion(f32[64,128,128]{2,1,0:T(8,128)S(1)} %copy-done.1, f32[64,128]{1,0:T(8,128)S(1)} %bitcast.630), kind=kLoop, calls=%fused_computation.1 | loop fusion | flops 2088960 | bytes 4259840 | tf_op jit(solution)/shard_map/reduce_sum | solution.py:19
  (242 shorter events, 24.8 us)
Async XLA Ops:
  0.6 4.7 %copy-start = (f32[128,128]{1,0:T(8,128)S(1)}, f32[128,128]{1,0:T(8,128)}, u32[]{:S(2)}) copy-start(f32[128,128]{1,0:T(8,128)} %param.10) | copy-start | bytes 196612
  0.6 4.5 %copy-start.17 = (f32[128,128]{1,0:T(8,128)S(1)}, f32[128,128]{1,0:T(8,128)}, u32[]{:S(2)}) copy-start(f32[128,128]{1,0:T(8,128)} %param.9) | copy-start | bytes 196612
  5.1 6.4 %copy-start.13 = (f32[64,128]{1,0:T(8,128)}, f32[64,128]{1,0:T(8,128)S(1)}, u32[]{:S(2)}) copy-start(f32[64,128]{1,0:T(8,128)S(1)} %multiply_reduce_fusion.7) | copy-start | bytes 98308
  11.6 3.7 %copy-start.2 = (f32[64,128,128]{1,2,0:T(8,128)}, f32[64,128,128]{1,2,0:T(8,128)S(1)}, u32[]{:S(2)}) copy-start(f32[64,128,128]{1,2,0:T(8,128)S(1)} %get-tuple-element.57) | copy-start | bytes 12582916
  14.0 15.2 %copy-start.4 = (f32[32,128,128]{1,2,0:T(8,128)}, f32[32,128,128]{1,2,0:T(8,128)S(1)}, u32[]{:S(2)}) copy-start(f32[32,128,128]{1,2,0:T(8,128)S(1)} %get-tuple-element.59) | copy-start | bytes 6291460
  14.0 14.9 %copy-start.32 = (pred[4,2]{0,1:T(4,128)(4,1)S(1)}, pred[4,2]{0,1:T(4,128)(4,1)}, u32[]{:S(2)}) copy-start(pred[4,2]{0,1:T(4,128)(4,1)} %fusion.64) | copy-start | bytes 28
  14.0 15.0 %copy-start.30 = (pred[8]{0:T(512)(128)(4,1)S(1)}, pred[8]{0:T(512)(128)(4,1)}, u32[]{:S(2)}) copy-start(pred[8]{0:T(512)(128)(4,1)} %iota_compare_fusion.2) | copy-start | bytes 28
  14.1 15.1 %copy-start.21 = (f32[16,1,128]{2,1,0:T(1,128)}, f32[16,1,128]{2,1,0:T(1,128)S(1)}, u32[]{:S(2)}) copy-start(f32[16,1,128]{2,1,0:T(1,128)S(1)} %slice_add_fusion.7) | copy-start | bytes 24580
  15.3 15.5 %copy-start.5 = (f32[16,128,128]{1,2,0:T(8,128)}, f32[16,128,128]{1,2,0:T(8,128)S(1)}, u32[]{:S(2)}) copy-start(f32[16,128,128]{1,2,0:T(8,128)S(1)} %get-tuple-element.61) | copy-start | bytes 3145732
  16.0 13.0 %copy-start.8 = (f32[8,128,128]{1,2,0:T(8,128)}, f32[8,128,128]{1,2,0:T(8,128)S(1)}, u32[]{:S(2)}) copy-start(f32[8,128,128]{1,2,0:T(8,128)S(1)} %get-tuple-element.63) | copy-start | bytes 1572868
  16.5 12.6 %copy-start.9 = (f32[4,128,128]{1,2,0:T(8,128)}, f32[4,128,128]{1,2,0:T(8,128)S(1)}, u32[]{:S(2)}) copy-start(f32[4,128,128]{1,2,0:T(8,128)S(1)} %get-tuple-element.65) | copy-start | bytes 786436
  16.9 12.2 %copy-start.12 = (f32[2,128,128]{1,2,0:T(8,128)}, f32[2,128,128]{1,2,0:T(8,128)S(1)}, u32[]{:S(2)}) copy-start(f32[2,128,128]{1,2,0:T(8,128)S(1)} %get-tuple-element.67) | copy-start | bytes 393220
  32.1 8.9 %copy-start.15 = (f32[2,128,128]{2,1,0:T(8,128)}, f32[2,128,128]{2,1,0:T(8,128)S(1)}, u32[]{:S(2)}) copy-start(f32[2,128,128]{2,1,0:T(8,128)S(1)} %fusion.34) | copy-start | bytes 393220
  33.6 16.6 %collective-permute-start.2 = (f32[129,128]{1,0:T(8,128)}, f32[129,128]{1,0:T(8,128)}, u32[]{:S(2)}, u32[]{:S(2)}) collective-permute-start(f32[129,128]{1,0:T(8,128)} %pad_maximum_fusion.6), channel_id=1, source_target_pairs={{0,8},{8,16},{16,24},{24,0},{1,9},{9,17},{17,25},{25,1},{2,10},{10... | collective-permute-start | bytes 198152 | tf_op jit(solution)/shard_map/ppermute | solution.py:149
  35.2 15.0 %collective-permute-start.1 = (f32[129,128]{1,0:T(8,128)}, f32[129,128]{1,0:T(8,128)}, u32[]{:S(2)}, u32[]{:S(2)}) collective-permute-start(f32[129,128]{1,0:T(8,128)} %pad_maximum_fusion.6), channel_id=1, source_target_pairs={{0,16},{8,24},{16,0},{24,8},{1,17},{9,25},{17,1},{25,9},{2,18},{10... | collective-permute-start | bytes 198152 | tf_op jit(solution)/shard_map/ppermute | solution.py:149
  37.8 12.4 %collective-permute-start = (f32[129,128]{1,0:T(8,128)}, f32[129,128]{1,0:T(8,128)}, u32[]{:S(2)}, u32[]{:S(2)}) collective-permute-start(f32[129,128]{1,0:T(8,128)} %pad_maximum_fusion.6), channel_id=1, source_target_pairs={{0,24},{8,0},{16,8},{24,16},{1,25},{9,1},{17,9},{25,17},{2,26},{10... | collective-permute-start | bytes 198152 | tf_op jit(solution)/shard_map/ppermute | solution.py:149
  50.1 10.4 %copy-start.26 = (f32[4,1,128]{2,1,0:T(1,128)S(1)}, f32[4,1,128]{2,1,0:T(1,128)}, u32[]{:S(2)}) copy-start(f32[4,1,128]{2,1,0:T(1,128)} %copy-done.25) | copy-start | bytes 6148
  50.1 11.7 %copy-start.24 = (f32[8,1,128]{2,1,0:T(1,128)S(1)}, f32[8,1,128]{2,1,0:T(1,128)}, u32[]{:S(2)}) copy-start(f32[8,1,128]{2,1,0:T(1,128)} %copy-done.23) | copy-start | bytes 12292
  50.1 13.3 %copy-start.22 = (f32[16,1,128]{2,1,0:T(1,128)S(1)}, f32[16,1,128]{2,1,0:T(1,128)}, u32[]{:S(2)}) copy-start(f32[16,1,128]{2,1,0:T(1,128)} %copy-done.21) | copy-start | bytes 24580
  50.1 15.6 %copy-start.3 = (f32[64,128,128]{1,2,0:T(8,128)S(1)}, f32[64,128,128]{1,2,0:T(8,128)}, u32[]{:S(2)}) copy-start(f32[64,128,128]{1,2,0:T(8,128)} %copy-done.2) | copy-start | bytes 12582916
  59.4 7.9 %copy-start.14 = (f32[64,128]{1,0:T(8,128)S(1)}, f32[64,128]{1,0:T(8,128)}, u32[]{:S(2)}) copy-start(f32[64,128]{1,0:T(8,128)} %copy-done.13) | copy-start | bytes 98308
  65.7 3.1 %copy-start.18 = (f32[128,128]{1,0:T(8,128)S(1)}, f32[128,128]{1,0:T(8,128)}, u32[]{:S(2)}) copy-start(f32[128,128]{1,0:T(8,128)} %param.9) | copy-start | bytes 196612
  65.8 3.3 %copy-start.1 = (f32[64,128,128]{2,1,0:T(8,128)S(1)}, f32[64,128,128]{2,1,0:T(8,128)}, u32[]{:S(2)}) copy-start(f32[64,128,128]{2,1,0:T(8,128)} %param.8) | copy-start | bytes 12582916
  68.8 33.4 %copy-start.20 = (f32[64,128]{1,0:T(8,128)}, f32[64,128]{1,0:T(8,128)S(1)}, u32[]{:S(2)}) copy-start(f32[64,128]{1,0:T(8,128)S(1)} %add.261) | copy-start | bytes 98308
  70.4 2.8 %copy-start.11 = (f32[2,128,128]{2,1,0:T(8,128)S(1)}, f32[2,128,128]{2,1,0:T(8,128)}, u32[]{:S(2)}) copy-start(f32[2,128,128]{2,1,0:T(8,128)} %copy-done.10) | copy-start | bytes 393220
  70.4 2.9 %copy-start.19 = (f32[1,128,128]{2,1,0:T(8,128)S(1)}, f32[1,128,128]{2,1,0:T(8,128)}, u32[]{:S(2)}) copy-start(f32[1,128,128]{2,1,0:T(8,128)} %convolution_bitcast_fusion.4) | copy-start | bytes 196612
  70.4 13.2 %copy-start.29 = (pred[8]{0:T(512)(128)(4,1)S(1)}, pred[8]{0:T(512)(128)(4,1)}, u32[]{:S(2)}) copy-start(pred[8]{0:T(512)(128)(4,1)} %iota_compare_fusion.1) | copy-start | bytes 28
  71.6 12.1 %copy-start.31 = (pred[4,2]{0,1:T(4,128)(4,1)S(1)}, pred[4,2]{0,1:T(4,128)(4,1)}, u32[]{:S(2)}) copy-start(pred[4,2]{0,1:T(4,128)(4,1)} %fusion.63) | copy-start | bytes 28
  83.5 13.1 %copy-start.16 = (f32[1,128,128]{2,0,1:T(1,128)S(1)}, f32[1,128,128]{2,0,1:T(1,128)}, u32[]{:S(2)}) copy-start(f32[1,128,128]{2,0,1:T(1,128)} %compare_convert_fusion) | copy-start | bytes 196612
  86.9 9.2 %collective-permute-start.5 = (f32[129,128]{1,0:T(8,128)S(1)}, f32[129,128]{1,0:T(8,128)S(1)}, u32[]{:S(2)}, u32[]{:S(2)}) collective-permute-start(f32[129,128]{1,0:T(8,128)S(1)} %pad_maximum_fusion.7), channel_id=1, source_target_pairs={{0,24},{8,0},{16,8},{24,16},{1,25},{9,1},{17,9},{25,17},{2,26},{10... | collective-permute-start | bytes 198152 | tf_op jit(solution)/shard_map/ppermute | solution.py:149
  87.4 8.6 %collective-permute-start.4 = (f32[129,128]{1,0:T(8,128)S(1)}, f32[129,128]{1,0:T(8,128)S(1)}, u32[]{:S(2)}, u32[]{:S(2)}) collective-permute-start(f32[129,128]{1,0:T(8,128)S(1)} %pad_maximum_fusion.7), channel_id=1, source_target_pairs={{0,16},{8,24},{16,0},{24,8},{1,17},{9,25},{17,1},{25,9},{2,18},{10... | collective-permute-start | bytes 198152 | tf_op jit(solution)/shard_map/ppermute | solution.py:149
  89.1 7.0 %collective-permute-start.3 = (f32[129,128]{1,0:T(8,128)S(1)}, f32[129,128]{1,0:T(8,128)S(1)}, u32[]{:S(2)}, u32[]{:S(2)}) collective-permute-start(f32[129,128]{1,0:T(8,128)S(1)} %pad_maximum_fusion.7), channel_id=1, source_target_pairs={{0,8},{8,16},{16,24},{24,0},{1,9},{9,17},{17,25},{25,1},{2,10},{10... | collective-permute-start | bytes 198152 | tf_op jit(solution)/shard_map/ppermute | solution.py:149
  (7 other events, 8.2 us)

commit v3 on v1

--- a/solution.py
+++ b/solution.py
@@ -100,19 +100,6 @@
     return jnp.concatenate((mat, vec[None, :]), axis=0)
 
 
-def group_level(mat, vec, axis, backward):
-    gathered = lax.all_gather(pack(mat, vec), axis)
-    mats, vecs = gathered[:, :-1], gathered[:, -1]
-    me = lax.axis_index(axis)
-    index = jnp.arange(mats.shape[0])
-    keep = index > me if backward else index < me
-    pm, pv = keep_only(mats, vecs, keep)
-    both_m = jnp.stack((pm, mats), axis=0)
-    both_v = jnp.stack((pv, vecs), axis=0)
-    rm, rv = reduce_maps(both_m, both_v, backward)
-    return (rm[0], rv[0]), (rm[1], rv[1])
-
-
 def from_other_groups(packed, backward):
     count = lax.axis_size("outer")
     me = lax.axis_index("outer")
@@ -123,19 +110,23 @@
         pairs = [(i, (i + step) % count) for i in range(count)]
         received.append(lax.ppermute(packed, "outer", pairs))
         keep.append(me + shift <= count - 1 if backward else me - shift >= 0)
-    if not received:
-        return None
-    maps = jnp.stack(received)
-    return keep_only(maps[:, :-1], maps[:, -1], jnp.stack(keep))
+    return received, keep
 
 
-def across(mat, vec, backward):
-    (pm, pv), (gm, gv) = group_level(mat, vec, "inner", backward)
-    others = from_other_groups(pack(gm, gv), backward)
-    if others is None:
-        return pm, pv
-    om, ov = reduce_maps(others[0], others[1], False)
-    return mm(pm, om), mv(pm, ov) + pv
+def across(mat, vec, start, backward):
+    gathered = lax.all_gather(pack(mat, vec), "inner")
+    mats, vecs = gathered[:, :-1], gathered[:, -1]
+    gm, gv = reduce_maps(mats, vecs, backward)
+    received, keep = from_other_groups(pack(gm, gv), backward)
+    me = lax.axis_index("inner")
+    index = jnp.arange(mats.shape[0])
+    mine = index > me if backward else index < me
+    pm, pv = reduce_maps(*keep_only(mats, vecs, mine), backward)
+    state = start
+    for block, kept in zip(received, keep):
+        moved = mv_whole(block[:-1], state) + block[-1]
+        state = jnp.where(kept, moved, state)
+    return mv_whole(pm, state) + pv
 
 
 def on_device(observations, gains, smoother_gains, transition, observation_map, initial_mean):
@@ -148,8 +139,7 @@
     forward_inputs = mv_whole(gains, observations)
     forward = local_tiers(forward_maps, forward_inputs, False)
     fm, fv = forward[-1][0][0], forward[-1][1][0]
-    before_m, before_v = across(fm, fv, False)
-    entry_state = mv(before_m, initial_mean) + before_v
+    entry_state = across(fm, fv, initial_mean, False)
     filtered = spread(forward, entry_state, False)
 
     predicted_all = jnp.dot(
@@ -161,8 +151,7 @@
     last = me == devices - 1
     extra = jnp.where(last, predicted_all[-1], 0.0)
     bv = bv + mv(bm, extra)
-    after_m, after_v = across(bm, bv, True)
-    after_state = after_v + extra
+    after_state = across(bm, bv, jnp.zeros_like(extra), True) + extra
     smoothed = spread(backward, after_state, True)
     return (filtered, smoothed)
 

time: 99.8 us -> 94 us (0.942)
  waiting for transfers between devices: 9.11 us -> 5.93 us
  local copies, waits for them, and re-layouts: 2.55 us -> 1.14 us
    reduce_sum x17 -> x23, other arithmetic: 16 us -> 19.4 us  [mv_whole(): return jnp.sum(a * v[..., None, :], axis=-1)]
    ppermute x6, waiting for transfers between devices: 9.11 us -> 5.93 us  [from_other_groups(): received.append(lax.ppermute(packed, 'outer', pairs))]
    select_n x2 -> x4, other arithmetic: 0.31 us -> 2.28 us  [across(): state = jnp.where(kept, moved, state)]
    dot_general x14 -> x13, matrix products: 6.71 us -> 5.01 us  [mv(): jnp.einsum('...ij,...j->...i', a, v, precision=exact, preferred_element_t...]
    another operation x6 -> x0, other arithmetic: 1.31 us -> none  [the longest x2 1.14 us: from_other_groups(): maps = jnp.stack(received)]
    concatenate x2 -> x0, other arithmetic: 1.09 us -> none  [pad_pow2(): mats = jnp.concatenate((mats, eye), axis=-3)]
    dot_general x23 -> x25, matrix products: 16.6 us -> 17.4 us  [mm(): return jnp.matmul(a, b, precision=exact, preferred_element_type=jnp.float32)]
  transfers between devices with their start and end apart: 6 -> 6, of which waited for: 3 -> 3; matrix products, arithmetic and copies ran while one was open for 2% -> 8% of each run, Pallas kernels for 0% -> 0%
where the time goes in v3:
time: 94 us; the launch traced here: 93.4 us
  matrix products  28.6 us (30%)
  other arithmetic  25.9 us (28%)
  blocking collectives  21.6 us (23%)
  starting transfers between devices  8.52 us (9%)
  waiting for transfers between devices  5.93 us (6%)
  between operations  1.76 us (2%)
  local copies, waits for them, and re-layouts  1.14 us (1%)
    all_gather x2, blocking collectives, across(): gathered = lax.all_gather(pack(mat, vec), 'inner')  21.6 us
    reduce_sum x23, other arithmetic, mv_whole(): return jnp.sum(a * v[..., None, :], axis=-1)  19.4 us
    dot_general x25, matrix products, mm(): return jnp.matmul(a, b, precision=exact, preferred_element_type=jnp.float32)  17.4 us
    ppermute x6, starting transfers between devices, from_other_groups(): received.append(lax.ppermute(packed, 'outer', pairs))  8.52 us
    ppermute x6, waiting for transfers between devices, from_other_groups(): received.append(lax.ppermute(packed, 'outer', pairs))  5.93 us
    dot_general x1, matrix products, on_device(): jnp.einsum('tij,jk->tik', gains, mapped, precision=exact, preferred_eleme...  5.92 us
    dot_general x13, matrix products, mv(): jnp.einsum('...ij,...j->...i', a, v, precision=exact, preferred_element_t...  5.01 us
    select_n x4, other arithmetic, across(): state = jnp.where(kept, moved, state)  2.28 us
  transfers between devices with their start and end apart: 6, of which 3 were waited for; matrix products, arithmetic and copies ran while one was open for 8% of the time, Pallas kernels for 0%

profile of v3, /device:TPU:0, one launch (start us, length us, event | category | flops | bytes accessed | tf_op | source)
XLA Modules:
  0.0 93.4 jit_solution(4829756975452317637)
XLA Ops:
  1.8 3.3 %multiply_reduce_fusion.7 = f32[64,128]{1,0:T(8,128)S(1)} fusion(f32[64,128,128]{2,1,0:T(8,128)} %param.7, f32[64,128]{1,0:T(8,128)} %param.6), kind=kLoop, calls=%fused_computation.8 | loop fusion | flops 2088960 | bytes 4259840 | tf_op jit(solution)/shard_map/reduce_sum | solution.py:19
  5.7 5.9 %multiply_reduce_fusion.6 = (f32[64,128]{1,0:T(8,128)S(1)}, f32[64,128,128]{1,2,0:T(8,128)S(1)}) fusion(f32[64,128]{1,0:T(8,128)S(1)} %bitcast.675, f32[128,128,1]{0,1,2:T(8,128)S(1)} %convolution_bitcast_fusion.4, f32[64,128,128]{2,1,0:T(8,128)} %param.7, f32[128,128]{0,1:T(8,128)S(1)} %copy.375), kind=kOutput, calls=%fused_computation.7 | convolution fusion | flops 1613750272 | bytes 8585216 | tf_op jit(solution)/shard_map/tij,jk->tik/dot_general | solution.py:136
  11.7 2.3 %multiply_reduce_fusion.11 = (f32[32,128]{1,0:T(8,128)S(1)}, f32[32,128,128]{1,2,0:T(8,128)S(1)}) fusion(f32[32,128]{1,0:T(8,128)S(1)} %bitcast.695, f32[32,2,128,128]{2,3,1,0:T(8,128)S(1)} %bitcast.629), kind=kOutput, calls=%fused_computation.18 | convolution fusion | flops 806350848 | bytes 6324224 | tf_op jit(solution)/shard_map/dot_general | solution.py:11
  14.1 1.2 %multiply_reduce_fusion.15 = (f32[16,128]{1,0:T(8,128)S(1)}, f32[16,128,128]{1,2,0:T(8,128)S(1)}) fusion(f32[16,128]{1,0:T(8,128)S(1)} %bitcast.717, f32[16,2,128,128]{2,3,1,0:T(8,128)S(1)} %bitcast.630), kind=kOutput, calls=%fused_computation.49 | convolution fusion | flops 403175424 | bytes 3162112 | tf_op jit(solution)/shard_map/dot_general | solution.py:11
  16.0 0.7 copy-done.4
  17.8 11.4 %all-gather.2 = f32[8,129,128]{2,1,0:T(8,128)S(1)} all-gather(f32[1,129,128]{2,1,0:T(8,128)S(1)} %maximum_bitcast_fusion), channel_id=2, replica_groups=mesh['outer'=4,'inner'=8] {'inner'}, dimensions={0}, use_global_device_ids=true | all-gather | bytes 594432 | tf_op jit(solution)/shard_map/all_gather | solution.py:117
  32.6 3.6 %collective-permute-start.2 = (f32[129,128]{1,0:T(8,128)}, f32[129,128]{1,0:T(8,128)}, u32[]{:S(2)}, u32[]{:S(2)}) collective-permute-start(f32[129,128]{1,0:T(8,128)} %pad_maximum_fusion), channel_id=1, source_target_pairs={{0,24},{8,0},{16,8},{24,16},{1,25},{9,1},{17,9},{25,17},{2,26},{10... | collective-permute-start | bytes 198152 | tf_op jit(solution)/shard_map/ppermute | solution.py:111
  36.3 1.0 %collective-permute-start = (f32[129,128]{1,0:T(8,128)}, f32[129,128]{1,0:T(8,128)}, u32[]{:S(2)}, u32[]{:S(2)}) collective-permute-start(f32[129,128]{1,0:T(8,128)} %pad_maximum_fusion), channel_id=1, source_target_pairs={{0,8},{8,16},{16,24},{24,0},{1,9},{9,17},{17,25},{25,1},{2,10},{10... | collective-permute-start | bytes 198152 | tf_op jit(solution)/shard_map/ppermute | solution.py:111
  38.0 0.9 %convolution_bitcast_fusion.3 = f32[1,2,128,128]{3,2,1,0:T(8,128)} fusion(f32[2,2,128,128]{3,2,1,0:T(8,128)S(1)} %bitcast.653), kind=kOutput, calls=%fused_computation.22 | convolution fusion | flops 50331648 | bytes 393216 | tf_op jit(solution)/shard_map/dot_general | solution.py:11
  39.5 1.1 %fusion.39 = f32[128]{0:T(128)S(1)} fusion(f32[129,128]{1,0:T(8,128)} %collective-permute-done.2, f32[128]{0:T(128)} %param.11), kind=kLoop, calls=%fused_computation.130 | loop fusion | flops 32640 | bytes 66560 | tf_op jit(solution)/shard_map/reduce_sum | solution.py:19
  40.6 0.9 broadcast_select_fusion.8
  41.4 2.5 %collective-permute-done.1 = f32[129,128]{1,0:T(8,128)} collective-permute-done((f32[129,128]{1,0:T(8,128)}, f32[129,128]{1,0:T(8,128)}, u32[]{:S(2)}, u32[]{:S(2)}) %collective-permute-start.1) | collective-permute-done | bytes 66080 | tf_op jit(solution)/shard_map/ppermute | solution.py:111
  43.9 0.9 %fusion.40 = f32[128]{0:T(128)S(1)} fusion(f32[129,128]{1,0:T(8,128)} %collective-permute-done.1, f32[128]{0:T(128)S(1)} %broadcast_select_fusion.8), kind=kLoop, calls=%fused_computation.132 | loop fusion | flops 32640 | bytes 66560 | tf_op jit(solution)/shard_map/reduce_sum | solution.py:19
  45.5 0.9 %fusion.41 = f32[128]{0:T(128)S(1)} fusion(f32[129,128]{1,0:T(8,128)} %collective-permute-done, f32[128]{0:T(128)S(1)} %broadcast_select_fusion.9), kind=kLoop, calls=%fused_computation.134 | loop fusion | flops 32640 | bytes 66560 | tf_op jit(solution)/shard_map/reduce_sum | solution.py:19
  47.2 1.2 %multiply_reduce_fusion.29 = f32[128]{0:T(128)S(1)} fusion(f32[128]{0:T(128)S(1)} %broadcast_select_fusion.10, f32[1,2,128,128]{3,2,1,0:T(8,128)} %convolution_bitcast_fusion.3), kind=kOutput, calls=%fused_computation.145 | convolution fusion | flops 25198464 | bytes 132096 | tf_op jit(solution)/shard_map/dot_general | solution.py:11
  48.4 1.0 %fusion.10 = f32[128]{0:T(128)S(1)} fusion(f32[128]{0:T(128)S(1)} %multiply_reduce_fusion.29, f32[1,2,128,128]{3,2,1,0:T(8,128)} %convolution_bitcast_fusion.3, f32[1,2,128]{2,1,0:T(2,128)S(1)} %add_bitcast_fusion.2), kind=kOutput, calls=%fused_computation.37 | convolution fusion | flops 196864 | bytes 67584 | tf_op jit(solution)/shard_map/...ij,...j->...i/dot_general | solution.py:15
  49.4 1.0 %multiply_reduce_fusion.26 = f32[2,128]{1,0:T(2,128)S(1)} fusion(f32[2,128,128]{1,2,0:T(8,128)} %copy-done.5, f32[128]{0:T(128)S(1)} %fusion.10), kind=kLoop, calls=%fused_computation.104 | loop fusion | flops 65280 | bytes 132608 | tf_op jit(solution)/shard_map/reduce_sum | solution.py:19
  50.6 1.3 %multiply_reduce_fusion.18 = f32[8,128]{1,0:T(8,128)S(1)} fusion(f32[8,128,128]{1,2,0:T(8,128)} %copy-done.4, f32[8,128]{1,0:T(8,128)S(1)} %bitcast.731), kind=kLoop, calls=%fused_computation.58 | loop fusion | flops 261120 | bytes 532480 | tf_op jit(solution)/shard_map/reduce_sum | solution.py:19
  52.4 0.9 multiply_reduce_fusion.10
  53.3 1.5 %multiply_reduce_fusion.5 = f32[64,128]{1,0:T(8,128)S(1)} fusion(f32[64,128,128]{1,2,0:T(8,128)S(1)} %copy-done.3, f32[64,128]{1,0:T(8,128)S(1)} %bitcast.679), kind=kLoop, calls=%fused_computation.6 | loop fusion | flops 2088960 | bytes 4259840 | tf_op jit(solution)/shard_map/reduce_sum | solution.py:19
  54.9 1.5 %multiply_reduce_fusion.4 = f32[64,128]{1,0:T(8,128)S(1)} fusion(f32[64,128,128]{1,2,0:T(8,128)S(1)} %copy-done.3, f32[64,128]{1,0:T(8,128)S(1)} %bitcast.676), kind=kLoop, calls=%fused_computation.5 | loop fusion | flops 2088960 | bytes 4259840 | tf_op jit(solution)/shard_map/reduce_sum | solution.py:19
  56.7 1.2 %multiply_reduce_fusion.3 = f32[64,128]{1,0:T(8,128)S(1)} fusion(f32[64,128,128]{2,1,0:T(8,128)S(1)} %copy-done.1, f32[64,128]{1,0:T(8,128)S(1)} %fusion.83), kind=kLoop, calls=%fused_computation.4 | loop fusion | flops 2088960 | bytes 4259840 | tf_op jit(solution)/shard_map/reduce_sum | solution.py:19
  57.9 1.2 %multiply_reduce_fusion.2 = f32[64,128]{1,0:T(8,128)S(1)} fusion(f32[64,128,128]{2,1,0:T(8,128)S(1)} %copy-done.1, f32[64,128]{1,0:T(8,128)S(1)} %bitcast.677), kind=kLoop, calls=%fused_computation.3 | loop fusion | flops 2088960 | bytes 4259840 | tf_op jit(solution)/shard_map/reduce_sum | solution.py:19
  59.2 3.9 %multiply_reduce_fusion.9 = (f32[32,128]{1,0:T(8,128)S(1)}, f32[32,128,128]{1,2,0:T(8,128)S(1)}) fusion(f32[32,128]{1,0:T(8,128)S(1)} %bitcast.696, f32[32,2,128,128]{3,2,1,0:T(8,128)S(1)} %bitcast.628), kind=kOutput, calls=%fused_computation.16 | convolution fusion | flops 806350848 | bytes 6324224 | tf_op jit(solution)/shard_map/dot_general | solution.py:11
  63.2 1.2 %multiply_reduce_fusion.13 = (f32[16,128]{1,0:T(8,128)S(1)}, f32[16,128,128]{1,2,0:T(8,128)S(1)}) fusion(f32[16,128]{1,0:T(8,128)S(1)} %bitcast.718, f32[16,2,128,128]{2,3,1,0:T(8,128)S(1)} %bitcast.631), kind=kOutput, calls=%fused_computation.47 | convolution fusion | flops 403175424 | bytes 3162112 | tf_op jit(solution)/shard_map/dot_general | solution.py:11
  66.4 10.2 %all-gather.3 = f32[8,129,128]{2,1,0:T(8,128)S(1)} all-gather(f32[1,129,128]{2,1,0:T(8,128)S(1)} %maximum_bitcast_fusion.1), channel_id=3, replica_groups=mesh['outer'=4,'inner'=8] {'inner'}, dimensions={0}, use_global_device_ids=true | all-gather | bytes 594432 | tf_op jit(solution)/shard_map/all_gather | solution.py:117
  78.9 2.4 %collective-permute-start.4 = (f32[129,128]{1,0:T(8,128)S(1)}, f32[129,128]{1,0:T(8,128)S(1)}, u32[]{:S(2)}, u32[]{:S(2)}) collective-permute-start(f32[129,128]{1,0:T(8,128)S(1)} %pad_maximum_fusion.1), channel_id=1, source_target_pairs={{0,16},{8,24},{16,0},{24,8},{1,17},{9,25},{17,1},{25,9},{2,18},{10... | collective-permute-start | bytes 198152 | tf_op jit(solution)/shard_map/ppermute | solution.py:111
  81.2 1.4 %collective-permute-start.3 = (f32[129,128]{1,0:T(8,128)S(1)}, f32[129,128]{1,0:T(8,128)S(1)}, u32[]{:S(2)}, u32[]{:S(2)}) collective-permute-start(f32[129,128]{1,0:T(8,128)S(1)} %pad_maximum_fusion.1), channel_id=1, source_target_pairs={{0,24},{8,0},{16,8},{24,16},{1,25},{9,1},{17,9},{25,17},{2,26},{10... | collective-permute-start | bytes 198152 | tf_op jit(solution)/shard_map/ppermute | solution.py:111
  84.2 1.5 %collective-permute-done.5 = f32[129,128]{1,0:T(8,128)S(1)} collective-permute-done((f32[129,128]{1,0:T(8,128)S(1)}, f32[129,128]{1,0:T(8,128)S(1)}, u32[]{:S(2)}, u32[]{:S(2)}) %collective-permute-start.5) | collective-permute-done | bytes 66080 | tf_op jit(solution)/shard_map/ppermute | solution.py:111
  85.8 1.9 %collective-permute-done.4 = f32[129,128]{1,0:T(8,128)S(1)} collective-permute-done((f32[129,128]{1,0:T(8,128)S(1)}, f32[129,128]{1,0:T(8,128)S(1)}, u32[]{:S(2)}, u32[]{:S(2)}) %collective-permute-start.4) | collective-permute-done | bytes 66080 | tf_op jit(solution)/shard_map/ppermute | solution.py:111
  90.4 1.2 %multiply_reduce_fusion.1 = f32[64,128]{1,0:T(8,128)S(1)} fusion(f32[64,128,128]{2,1,0:T(8,128)S(1)} %copy-done.1, f32[64,128]{1,0:T(8,128)S(1)} %bitcast.680), kind=kLoop, calls=%fused_computation.2 | loop fusion | flops 2088960 | bytes 4259840 | tf_op jit(solution)/shard_map/reduce_sum | solution.py:19
  91.6 1.2 %multiply_reduce_fusion = f32[64,128]{1,0:T(8,128)S(1)} fusion(f32[64,128,128]{2,1,0:T(8,128)S(1)} %copy-done.1, f32[64,128]{1,0:T(8,128)S(1)} %bitcast.678), kind=kLoop, calls=%fused_computation.1 | loop fusion | flops 2088960 | bytes 4259840 | tf_op jit(solution)/shard_map/reduce_sum | solution.py:19
  (183 shorter events, 19.3 us)
Async XLA Ops:
  0.6 4.7 %copy-start = (f32[128,128]{1,0:T(8,128)S(1)}, f32[128,128]{1,0:T(8,128)}, u32[]{:S(2)}) copy-start(f32[128,128]{1,0:T(8,128)} %param.10) | copy-start | bytes 196612
  0.6 4.6 %copy-start.8 = (f32[128,128]{1,0:T(8,128)S(1)}, f32[128,128]{1,0:T(8,128)}, u32[]{:S(2)}) copy-start(f32[128,128]{1,0:T(8,128)} %param.9) | copy-start | bytes 196612
  11.6 3.7 %copy-start.2 = (f32[64,128,128]{1,2,0:T(8,128)}, f32[64,128,128]{1,2,0:T(8,128)S(1)}, u32[]{:S(2)}) copy-start(f32[64,128,128]{1,2,0:T(8,128)S(1)} %get-tuple-element.39) | copy-start | bytes 12582916
  14.0 15.3 %copy-start.6 = (f32[128,128]{1,0:T(8,128)S(1)}, f32[128,128]{1,0:T(8,128)}, u32[]{:S(2)}) copy-start(f32[128,128]{1,0:T(8,128)} %fusion.45) | copy-start | bytes 196612
  14.1 16.2 %copy-start.12 = (pred[4,2]{0,1:T(4,128)(4,1)S(1)}, pred[4,2]{0,1:T(4,128)(4,1)}, u32[]{:S(2)}) copy-start(pred[4,2]{0,1:T(4,128)(4,1)} %fusion.51) | copy-start | bytes 28
  16.0 0.8 copy-start.4
  17.5 11.8 %copy-start.5 = (f32[2,128,128]{1,2,0:T(8,128)}, f32[2,128,128]{1,2,0:T(8,128)S(1)}, u32[]{:S(2)}) copy-start(f32[2,128,128]{1,2,0:T(8,128)S(1)} %get-tuple-element.49) | copy-start | bytes 393220
  32.6 6.8 %collective-permute-start.2 = (f32[129,128]{1,0:T(8,128)}, f32[129,128]{1,0:T(8,128)}, u32[]{:S(2)}, u32[]{:S(2)}) collective-permute-start(f32[129,128]{1,0:T(8,128)} %pad_maximum_fusion), channel_id=1, source_target_pairs={{0,24},{8,0},{16,8},{24,16},{1,25},{9,1},{17,9},{25,17},{2,26},{10... | collective-permute-start | bytes 198152 | tf_op jit(solution)/shard_map/ppermute | solution.py:111
  36.3 7.6 %collective-permute-start.1 = (f32[129,128]{1,0:T(8,128)}, f32[129,128]{1,0:T(8,128)}, u32[]{:S(2)}, u32[]{:S(2)}) collective-permute-start(f32[129,128]{1,0:T(8,128)} %pad_maximum_fusion), channel_id=1, source_target_pairs={{0,16},{8,24},{16,0},{24,8},{1,17},{9,25},{17,1},{25,9},{2,18},{10... | collective-permute-start | bytes 198152 | tf_op jit(solution)/shard_map/ppermute | solution.py:111
  36.3 9.3 %collective-permute-start = (f32[129,128]{1,0:T(8,128)}, f32[129,128]{1,0:T(8,128)}, u32[]{:S(2)}, u32[]{:S(2)}) collective-permute-start(f32[129,128]{1,0:T(8,128)} %pad_maximum_fusion), channel_id=1, source_target_pairs={{0,8},{8,16},{16,24},{24,0},{1,9},{9,17},{17,25},{25,1},{2,10},{10... | collective-permute-start | bytes 198152 | tf_op jit(solution)/shard_map/ppermute | solution.py:111
  39.4 13.9 %copy-start.3 = (f32[64,128,128]{1,2,0:T(8,128)S(1)}, f32[64,128,128]{1,2,0:T(8,128)}, u32[]{:S(2)}) copy-start(f32[64,128,128]{1,2,0:T(8,128)} %copy-done.2) | copy-start | bytes 12582916
  53.3 3.1 %copy-start.9 = (f32[128,128]{1,0:T(8,128)S(1)}, f32[128,128]{1,0:T(8,128)}, u32[]{:S(2)}) copy-start(f32[128,128]{1,0:T(8,128)} %param.9) | copy-start | bytes 196612
  53.3 3.3 %copy-start.1 = (f32[64,128,128]{2,1,0:T(8,128)S(1)}, f32[64,128,128]{2,1,0:T(8,128)}, u32[]{:S(2)}) copy-start(f32[64,128,128]{2,1,0:T(8,128)} %param.8) | copy-start | bytes 12582916
  56.4 36.4 %copy-start.10 = (f32[64,128]{1,0:T(8,128)}, f32[64,128]{1,0:T(8,128)S(1)}, u32[]{:S(2)}) copy-start(f32[64,128]{1,0:T(8,128)S(1)} %add.303) | copy-start | bytes 98308
  63.1 13.5 %copy-start.7 = (f32[128,128]{1,0:T(8,128)S(1)}, f32[128,128]{1,0:T(8,128)}, u32[]{:S(2)}) copy-start(f32[128,128]{1,0:T(8,128)} %fusion.45) | copy-start | bytes 196612
  63.1 13.5 %copy-start.11 = (pred[8]{0:T(512)(128)(4,1)S(1)}, pred[8]{0:T(512)(128)(4,1)}, u32[]{:S(2)}) copy-start(pred[8]{0:T(512)(128)(4,1)} %iota_compare_fusion.1) | copy-start | bytes 28
  78.8 7.0 %collective-permute-start.5 = (f32[129,128]{1,0:T(8,128)S(1)}, f32[129,128]{1,0:T(8,128)S(1)}, u32[]{:S(2)}, u32[]{:S(2)}) collective-permute-start(f32[129,128]{1,0:T(8,128)S(1)} %pad_maximum_fusion.1), channel_id=1, source_target_pairs={{0,8},{8,16},{16,24},{24,0},{1,9},{9,17},{17,25},{25,1},{2,10},{10... | collective-permute-start | bytes 198152 | tf_op jit(solution)/shard_map/ppermute | solution.py:111
  78.9 8.9 %collective-permute-start.4 = (f32[129,128]{1,0:T(8,128)S(1)}, f32[129,128]{1,0:T(8,128)S(1)}, u32[]{:S(2)}, u32[]{:S(2)}) collective-permute-start(f32[129,128]{1,0:T(8,128)S(1)} %pad_maximum_fusion.1), channel_id=1, source_target_pairs={{0,16},{8,24},{16,0},{24,8},{1,17},{9,25},{17,1},{25,9},{2,18},{10... | collective-permute-start | bytes 198152 | tf_op jit(solution)/shard_map/ppermute | solution.py:111
  81.2 6.7 %collective-permute-start.3 = (f32[129,128]{1,0:T(8,128)S(1)}, f32[129,128]{1,0:T(8,128)S(1)}, u32[]{:S(2)}, u32[]{:S(2)}) collective-permute-start(f32[129,128]{1,0:T(8,128)S(1)} %pad_maximum_fusion.1), channel_id=1, source_target_pairs={{0,24},{8,0},{16,8},{24,16},{1,25},{9,1},{17,9},{25,17},{2,26},{10... | collective-permute-start | bytes 198152 | tf_op jit(solution)/shard_map/ppermute | solution.py:111

commit v4 on v3

--- a/solution.py
+++ b/solution.py
@@ -107,7 +107,7 @@
     keep = []
     for shift in reversed(range(1, count)):
         step = -shift if backward else shift
-        pairs = [(i, (i + step) % count) for i in range(count)]
+        pairs = [(i, i + step) for i in range(count) if 0 <= i + step < count]
         received.append(lax.ppermute(packed, "outer", pairs))
         keep.append(me + shift <= count - 1 if backward else me - shift >= 0)
     return received, keep

time: 94 us -> 99.7 us (1.061)
  starting transfers between devices: 8.52 us -> 14.4 us
    ppermute x6, starting transfers between devices: 8.52 us -> 14.4 us  [from_other_groups(): received.append(lax.ppermute(packed, 'outer', pairs))]
  transfers between devices with their start and end apart: 6 -> 6, of which waited for: 3 -> 2; matrix products, arithmetic and copies ran while one was open for 8% -> 8% of each run, Pallas kernels for 0% -> 0%
where the time goes in v4:
time: 99.7 us; the launch traced here: 99 us
  matrix products  28.6 us (29%)
  other arithmetic  25.9 us (26%)
  blocking collectives  21.6 us (22%)
  starting transfers between devices  14.4 us (14%)
  waiting for transfers between devices  5.61 us (6%)
  between operations  1.79 us (2%)
  local copies, waits for them, and re-layouts  1.14 us (1%)
    all_gather x2, blocking collectives, across(): gathered = lax.all_gather(pack(mat, vec), 'inner')  21.6 us
    reduce_sum x23, other arithmetic, mv_whole(): return jnp.sum(a * v[..., None, :], axis=-1)  19.4 us
    dot_general x25, matrix products, mm(): return jnp.matmul(a, b, precision=exact, preferred_element_type=jnp.float32)  17.4 us
    ppermute x6, starting transfers between devices, from_other_groups(): received.append(lax.ppermute(packed, 'outer', pairs))  14.4 us
    dot_general x1, matrix products, on_device(): jnp.einsum('tij,jk->tik', gains, mapped, precision=exact, preferred_eleme...  5.92 us
    ppermute x6, waiting for transfers between devices, from_other_groups(): received.append(lax.ppermute(packed, 'outer', pairs))  5.61 us
    dot_general x13, matrix products, mv(): jnp.einsum('...ij,...j->...i', a, v, precision=exact, preferred_element_t...  5.01 us
    select_n x4, other arithmetic, across(): state = jnp.where(kept, moved, state)  2.28 us
  transfers between devices with their start and end apart: 6, of which 2 were waited for; matrix products, arithmetic and copies ran while one was open for 8% of the time, Pallas kernels for 0%

profile of v4, /device:TPU:0, one launch (start us, length us, event | category | flops | bytes accessed | tf_op | source)
XLA Modules:
  0.0 99.0 jit_solution(6178828039130756624)
XLA Ops:
  1.8 3.3 %multiply_reduce_fusion.7 = f32[64,128]{1,0:T(8,128)S(1)} fusion(f32[64,128,128]{2,1,0:T(8,128)} %param.7, f32[64,128]{1,0:T(8,128)} %param.6), kind=kLoop, calls=%fused_computation.8 | loop fusion | flops 2088960 | bytes 4259840 | tf_op jit(solution)/shard_map/reduce_sum | solution.py:19
  5.7 5.9 %multiply_reduce_fusion.6 = (f32[64,128]{1,0:T(8,128)S(1)}, f32[64,128,128]{1,2,0:T(8,128)S(1)}) fusion(f32[64,128]{1,0:T(8,128)S(1)} %bitcast.675, f32[128,128,1]{0,1,2:T(8,128)S(1)} %convolution_bitcast_fusion.4, f32[64,128,128]{2,1,0:T(8,128)} %param.7, f32[128,128]{0,1:T(8,128)S(1)} %copy.375), kind=kOutput, calls=%fused_computation.7 | convolution fusion | flops 1613750272 | bytes 8585216 | tf_op jit(solution)/shard_map/tij,jk->tik/dot_general | solution.py:136
  11.7 2.3 %multiply_reduce_fusion.11 = (f32[32,128]{1,0:T(8,128)S(1)}, f32[32,128,128]{1,2,0:T(8,128)S(1)}) fusion(f32[32,128]{1,0:T(8,128)S(1)} %bitcast.695, f32[32,2,128,128]{2,3,1,0:T(8,128)S(1)} %bitcast.629), kind=kOutput, calls=%fused_computation.18 | convolution fusion | flops 806350848 | bytes 6324224 | tf_op jit(solution)/shard_map/dot_general | solution.py:11
  14.1 1.2 %multiply_reduce_fusion.15 = (f32[16,128]{1,0:T(8,128)S(1)}, f32[16,128,128]{1,2,0:T(8,128)S(1)}) fusion(f32[16,128]{1,0:T(8,128)S(1)} %bitcast.717, f32[16,2,128,128]{2,3,1,0:T(8,128)S(1)} %bitcast.630), kind=kOutput, calls=%fused_computation.49 | convolution fusion | flops 403175424 | bytes 3162112 | tf_op jit(solution)/shard_map/dot_general | solution.py:11
  17.8 11.4 %all-gather.2 = f32[8,129,128]{2,1,0:T(8,128)S(1)} all-gather(f32[1,129,128]{2,1,0:T(8,128)S(1)} %maximum_bitcast_fusion), channel_id=2, replica_groups=mesh['outer'=4,'inner'=8] {'inner'}, dimensions={0}, use_global_device_ids=true | all-gather | bytes 594432 | tf_op jit(solution)/shard_map/all_gather | solution.py:117
  32.6 6.1 %collective-permute-start.2 = (f32[129,128]{1,0:T(8,128)}, f32[129,128]{1,0:T(8,128)}, u32[]{:S(2)}, u32[]{:S(2)}) collective-permute-start(f32[129,128]{1,0:T(8,128)} %pad_maximum_fusion), channel_id=1, source_target_pairs={{0,24},{1,25},{2,26},{3,27},{4,28},{5,29},{6,30},{7,31}} | collective-permute-start | bytes 198152 | tf_op jit(solution)/shard_map/ppermute | solution.py:111
  38.8 1.9 %collective-permute-start.1 = (f32[129,128]{1,0:T(8,128)}, f32[129,128]{1,0:T(8,128)}, u32[]{:S(2)}, u32[]{:S(2)}) collective-permute-start(f32[129,128]{1,0:T(8,128)} %pad_maximum_fusion), channel_id=1, source_target_pairs={{0,16},{8,24},{1,17},{9,25},{2,18},{10,26},{3,19},{11,27},{4,20},{... | collective-permute-start | bytes 198152 | tf_op jit(solution)/shard_map/ppermute | solution.py:111
  40.7 2.5 %collective-permute-start = (f32[129,128]{1,0:T(8,128)}, f32[129,128]{1,0:T(8,128)}, u32[]{:S(2)}, u32[]{:S(2)}) collective-permute-start(f32[129,128]{1,0:T(8,128)} %pad_maximum_fusion), channel_id=1, source_target_pairs={{0,8},{8,16},{16,24},{1,9},{9,17},{17,25},{2,10},{10,18},{18,26},{... | collective-permute-start | bytes 198152 | tf_op jit(solution)/shard_map/ppermute | solution.py:111
  43.9 0.9 convolution_bitcast_fusion.3
  45.4 1.1 %fusion.39 = f32[128]{0:T(128)S(1)} fusion(f32[129,128]{1,0:T(8,128)} %collective-permute-done.2, f32[128]{0:T(128)} %param.11), kind=kLoop, calls=%fused_computation.130 | loop fusion | flops 32640 | bytes 66560 | tf_op jit(solution)/shard_map/reduce_sum | solution.py:19
  46.5 0.9 broadcast_select_fusion.8
  47.3 0.9 fusion.40
  49.0 0.9 fusion.41
  50.6 1.2 %multiply_reduce_fusion.29 = f32[128]{0:T(128)S(1)} fusion(f32[128]{0:T(128)S(1)} %broadcast_select_fusion.10, f32[1,2,128,128]{3,2,1,0:T(8,128)} %convolution_bitcast_fusion.3), kind=kOutput, calls=%fused_computation.145 | convolution fusion | flops 25198464 | bytes 132096 | tf_op jit(solution)/shard_map/dot_general | solution.py:11
  51.8 1.0 %fusion.10 = f32[128]{0:T(128)S(1)} fusion(f32[128]{0:T(128)S(1)} %multiply_reduce_fusion.29, f32[1,2,128,128]{3,2,1,0:T(8,128)} %convolution_bitcast_fusion.3, f32[1,2,128]{2,1,0:T(2,128)S(1)} %add_bitcast_fusion.2), kind=kOutput, calls=%fused_computation.37 | convolution fusion | flops 196864 | bytes 67584 | tf_op jit(solution)/shard_map/...ij,...j->...i/dot_general | solution.py:15
  52.8 1.0 %multiply_reduce_fusion.26 = f32[2,128]{1,0:T(2,128)S(1)} fusion(f32[2,128,128]{1,2,0:T(8,128)} %copy-done.5, f32[128]{0:T(128)S(1)} %fusion.10), kind=kLoop, calls=%fused_computation.104 | loop fusion | flops 65280 | bytes 132608 | tf_op jit(solution)/shard_map/reduce_sum | solution.py:19
  54.1 1.3 %multiply_reduce_fusion.18 = f32[8,128]{1,0:T(8,128)S(1)} fusion(f32[8,128,128]{1,2,0:T(8,128)} %copy-done.4, f32[8,128]{1,0:T(8,128)S(1)} %bitcast.731), kind=kLoop, calls=%fused_computation.58 | loop fusion | flops 261120 | bytes 532480 | tf_op jit(solution)/shard_map/reduce_sum | solution.py:19
  55.8 0.9 multiply_reduce_fusion.10
  56.8 1.5 %multiply_reduce_fusion.5 = f32[64,128]{1,0:T(8,128)S(1)} fusion(f32[64,128,128]{1,2,0:T(8,128)S(1)} %copy-done.3, f32[64,128]{1,0:T(8,128)S(1)} %bitcast.679), kind=kLoop, calls=%fused_computation.6 | loop fusion | flops 2088960 | bytes 4259840 | tf_op jit(solution)/shard_map/reduce_sum | solution.py:19
  58.3 1.5 %multiply_reduce_fusion.4 = f32[64,128]{1,0:T(8,128)S(1)} fusion(f32[64,128,128]{1,2,0:T(8,128)S(1)} %copy-done.3, f32[64,128]{1,0:T(8,128)S(1)} %bitcast.676), kind=kLoop, calls=%fused_computation.5 | loop fusion | flops 2088960 | bytes 4259840 | tf_op jit(solution)/shard_map/reduce_sum | solution.py:19
  60.1 1.2 %multiply_reduce_fusion.3 = f32[64,128]{1,0:T(8,128)S(1)} fusion(f32[64,128,128]{2,1,0:T(8,128)S(1)} %copy-done.1, f32[64,128]{1,0:T(8,128)S(1)} %fusion.83), kind=kLoop, calls=%fused_computation.4 | loop fusion | flops 2088960 | bytes 4259840 | tf_op jit(solution)/shard_map/reduce_sum | solution.py:19
  61.4 1.2 %multiply_reduce_fusion.2 = f32[64,128]{1,0:T(8,128)S(1)} fusion(f32[64,128,128]{2,1,0:T(8,128)S(1)} %copy-done.1, f32[64,128]{1,0:T(8,128)S(1)} %bitcast.677), kind=kLoop, calls=%fused_computation.3 | loop fusion | flops 2088960 | bytes 4259840 | tf_op jit(solution)/shard_map/reduce_sum | solution.py:19
  62.6 3.9 %multiply_reduce_fusion.9 = (f32[32,128]{1,0:T(8,128)S(1)}, f32[32,128,128]{1,2,0:T(8,128)S(1)}) fusion(f32[32,128]{1,0:T(8,128)S(1)} %bitcast.696, f32[32,2,128,128]{3,2,1,0:T(8,128)S(1)} %bitcast.628), kind=kOutput, calls=%fused_computation.16 | convolution fusion | flops 806350848 | bytes 6324224 | tf_op jit(solution)/shard_map/dot_general | solution.py:11
  66.6 1.2 %multiply_reduce_fusion.13 = (f32[16,128]{1,0:T(8,128)S(1)}, f32[16,128,128]{1,2,0:T(8,128)S(1)}) fusion(f32[16,128]{1,0:T(8,128)S(1)} %bitcast.718, f32[16,2,128,128]{2,3,1,0:T(8,128)S(1)} %bitcast.631), kind=kOutput, calls=%fused_computation.47 | convolution fusion | flops 403175424 | bytes 3162112 | tf_op jit(solution)/shard_map/dot_general | solution.py:11
  69.8 10.2 %all-gather.3 = f32[8,129,128]{2,1,0:T(8,128)S(1)} all-gather(f32[1,129,128]{2,1,0:T(8,128)S(1)} %maximum_bitcast_fusion.1), channel_id=3, replica_groups=mesh['outer'=4,'inner'=8] {'inner'}, dimensions={0}, use_global_device_ids=true | all-gather | bytes 594432 | tf_op jit(solution)/shard_map/all_gather | solution.py:117
  82.2 1.3 %collective-permute-start.5 = (f32[129,128]{1,0:T(8,128)S(1)}, f32[129,128]{1,0:T(8,128)S(1)}, u32[]{:S(2)}, u32[]{:S(2)}) collective-permute-start(f32[129,128]{1,0:T(8,128)S(1)} %pad_maximum_fusion.1), channel_id=1, source_target_pairs={{24,0},{25,1},{26,2},{27,3},{28,4},{29,5},{30,6},{31,7}} | collective-permute-start | bytes 198152 | tf_op jit(solution)/shard_map/ppermute | solution.py:111
  83.5 1.3 %collective-permute-start.4 = (f32[129,128]{1,0:T(8,128)S(1)}, f32[129,128]{1,0:T(8,128)S(1)}, u32[]{:S(2)}, u32[]{:S(2)}) collective-permute-start(f32[129,128]{1,0:T(8,128)S(1)} %pad_maximum_fusion.1), channel_id=1, source_target_pairs={{16,0},{24,8},{17,1},{25,9},{18,2},{26,10},{19,3},{27,11},{20,4},{... | collective-permute-start | bytes 198152 | tf_op jit(solution)/shard_map/ppermute | solution.py:111
  84.8 1.3 %collective-permute-start.3 = (f32[129,128]{1,0:T(8,128)S(1)}, f32[129,128]{1,0:T(8,128)S(1)}, u32[]{:S(2)}, u32[]{:S(2)}) collective-permute-start(f32[129,128]{1,0:T(8,128)S(1)} %pad_maximum_fusion.1), channel_id=1, source_target_pairs={{8,0},{16,8},{24,16},{9,1},{17,9},{25,17},{10,2},{18,10},{26,18},{... | collective-permute-start | bytes 198152 | tf_op jit(solution)/shard_map/ppermute | solution.py:111
  87.7 3.0 %collective-permute-done.5 = f32[129,128]{1,0:T(8,128)S(1)} collective-permute-done((f32[129,128]{1,0:T(8,128)S(1)}, f32[129,128]{1,0:T(8,128)S(1)}, u32[]{:S(2)}, u32[]{:S(2)}) %collective-permute-start.5) | collective-permute-done | bytes 66080 | tf_op jit(solution)/shard_map/ppermute | solution.py:111
  90.8 2.6 %collective-permute-done.4 = f32[129,128]{1,0:T(8,128)S(1)} collective-permute-done((f32[129,128]{1,0:T(8,128)S(1)}, f32[129,128]{1,0:T(8,128)S(1)}, u32[]{:S(2)}, u32[]{:S(2)}) %collective-permute-start.4) | collective-permute-done | bytes 66080 | tf_op jit(solution)/shard_map/ppermute | solution.py:111
  96.0 1.2 %multiply_reduce_fusion.1 = f32[64,128]{1,0:T(8,128)S(1)} fusion(f32[64,128,128]{2,1,0:T(8,128)S(1)} %copy-done.1, f32[64,128]{1,0:T(8,128)S(1)} %bitcast.680), kind=kLoop, calls=%fused_computation.2 | loop fusion | flops 2088960 | bytes 4259840 | tf_op jit(solution)/shard_map/reduce_sum | solution.py:19
  97.2 1.2 %multiply_reduce_fusion = f32[64,128]{1,0:T(8,128)S(1)} fusion(f32[64,128,128]{2,1,0:T(8,128)S(1)} %copy-done.1, f32[64,128]{1,0:T(8,128)S(1)} %bitcast.678), kind=kLoop, calls=%fused_computation.1 | loop fusion | flops 2088960 | bytes 4259840 | tf_op jit(solution)/shard_map/reduce_sum | solution.py:19
  (183 shorter events, 20.0 us)
Async XLA Ops:
  0.6 4.7 %copy-start = (f32[128,128]{1,0:T(8,128)S(1)}, f32[128,128]{1,0:T(8,128)}, u32[]{:S(2)}) copy-start(f32[128,128]{1,0:T(8,128)} %param.10) | copy-start | bytes 196612
  0.6 4.6 %copy-start.8 = (f32[128,128]{1,0:T(8,128)S(1)}, f32[128,128]{1,0:T(8,128)}, u32[]{:S(2)}) copy-start(f32[128,128]{1,0:T(8,128)} %param.9) | copy-start | bytes 196612
  11.6 3.7 %copy-start.2 = (f32[64,128,128]{1,2,0:T(8,128)}, f32[64,128,128]{1,2,0:T(8,128)S(1)}, u32[]{:S(2)}) copy-start(f32[64,128,128]{1,2,0:T(8,128)S(1)} %get-tuple-element.39) | copy-start | bytes 12582916
  14.0 15.3 %copy-start.6 = (f32[128,128]{1,0:T(8,128)S(1)}, f32[128,128]{1,0:T(8,128)}, u32[]{:S(2)}) copy-start(f32[128,128]{1,0:T(8,128)} %fusion.45) | copy-start | bytes 196612
  14.1 16.2 %copy-start.12 = (pred[4,2]{0,1:T(4,128)(4,1)S(1)}, pred[4,2]{0,1:T(4,128)(4,1)}, u32[]{:S(2)}) copy-start(pred[4,2]{0,1:T(4,128)(4,1)} %fusion.51) | copy-start | bytes 28
  16.0 0.8 copy-start.4
  17.5 11.8 %copy-start.5 = (f32[2,128,128]{1,2,0:T(8,128)}, f32[2,128,128]{1,2,0:T(8,128)S(1)}, u32[]{:S(2)}) copy-start(f32[2,128,128]{1,2,0:T(8,128)S(1)} %get-tuple-element.49) | copy-start | bytes 393220
  32.6 12.7 %collective-permute-start.2 = (f32[129,128]{1,0:T(8,128)}, f32[129,128]{1,0:T(8,128)}, u32[]{:S(2)}, u32[]{:S(2)}) collective-permute-start(f32[129,128]{1,0:T(8,128)} %pad_maximum_fusion), channel_id=1, source_target_pairs={{0,24},{1,25},{2,26},{3,27},{4,28},{5,29},{6,30},{7,31}} | collective-permute-start | bytes 198152 | tf_op jit(solution)/shard_map/ppermute | solution.py:111
  38.8 8.6 %collective-permute-start.1 = (f32[129,128]{1,0:T(8,128)}, f32[129,128]{1,0:T(8,128)}, u32[]{:S(2)}, u32[]{:S(2)}) collective-permute-start(f32[129,128]{1,0:T(8,128)} %pad_maximum_fusion), channel_id=1, source_target_pairs={{0,16},{8,24},{1,17},{9,25},{2,18},{10,26},{3,19},{11,27},{4,20},{... | collective-permute-start | bytes 198152 | tf_op jit(solution)/shard_map/ppermute | solution.py:111
  40.7 8.3 %collective-permute-start = (f32[129,128]{1,0:T(8,128)}, f32[129,128]{1,0:T(8,128)}, u32[]{:S(2)}, u32[]{:S(2)}) collective-permute-start(f32[129,128]{1,0:T(8,128)} %pad_maximum_fusion), channel_id=1, source_target_pairs={{0,8},{8,16},{16,24},{1,9},{9,17},{17,25},{2,10},{10,18},{18,26},{... | collective-permute-start | bytes 198152 | tf_op jit(solution)/shard_map/ppermute | solution.py:111
  45.3 11.4 %copy-start.3 = (f32[64,128,128]{1,2,0:T(8,128)S(1)}, f32[64,128,128]{1,2,0:T(8,128)}, u32[]{:S(2)}) copy-start(f32[64,128,128]{1,2,0:T(8,128)} %copy-done.2) | copy-start | bytes 12582916
  56.8 3.1 %copy-start.9 = (f32[128,128]{1,0:T(8,128)S(1)}, f32[128,128]{1,0:T(8,128)}, u32[]{:S(2)}) copy-start(f32[128,128]{1,0:T(8,128)} %param.9) | copy-start | bytes 196612
  56.8 3.3 %copy-start.1 = (f32[64,128,128]{2,1,0:T(8,128)S(1)}, f32[64,128,128]{2,1,0:T(8,128)}, u32[]{:S(2)}) copy-start(f32[64,128,128]{2,1,0:T(8,128)} %param.8) | copy-start | bytes 12582916
  59.9 38.5 %copy-start.10 = (f32[64,128]{1,0:T(8,128)}, f32[64,128]{1,0:T(8,128)S(1)}, u32[]{:S(2)}) copy-start(f32[64,128]{1,0:T(8,128)S(1)} %add.303) | copy-start | bytes 98308
  66.6 13.5 %copy-start.7 = (f32[128,128]{1,0:T(8,128)S(1)}, f32[128,128]{1,0:T(8,128)}, u32[]{:S(2)}) copy-start(f32[128,128]{1,0:T(8,128)} %fusion.45) | copy-start | bytes 196612
  66.6 13.5 %copy-start.11 = (pred[8]{0:T(512)(128)(4,1)S(1)}, pred[8]{0:T(512)(128)(4,1)}, u32[]{:S(2)}) copy-start(pred[8]{0:T(512)(128)(4,1)} %iota_compare_fusion.1) | copy-start | bytes 28
  82.2 8.5 %collective-permute-start.5 = (f32[129,128]{1,0:T(8,128)S(1)}, f32[129,128]{1,0:T(8,128)S(1)}, u32[]{:S(2)}, u32[]{:S(2)}) collective-permute-start(f32[129,128]{1,0:T(8,128)S(1)} %pad_maximum_fusion.1), channel_id=1, source_target_pairs={{24,0},{25,1},{26,2},{27,3},{28,4},{29,5},{30,6},{31,7}} | collective-permute-start | bytes 198152 | tf_op jit(solution)/shard_map/ppermute | solution.py:111
  83.5 9.9 %collective-permute-start.4 = (f32[129,128]{1,0:T(8,128)S(1)}, f32[129,128]{1,0:T(8,128)S(1)}, u32[]{:S(2)}, u32[]{:S(2)}) collective-permute-start(f32[129,128]{1,0:T(8,128)S(1)} %pad_maximum_fusion.1), channel_id=1, source_target_pairs={{16,0},{24,8},{17,1},{25,9},{18,2},{26,10},{19,3},{27,11},{20,4},{... | collective-permute-start | bytes 198152 | tf_op jit(solution)/shard_map/ppermute | solution.py:111
  84.8 8.7 %collective-permute-start.3 = (f32[129,128]{1,0:T(8,128)S(1)}, f32[129,128]{1,0:T(8,128)S(1)}, u32[]{:S(2)}, u32[]{:S(2)}) collective-permute-start(f32[129,128]{1,0:T(8,128)S(1)} %pad_maximum_fusion.1), channel_id=1, source_target_pairs={{8,0},{16,8},{24,16},{9,1},{17,9},{25,17},{10,2},{18,10},{26,18},{... | collective-permute-start | bytes 198152 | tf_op jit(solution)/shard_map/ppermute | solution.py:111

commit v5 on v3

--- a/solution.py
+++ b/solution.py
@@ -85,7 +85,7 @@
 def reduce_maps(mats, vecs, backward):
     mats, vecs = pad_pow2(mats, vecs)
     while mats.shape[-3] > 1:
-        mats, vecs = pair_up(mats, vecs, backward)
+        mats, vecs = local_pair(mats, vecs, backward)
     return mats[..., 0, :, :], vecs[..., 0, :]
 
 
@@ -150,7 +150,7 @@
     bm, bv = backward[-1][0][0], backward[-1][1][0]
     last = me == devices - 1
     extra = jnp.where(last, predicted_all[-1], 0.0)
-    bv = bv + mv(bm, extra)
+    bv = bv + mv_whole(bm, extra)
     after_state = across(bm, bv, jnp.zeros_like(extra), True) + extra
     smoothed = spread(backward, after_state, True)
     return (filtered, smoothed)

time: 94 us -> 92.5 us (0.984)
  waiting for transfers between devices: 5.93 us -> 3.3 us
  matrix products: 28.6 us -> 26.1 us
  other arithmetic: 25.9 us -> 27.7 us
  starting transfers between devices: 8.52 us -> 9.59 us
    dot_general x13 -> x0, matrix products: 5.01 us -> none  [mv(): jnp.einsum('...ij,...j->...i', a, v, precision=exact, preferred_element_t...]
    ppermute x6, waiting for transfers between devices: 5.93 us -> 3.3 us  [from_other_groups(): received.append(lax.ppermute(packed, 'outer', pairs))]
    dot_general x25, matrix products: 17.4 us -> 19.9 us  [mm(): return jnp.matmul(a, b, precision=exact, preferred_element_type=jnp.float32)]
    ppermute x6, starting transfers between devices: 8.52 us -> 9.59 us  [from_other_groups(): received.append(lax.ppermute(packed, 'outer', pairs))]
    reduce_sum x23 -> x25, other arithmetic: 19.4 us -> 20.2 us  [mv_whole(): return jnp.sum(a * v[..., None, :], axis=-1)]
  transfers between devices with their start and end apart: 6 -> 6, of which waited for: 3 -> 2; matrix products, arithmetic and copies ran while one was open for 8% -> 11% of each run, Pallas kernels for 0% -> 0%
where the time goes in v5:
time: 92.5 us; the launch traced here: 92 us
  other arithmetic  27.7 us (30%)
  matrix products  26.1 us (28%)
  blocking collectives  21.6 us (23%)
  starting transfers between devices  9.59 us (10%)
  waiting for transfers between devices  3.3 us (4%)
  between operations  1.95 us (2%)
  local copies, waits for them, and re-layouts  1.71 us (2%)
    all_gather x2, blocking collectives, across(): gathered = lax.all_gather(pack(mat, vec), 'inner')  21.6 us
    reduce_sum x25, other arithmetic, mv_whole(): return jnp.sum(a * v[..., None, :], axis=-1)  20.2 us
    dot_general x25, matrix products, mm(): return jnp.matmul(a, b, precision=exact, preferred_element_type=jnp.float32)  19.9 us
    ppermute x6, starting transfers between devices, from_other_groups(): received.append(lax.ppermute(packed, 'outer', pairs))  9.59 us
    dot_general x1, matrix products, on_device(): jnp.einsum('tij,jk->tik', gains, mapped, precision=exact, preferred_eleme...  5.92 us
    ppermute x6, waiting for transfers between devices, from_other_groups(): received.append(lax.ppermute(packed, 'outer', pairs))  3.3 us
    select_n x4, other arithmetic, across(): state = jnp.where(kept, moved, state)  2.25 us
  transfers between devices with their start and end apart: 6, of which 2 were waited for; matrix products, arithmetic and copies ran while one was open for 11% of the time, Pallas kernels for 0%

profile of v5, /device:TPU:0, one launch (start us, length us, event | category | flops | bytes accessed | tf_op | source)
XLA Modules:
  0.0 92.0 jit_solution(7089198501411830448)
XLA Ops:
  2.3 3.3 %multiply_reduce_fusion.7 = f32[64,128]{1,0:T(8,128)S(1)} fusion(f32[64,128,128]{2,1,0:T(8,128)} %param.7, f32[64,128]{1,0:T(8,128)} %param.6), kind=kLoop, calls=%fused_computation.8 | loop fusion | flops 2088960 | bytes 4259840 | tf_op jit(solution)/shard_map/reduce_sum | solution.py:19
  6.2 5.9 %multiply_reduce_fusion.6 = (f32[64,128]{1,0:T(8,128)S(1)}, f32[64,128,128]{1,2,0:T(8,128)S(1)}) fusion(f32[64,128]{1,0:T(8,128)S(1)} %bitcast.577, f32[128,128,1]{0,1,2:T(8,128)S(1)} %convolution_bitcast_fusion, f32[64,128,128]{2,1,0:T(8,128)} %param.7, f32[128,128]{0,1:T(8,128)S(1)} %copy.409), kind=kOutput, calls=%fused_computation.7 | convolution fusion | flops 1613750272 | bytes 8585216 | tf_op jit(solution)/shard_map/tij,jk->tik/dot_general | solution.py:136
  12.2 2.3 %multiply_reduce_fusion.11 = (f32[32,128]{1,0:T(8,128)S(1)}, f32[32,128,128]{1,2,0:T(8,128)S(1)}) fusion(f32[32,128]{1,0:T(8,128)S(1)} %bitcast.597, f32[32,2,128,128]{2,3,1,0:T(8,128)S(1)} %bitcast.535), kind=kOutput, calls=%fused_computation.18 | convolution fusion | flops 806350848 | bytes 6324224 | tf_op jit(solution)/shard_map/dot_general | solution.py:11
  14.6 1.2 %multiply_reduce_fusion.15 = (f32[16,128]{1,0:T(8,128)S(1)}, f32[16,128,128]{1,2,0:T(8,128)S(1)}) fusion(f32[16,128]{1,0:T(8,128)S(1)} %bitcast.621, f32[16,2,128,128]{2,3,1,0:T(8,128)S(1)} %bitcast.536), kind=kOutput, calls=%fused_computation.29 | convolution fusion | flops 403175424 | bytes 3162112 | tf_op jit(solution)/shard_map/dot_general | solution.py:11
  16.6 0.7 copy-done.4
  18.4 11.4 %all-gather.2 = f32[8,129,128]{2,1,0:T(8,128)S(1)} all-gather(f32[1,129,128]{2,1,0:T(8,128)S(1)} %maximum_bitcast_fusion), channel_id=2, replica_groups=mesh['outer'=4,'inner'=8] {'inner'}, dimensions={0}, use_global_device_ids=true | all-gather | bytes 594432 | tf_op jit(solution)/shard_map/all_gather | solution.py:117
  32.3 3.6 %collective-permute-start.2 = (f32[129,128]{1,0:T(8,128)}, f32[129,128]{1,0:T(8,128)}, u32[]{:S(2)}, u32[]{:S(2)}) collective-permute-start(f32[129,128]{1,0:T(8,128)} %pad_maximum_fusion), channel_id=1, source_target_pairs={{0,24},{8,0},{16,8},{24,16},{1,25},{9,1},{17,9},{25,17},{2,26},{10... | collective-permute-start | bytes 198152 | tf_op jit(solution)/shard_map/ppermute | solution.py:111
  35.9 1.0 %collective-permute-start = (f32[129,128]{1,0:T(8,128)}, f32[129,128]{1,0:T(8,128)}, u32[]{:S(2)}, u32[]{:S(2)}) collective-permute-start(f32[129,128]{1,0:T(8,128)} %pad_maximum_fusion), channel_id=1, source_target_pairs={{0,8},{8,16},{16,24},{24,0},{1,9},{9,17},{17,25},{25,1},{2,10},{10... | collective-permute-start | bytes 198152 | tf_op jit(solution)/shard_map/ppermute | solution.py:111
  37.6 1.3 %multiply_reduce_fusion.29 = (f32[4,128]{1,0:T(4,128)S(1)}, f32[4,128,128]{1,2,0:T(8,128)}) fusion(f32[4,128]{1,0:T(4,128)S(1)} %bitcast.666, f32[4,2,128,128]{3,2,1,0:T(8,128)S(1)} %bitcast.544), kind=kOutput, calls=%fused_computation.67 | convolution fusion | flops 100793856 | bytes 790528 | tf_op jit(solution)/shard_map/dot_general | solution.py:11
  40.1 1.9 %multiply_reduce_fusion.37 = (f32[2,128]{1,0:T(2,128)S(1)}, f32[2,128,128]{1,2,0:T(8,128)}) fusion(f32[2,128]{1,0:T(2,128)S(1)} %maximum_bitcast_fusion.4, f32[2,2,128,128]{2,3,1,0:T(8,128)} %bitcast.550), kind=kOutput, calls=%fused_computation.95 | convolution fusion | flops 50396928 | bytes 395264 | tf_op jit(solution)/shard_map/dot_general | solution.py:11
  42.0 1.1 %fusion.24 = f32[128]{0:T(128)S(1)} fusion(f32[129,128]{1,0:T(8,128)} %collective-permute-done.2, f32[128]{0:T(128)S(1)} %copy-done.11), kind=kLoop, calls=%fused_computation.118 | loop fusion | flops 32640 | bytes 66560 | tf_op jit(solution)/shard_map/reduce_sum | solution.py:19
  43.1 0.8 broadcast_select_fusion.8
  44.0 0.9 %fusion.25 = f32[128]{0:T(128)S(1)} fusion(f32[129,128]{1,0:T(8,128)} %collective-permute-done.1, f32[128]{0:T(128)S(1)} %broadcast_select_fusion.8), kind=kLoop, calls=%fused_computation.120 | loop fusion | flops 32640 | bytes 66560 | tf_op jit(solution)/shard_map/reduce_sum | solution.py:19
  45.6 0.9 %fusion.26 = f32[128]{0:T(128)S(1)} fusion(f32[129,128]{1,0:T(8,128)} %collective-permute-done, f32[128]{0:T(128)S(1)} %broadcast_select_fusion.9), kind=kLoop, calls=%fused_computation.122 | loop fusion | flops 32640 | bytes 66560 | tf_op jit(solution)/shard_map/reduce_sum | solution.py:19
  47.3 1.1 %multiply_reduce_fusion.42 = f32[128]{0:T(128)S(1)} fusion(f32[128]{0:T(128)S(1)} %broadcast_select_fusion.10, f32[1,2,128,128]{2,3,1,0:T(8,128)} %bitcast.558), kind=kOutput, calls=%fused_computation.134 | convolution fusion | flops 25198464 | bytes 132096 | tf_op jit(solution)/shard_map/dot_general | solution.py:11
  48.4 1.0 %multiply_reduce_fusion.36 = f32[2,128]{1,0:T(2,128)S(1)} fusion(f32[2,128,128]{1,2,0:T(8,128)} %copy-done.5, f32[128]{0:T(128)S(1)} %bitcast.688), kind=kLoop, calls=%fused_computation.94 | loop fusion | flops 65280 | bytes 132608 | tf_op jit(solution)/shard_map/reduce_sum | solution.py:19
  49.6 1.3 %multiply_reduce_fusion.20 = f32[8,128]{1,0:T(8,128)S(1)} fusion(f32[8,128,128]{1,2,0:T(8,128)} %copy-done.4, f32[8,128]{1,0:T(8,128)S(1)} %bitcast.639), kind=kLoop, calls=%fused_computation.40 | loop fusion | flops 261120 | bytes 532480 | tf_op jit(solution)/shard_map/reduce_sum | solution.py:19
  51.3 0.9 multiply_reduce_fusion.10
  52.3 1.5 %multiply_reduce_fusion.5 = f32[64,128]{1,0:T(8,128)S(1)} fusion(f32[64,128,128]{1,2,0:T(8,128)S(1)} %copy-done.3, f32[64,128]{1,0:T(8,128)S(1)} %bitcast.581), kind=kLoop, calls=%fused_computation.6 | loop fusion | flops 2088960 | bytes 4259840 | tf_op jit(solution)/shard_map/reduce_sum | solution.py:19
  53.8 1.5 %multiply_reduce_fusion.4 = f32[64,128]{1,0:T(8,128)S(1)} fusion(f32[64,128,128]{1,2,0:T(8,128)S(1)} %copy-done.3, f32[64,128]{1,0:T(8,128)S(1)} %bitcast.578), kind=kLoop, calls=%fused_computation.5 | loop fusion | flops 2088960 | bytes 4259840 | tf_op jit(solution)/shard_map/reduce_sum | solution.py:19
  55.6 1.2 %multiply_reduce_fusion.3 = f32[64,128]{1,0:T(8,128)S(1)} fusion(f32[64,128,128]{2,1,0:T(8,128)S(1)} %copy-done.1, f32[64,128]{1,0:T(8,128)S(1)} %fusion.66), kind=kLoop, calls=%fused_computation.4 | loop fusion | flops 2088960 | bytes 4259840 | tf_op jit(solution)/shard_map/reduce_sum | solution.py:19
  56.9 1.2 %multiply_reduce_fusion.2 = f32[64,128]{1,0:T(8,128)S(1)} fusion(f32[64,128,128]{2,1,0:T(8,128)S(1)} %copy-done.1, f32[64,128]{1,0:T(8,128)S(1)} %bitcast.579), kind=kLoop, calls=%fused_computation.3 | loop fusion | flops 2088960 | bytes 4259840 | tf_op jit(solution)/shard_map/reduce_sum | solution.py:19
  58.1 3.9 %multiply_reduce_fusion.9 = (f32[32,128]{1,0:T(8,128)S(1)}, f32[32,128,128]{1,2,0:T(8,128)S(1)}) fusion(f32[32,128]{1,0:T(8,128)S(1)} %bitcast.598, f32[32,2,128,128]{3,2,1,0:T(8,128)S(1)} %bitcast.534), kind=kOutput, calls=%fused_computation.16 | convolution fusion | flops 806350848 | bytes 6324224 | tf_op jit(solution)/shard_map/dot_general | solution.py:11
  62.1 1.2 %multiply_reduce_fusion.13 = (f32[16,128]{1,0:T(8,128)S(1)}, f32[16,128,128]{1,2,0:T(8,128)S(1)}) fusion(f32[16,128]{1,0:T(8,128)S(1)} %bitcast.622, f32[16,2,128,128]{2,3,1,0:T(8,128)S(1)} %bitcast.537), kind=kOutput, calls=%fused_computation.27 | convolution fusion | flops 403175424 | bytes 3162112 | tf_op jit(solution)/shard_map/dot_general | solution.py:11
  65.2 10.2 %all-gather.3 = f32[8,129,128]{2,1,0:T(8,128)S(1)} all-gather(f32[1,129,128]{2,1,0:T(8,128)S(1)} %maximum_bitcast_fusion.1), channel_id=3, replica_groups=mesh['outer'=4,'inner'=8] {'inner'}, dimensions={0}, use_global_device_ids=true | all-gather | bytes 594432 | tf_op jit(solution)/shard_map/all_gather | solution.py:117
  77.3 2.5 %collective-permute-start.5 = (f32[129,128]{1,0:T(8,128)S(1)}, f32[129,128]{1,0:T(8,128)S(1)}, u32[]{:S(2)}, u32[]{:S(2)}) collective-permute-start(f32[129,128]{1,0:T(8,128)S(1)} %pad_maximum_fusion.1), channel_id=1, source_target_pairs={{0,8},{8,16},{16,24},{24,0},{1,9},{9,17},{17,25},{25,1},{2,10},{10... | collective-permute-start | bytes 198152 | tf_op jit(solution)/shard_map/ppermute | solution.py:111
  79.8 0.9 collective-permute-start.4
  80.7 1.5 %collective-permute-start.3 = (f32[129,128]{1,0:T(8,128)S(1)}, f32[129,128]{1,0:T(8,128)S(1)}, u32[]{:S(2)}, u32[]{:S(2)}) collective-permute-start(f32[129,128]{1,0:T(8,128)S(1)} %pad_maximum_fusion.1), channel_id=1, source_target_pairs={{0,24},{8,0},{16,8},{24,16},{1,25},{9,1},{17,9},{25,17},{2,26},{10... | collective-permute-start | bytes 198152 | tf_op jit(solution)/shard_map/ppermute | solution.py:111
  83.2 0.8 collective-permute-done.5
  84.1 2.5 %collective-permute-done.4 = f32[129,128]{1,0:T(8,128)S(1)} collective-permute-done((f32[129,128]{1,0:T(8,128)S(1)}, f32[129,128]{1,0:T(8,128)S(1)}, u32[]{:S(2)}, u32[]{:S(2)}) %collective-permute-start.4) | collective-permute-done | bytes 66080 | tf_op jit(solution)/shard_map/ppermute | solution.py:111
  88.9 1.2 %multiply_reduce_fusion.1 = f32[64,128]{1,0:T(8,128)S(1)} fusion(f32[64,128,128]{2,1,0:T(8,128)S(1)} %copy-done.1, f32[64,128]{1,0:T(8,128)S(1)} %bitcast.582), kind=kLoop, calls=%fused_computation.2 | loop fusion | flops 2088960 | bytes 4259840 | tf_op jit(solution)/shard_map/reduce_sum | solution.py:19
  90.2 1.2 %multiply_reduce_fusion = f32[64,128]{1,0:T(8,128)S(1)} fusion(f32[64,128,128]{2,1,0:T(8,128)S(1)} %copy-done.1, f32[64,128]{1,0:T(8,128)S(1)} %bitcast.580), kind=kLoop, calls=%fused_computation.1 | loop fusion | flops 2088960 | bytes 4259840 | tf_op jit(solution)/shard_map/reduce_sum | solution.py:19
  (203 shorter events, 18.1 us)
Async XLA Ops:
  0.6 5.2 %copy-start = (f32[128,128]{1,0:T(8,128)S(1)}, f32[128,128]{1,0:T(8,128)}, u32[]{:S(2)}) copy-start(f32[128,128]{1,0:T(8,128)} %param.10) | copy-start | bytes 196612
  0.6 5.1 %copy-start.8 = (f32[128,128]{1,0:T(8,128)S(1)}, f32[128,128]{1,0:T(8,128)}, u32[]{:S(2)}) copy-start(f32[128,128]{1,0:T(8,128)} %param.9) | copy-start | bytes 196612
  12.1 3.7 %copy-start.2 = (f32[64,128,128]{1,2,0:T(8,128)}, f32[64,128,128]{1,2,0:T(8,128)S(1)}, u32[]{:S(2)}) copy-start(f32[64,128,128]{1,2,0:T(8,128)S(1)} %get-tuple-element.63) | copy-start | bytes 12582916
  14.5 15.3 %copy-start.14 = (pred[4,2]{1,0:T(4,128)(4,1)S(1)}, pred[4,2]{1,0:T(4,128)(4,1)}, u32[]{:S(2)}) copy-start(pred[4,2]{1,0:T(4,128)(4,1)} %fusion.32) | copy-start | bytes 28
  14.5 15.4 %copy-start.6 = (f32[128,128]{1,0:T(8,128)S(1)}, f32[128,128]{1,0:T(8,128)}, u32[]{:S(2)}) copy-start(f32[128,128]{1,0:T(8,128)} %fusion.30) | copy-start | bytes 196612
  14.5 15.4 %copy-start.12 = (pred[8]{0:T(512)(128)(4,1)S(1)}, pred[8]{0:T(512)(128)(4,1)}, u32[]{:S(2)}) copy-start(pred[8]{0:T(512)(128)(4,1)} %iota_compare_fusion.2) | copy-start | bytes 28
  15.8 26.2 %copy-start.11 = (f32[128]{0:T(128)S(1)}, f32[128]{0:T(128)}, u32[]{:S(2)}) copy-start(f32[128]{0:T(128)} %param.11) | copy-start | bytes 1540
  16.5 0.8 copy-start.4
  18.0 11.9 %copy-start.5 = (f32[2,128,128]{1,2,0:T(8,128)}, f32[2,128,128]{1,2,0:T(8,128)S(1)}, u32[]{:S(2)}) copy-start(f32[2,128,128]{1,2,0:T(8,128)S(1)} %get-tuple-element.73) | copy-start | bytes 393220
  32.3 9.7 %collective-permute-start.2 = (f32[129,128]{1,0:T(8,128)}, f32[129,128]{1,0:T(8,128)}, u32[]{:S(2)}, u32[]{:S(2)}) collective-permute-start(f32[129,128]{1,0:T(8,128)} %pad_maximum_fusion), channel_id=1, source_target_pairs={{0,24},{8,0},{16,8},{24,16},{1,25},{9,1},{17,9},{25,17},{2,26},{10... | collective-permute-start | bytes 198152 | tf_op jit(solution)/shard_map/ppermute | solution.py:111
  35.9 8.0 %collective-permute-start.1 = (f32[129,128]{1,0:T(8,128)}, f32[129,128]{1,0:T(8,128)}, u32[]{:S(2)}, u32[]{:S(2)}) collective-permute-start(f32[129,128]{1,0:T(8,128)} %pad_maximum_fusion), channel_id=1, source_target_pairs={{0,16},{8,24},{16,0},{24,8},{1,17},{9,25},{17,1},{25,9},{2,18},{10... | collective-permute-start | bytes 198152 | tf_op jit(solution)/shard_map/ppermute | solution.py:111
  35.9 9.7 %collective-permute-start = (f32[129,128]{1,0:T(8,128)}, f32[129,128]{1,0:T(8,128)}, u32[]{:S(2)}, u32[]{:S(2)}) collective-permute-start(f32[129,128]{1,0:T(8,128)} %pad_maximum_fusion), channel_id=1, source_target_pairs={{0,8},{8,16},{16,24},{24,0},{1,9},{9,17},{17,25},{25,1},{2,10},{10... | collective-permute-start | bytes 198152 | tf_op jit(solution)/shard_map/ppermute | solution.py:111
  42.0 10.3 %copy-start.3 = (f32[64,128,128]{1,2,0:T(8,128)S(1)}, f32[64,128,128]{1,2,0:T(8,128)}, u32[]{:S(2)}) copy-start(f32[64,128,128]{1,2,0:T(8,128)} %copy-done.2) | copy-start | bytes 12582916
  52.3 3.1 %copy-start.9 = (f32[128,128]{1,0:T(8,128)S(1)}, f32[128,128]{1,0:T(8,128)}, u32[]{:S(2)}) copy-start(f32[128,128]{1,0:T(8,128)} %param.9) | copy-start | bytes 196612
  52.3 3.3 %copy-start.1 = (f32[64,128,128]{2,1,0:T(8,128)S(1)}, f32[64,128,128]{2,1,0:T(8,128)}, u32[]{:S(2)}) copy-start(f32[64,128,128]{2,1,0:T(8,128)} %param.8) | copy-start | bytes 12582916
  55.3 36.0 %copy-start.10 = (f32[64,128]{1,0:T(8,128)}, f32[64,128]{1,0:T(8,128)S(1)}, u32[]{:S(2)}) copy-start(f32[64,128]{1,0:T(8,128)S(1)} %add.391) | copy-start | bytes 98308
  62.0 13.4 %copy-start.13 = (pred[4,2]{1,0:T(4,128)(4,1)S(1)}, pred[4,2]{1,0:T(4,128)(4,1)}, u32[]{:S(2)}) copy-start(pred[4,2]{1,0:T(4,128)(4,1)} %fusion.31) | copy-start | bytes 28
  62.0 13.5 %copy-start.7 = (f32[128,128]{1,0:T(8,128)S(1)}, f32[128,128]{1,0:T(8,128)}, u32[]{:S(2)}) copy-start(f32[128,128]{1,0:T(8,128)} %fusion.30) | copy-start | bytes 196612
  77.3 6.8 %collective-permute-start.5 = (f32[129,128]{1,0:T(8,128)S(1)}, f32[129,128]{1,0:T(8,128)S(1)}, u32[]{:S(2)}, u32[]{:S(2)}) collective-permute-start(f32[129,128]{1,0:T(8,128)S(1)} %pad_maximum_fusion.1), channel_id=1, source_target_pairs={{0,8},{8,16},{16,24},{24,0},{1,9},{9,17},{17,25},{25,1},{2,10},{10... | collective-permute-start | bytes 198152 | tf_op jit(solution)/shard_map/ppermute | solution.py:111
  79.8 6.8 %collective-permute-start.4 = (f32[129,128]{1,0:T(8,128)S(1)}, f32[129,128]{1,0:T(8,128)S(1)}, u32[]{:S(2)}, u32[]{:S(2)}) collective-permute-start(f32[129,128]{1,0:T(8,128)S(1)} %pad_maximum_fusion.1), channel_id=1, source_target_pairs={{0,16},{8,24},{16,0},{24,8},{1,17},{9,25},{17,1},{25,9},{2,18},{10... | collective-permute-start | bytes 198152 | tf_op jit(solution)/shard_map/ppermute | solution.py:111
  80.7 6.1 %collective-permute-start.3 = (f32[129,128]{1,0:T(8,128)S(1)}, f32[129,128]{1,0:T(8,128)S(1)}, u32[]{:S(2)}, u32[]{:S(2)}) collective-permute-start(f32[129,128]{1,0:T(8,128)S(1)} %pad_maximum_fusion.1), channel_id=1, source_target_pairs={{0,24},{8,0},{16,8},{24,16},{1,25},{9,1},{17,9},{25,17},{2,26},{10... | collective-permute-start | bytes 198152 | tf_op jit(solution)/shard_map/ppermute | solution.py:111

commit v6 on v5

--- a/solution.py
+++ b/solution.py
@@ -122,10 +122,10 @@
     index = jnp.arange(mats.shape[0])
     mine = index > me if backward else index < me
     pm, pv = reduce_maps(*keep_only(mats, vecs, mine), backward)
+    eye = jnp.eye(mat.shape[-1], dtype=jnp.float32)
     state = start
     for block, kept in zip(received, keep):
-        moved = mv_whole(block[:-1], state) + block[-1]
-        state = jnp.where(kept, moved, state)
+        state = mv_whole(jnp.where(kept, block[:-1], eye), state) + jnp.where(kept, block[-1], 0.0)
     return mv_whole(pm, state) + pv
 
 

time: 92.5 us -> 91 us (0.984)
  other arithmetic: 27.7 us -> 26 us
  waiting for transfers between devices: 3.3 us -> 4.93 us
    select_n x4 -> x0, other arithmetic: 2.25 us -> none  [across(): state = jnp.where(kept, moved, state)]
    ppermute x6, waiting for transfers between devices: 3.3 us -> 4.93 us  [from_other_groups(): received.append(lax.ppermute(packed, 'outer', pairs))]
    mul x9 -> x13, other arithmetic: 0.73 us -> 2.34 us  [mv_whole(): return jnp.sum(a * v[..., None, :], axis=-1)]
    lt x2, other arithmetic: 1.03 us -> 0.01 us  [across(): mine = index > me if backward else index < me]
  transfers between devices with their start and end apart: 6 -> 6, of which waited for: 2 -> 3; matrix products, arithmetic and copies ran while one was open for 11% -> 9% of each run, Pallas kernels for 0% -> 0%
where the time goes in v6:
time: 91 us; the launch traced here: 90.5 us
  matrix products  26.1 us (29%)
  other arithmetic  26 us (29%)
  blocking collectives  21.6 us (24%)
  starting transfers between devices  8.78 us (10%)
  waiting for transfers between devices  4.93 us (5%)
  between operations  1.93 us (2%)
  local copies, waits for them, and re-layouts  1.19 us (1%)
    all_gather x2, blocking collectives, across(): gathered = lax.all_gather(pack(mat, vec), 'inner')  21.6 us
    reduce_sum x25, other arithmetic, mv_whole(): return jnp.sum(a * v[..., None, :], axis=-1)  20.2 us
    dot_general x25, matrix products, mm(): return jnp.matmul(a, b, precision=exact, preferred_element_type=jnp.float32)  20 us
    ppermute x6, starting transfers between devices, from_other_groups(): received.append(lax.ppermute(packed, 'outer', pairs))  8.78 us
    dot_general x1, matrix products, on_device(): jnp.einsum('tij,jk->tik', gains, mapped, precision=exact, preferred_eleme...  5.92 us
    ppermute x6, waiting for transfers between devices, from_other_groups(): received.append(lax.ppermute(packed, 'outer', pairs))  4.93 us
    mul x13, other arithmetic, mv_whole(): return jnp.sum(a * v[..., None, :], axis=-1)  2.34 us
  transfers between devices with their start and end apart: 6, of which 3 were waited for; matrix products, arithmetic and copies ran while one was open for 9% of the time, Pallas kernels for 0%

profile of v6, /device:TPU:0, one launch (start us, length us, event | category | flops | bytes accessed | tf_op | source)
XLA Modules:
  0.0 90.5 jit_solution(17362801341887242571)
XLA Ops:
  1.3 3.3 %multiply_reduce_fusion.7 = f32[64,128]{1,0:T(8,128)S(1)} fusion(f32[64,128,128]{2,1,0:T(8,128)} %param.7, f32[64,128]{1,0:T(8,128)} %param.6), kind=kLoop, calls=%fused_computation.8 | loop fusion | flops 2088960 | bytes 4259840 | tf_op jit(solution)/shard_map/reduce_sum | solution.py:19
  5.2 5.9 %multiply_reduce_fusion.6 = (f32[64,128]{1,0:T(8,128)S(1)}, f32[64,128,128]{1,2,0:T(8,128)S(1)}) fusion(f32[64,128]{1,0:T(8,128)S(1)} %bitcast.568, f32[128,128,1]{0,1,2:T(8,128)S(1)} %convolution_bitcast_fusion, f32[64,128,128]{2,1,0:T(8,128)} %param.7, f32[128,128]{0,1:T(8,128)S(1)} %copy.409), kind=kOutput, calls=%fused_computation.7 | convolution fusion | flops 1613750272 | bytes 8585216 | tf_op jit(solution)/shard_map/tij,jk->tik/dot_general | solution.py:136
  11.2 2.3 %multiply_reduce_fusion.11 = (f32[32,128]{1,0:T(8,128)S(1)}, f32[32,128,128]{1,2,0:T(8,128)S(1)}) fusion(f32[32,128]{1,0:T(8,128)S(1)} %bitcast.588, f32[32,2,128,128]{2,3,1,0:T(8,128)S(1)} %bitcast.526), kind=kOutput, calls=%fused_computation.18 | convolution fusion | flops 806350848 | bytes 6324224 | tf_op jit(solution)/shard_map/dot_general | solution.py:11
  13.6 1.2 %multiply_reduce_fusion.15 = (f32[16,128]{1,0:T(8,128)S(1)}, f32[16,128,128]{1,2,0:T(8,128)S(1)}) fusion(f32[16,128]{1,0:T(8,128)S(1)} %bitcast.612, f32[16,2,128,128]{2,3,1,0:T(8,128)S(1)} %bitcast.527), kind=kOutput, calls=%fused_computation.29 | convolution fusion | flops 403175424 | bytes 3162112 | tf_op jit(solution)/shard_map/dot_general | solution.py:11
  17.3 11.4 %all-gather.2 = f32[8,129,128]{2,1,0:T(8,128)S(1)} all-gather(f32[1,129,128]{2,1,0:T(8,128)S(1)} %maximum_bitcast_fusion), channel_id=2, replica_groups=mesh['outer'=4,'inner'=8] {'inner'}, dimensions={0}, use_global_device_ids=true | all-gather | bytes 594432 | tf_op jit(solution)/shard_map/all_gather | solution.py:117
  31.3 3.6 %collective-permute-start.2 = (f32[129,128]{1,0:T(8,128)}, f32[129,128]{1,0:T(8,128)}, u32[]{:S(2)}, u32[]{:S(2)}) collective-permute-start(f32[129,128]{1,0:T(8,128)} %pad_maximum_fusion), channel_id=1, source_target_pairs={{0,24},{8,0},{16,8},{24,16},{1,25},{9,1},{17,9},{25,17},{2,26},{10... | collective-permute-start | bytes 198152 | tf_op jit(solution)/shard_map/ppermute | solution.py:111
  34.9 1.0 %collective-permute-start = (f32[129,128]{1,0:T(8,128)}, f32[129,128]{1,0:T(8,128)}, u32[]{:S(2)}, u32[]{:S(2)}) collective-permute-start(f32[129,128]{1,0:T(8,128)} %pad_maximum_fusion), channel_id=1, source_target_pairs={{0,8},{8,16},{16,24},{24,0},{1,9},{9,17},{17,25},{25,1},{2,10},{10... | collective-permute-start | bytes 198152 | tf_op jit(solution)/shard_map/ppermute | solution.py:111
  36.5 1.3 %multiply_reduce_fusion.29 = (f32[4,128]{1,0:T(4,128)S(1)}, f32[4,128,128]{1,2,0:T(8,128)}) fusion(f32[4,128]{1,0:T(4,128)S(1)} %bitcast.657, f32[4,2,128,128]{3,2,1,0:T(8,128)S(1)} %bitcast.535), kind=kOutput, calls=%fused_computation.67 | convolution fusion | flops 100793856 | bytes 790528 | tf_op jit(solution)/shard_map/dot_general | solution.py:11
  37.8 1.9 %multiply_reduce_fusion.37 = (f32[2,128]{1,0:T(2,128)S(1)}, f32[2,128,128]{1,2,0:T(8,128)}) fusion(f32[2,128]{1,0:T(2,128)S(1)} %maximum_bitcast_fusion.4, f32[2,2,128,128]{2,3,1,0:T(8,128)} %bitcast.541), kind=kOutput, calls=%fused_computation.101 | convolution fusion | flops 50396928 | bytes 395264 | tf_op jit(solution)/shard_map/dot_general | solution.py:11
  39.7 1.1 %fusion.23 = f32[128]{0:T(128)S(1)} fusion(f32[129,128]{1,0:T(8,128)} %collective-permute-done.2, f32[128]{0:T(128)} %param.11, pred[]{:T(512)S(6)} %ge.11), kind=kLoop, calls=%fused_computation.113 | loop fusion | flops 81792 | bytes 66561 | tf_op jit(solution)/shard_map/reduce_sum | solution.py:19
  40.9 0.9 fusion.40
  41.7 0.8 collective-permute-done.1
  42.5 0.9 %fusion.21 = f32[128]{0:T(128)S(1)} fusion(f32[129,128]{1,0:T(8,128)} %collective-permute-done.1, f32[128]{0:T(128)S(1)} %fusion.40, pred[]{:T(512)S(6)} %ge.10), kind=kLoop, calls=%fused_computation.111 | loop fusion | flops 81792 | bytes 66561 | tf_op jit(solution)/shard_map/reduce_sum | solution.py:19
  44.2 0.9 %fusion.19 = f32[128]{0:T(128)S(1)} fusion(f32[129,128]{1,0:T(8,128)} %collective-permute-done, f32[128]{0:T(128)S(1)} %fusion.42, pred[]{:T(512)S(6)} %ge.9), kind=kLoop, calls=%fused_computation.109 | loop fusion | flops 81792 | bytes 66561 | tf_op jit(solution)/shard_map/reduce_sum | solution.py:19
  45.8 1.1 %multiply_reduce_fusion.42 = f32[128]{0:T(128)S(1)} fusion(f32[128]{0:T(128)S(1)} %fusion.44, f32[1,2,128,128]{2,3,1,0:T(8,128)} %bitcast.549), kind=kOutput, calls=%fused_computation.140 | convolution fusion | flops 25198464 | bytes 132096 | tf_op jit(solution)/shard_map/dot_general | solution.py:11
  46.9 1.0 %multiply_reduce_fusion.36 = f32[2,128]{1,0:T(2,128)S(1)} fusion(f32[2,128,128]{1,2,0:T(8,128)} %copy-done.5, f32[128]{0:T(128)S(1)} %bitcast.678), kind=kLoop, calls=%fused_computation.100 | loop fusion | flops 65280 | bytes 132608 | tf_op jit(solution)/shard_map/reduce_sum | solution.py:19
  48.2 1.3 %multiply_reduce_fusion.20 = f32[8,128]{1,0:T(8,128)S(1)} fusion(f32[8,128,128]{1,2,0:T(8,128)} %copy-done.4, f32[8,128]{1,0:T(8,128)S(1)} %bitcast.630), kind=kLoop, calls=%fused_computation.40 | loop fusion | flops 261120 | bytes 532480 | tf_op jit(solution)/shard_map/reduce_sum | solution.py:19
  49.9 0.9 multiply_reduce_fusion.10
  50.9 1.5 %multiply_reduce_fusion.5 = f32[64,128]{1,0:T(8,128)S(1)} fusion(f32[64,128,128]{1,2,0:T(8,128)S(1)} %copy-done.3, f32[64,128]{1,0:T(8,128)S(1)} %bitcast.572), kind=kLoop, calls=%fused_computation.6 | loop fusion | flops 2088960 | bytes 4259840 | tf_op jit(solution)/shard_map/reduce_sum | solution.py:19
  52.4 1.5 %multiply_reduce_fusion.4 = f32[64,128]{1,0:T(8,128)S(1)} fusion(f32[64,128,128]{1,2,0:T(8,128)S(1)} %copy-done.3, f32[64,128]{1,0:T(8,128)S(1)} %bitcast.569), kind=kLoop, calls=%fused_computation.5 | loop fusion | flops 2088960 | bytes 4259840 | tf_op jit(solution)/shard_map/reduce_sum | solution.py:19
  54.2 1.2 %multiply_reduce_fusion.3 = f32[64,128]{1,0:T(8,128)S(1)} fusion(f32[64,128,128]{2,1,0:T(8,128)S(1)} %copy-done.1, f32[64,128]{1,0:T(8,128)S(1)} %fusion.79), kind=kLoop, calls=%fused_computation.4 | loop fusion | flops 2088960 | bytes 4259840 | tf_op jit(solution)/shard_map/reduce_sum | solution.py:19
  55.4 1.2 %multiply_reduce_fusion.2 = f32[64,128]{1,0:T(8,128)S(1)} fusion(f32[64,128,128]{2,1,0:T(8,128)S(1)} %copy-done.1, f32[64,128]{1,0:T(8,128)S(1)} %bitcast.570), kind=kLoop, calls=%fused_computation.3 | loop fusion | flops 2088960 | bytes 4259840 | tf_op jit(solution)/shard_map/reduce_sum | solution.py:19
  56.7 3.9 %multiply_reduce_fusion.9 = (f32[32,128]{1,0:T(8,128)S(1)}, f32[32,128,128]{1,2,0:T(8,128)S(1)}) fusion(f32[32,128]{1,0:T(8,128)S(1)} %bitcast.589, f32[32,2,128,128]{3,2,1,0:T(8,128)S(1)} %bitcast.525), kind=kOutput, calls=%fused_computation.16 | convolution fusion | flops 806350848 | bytes 6324224 | tf_op jit(solution)/shard_map/dot_general | solution.py:11
  60.7 1.2 %multiply_reduce_fusion.13 = (f32[16,128]{1,0:T(8,128)S(1)}, f32[16,128,128]{1,2,0:T(8,128)S(1)}) fusion(f32[16,128]{1,0:T(8,128)S(1)} %bitcast.613, f32[16,2,128,128]{2,3,1,0:T(8,128)S(1)} %bitcast.528), kind=kOutput, calls=%fused_computation.27 | convolution fusion | flops 403175424 | bytes 3162112 | tf_op jit(solution)/shard_map/dot_general | solution.py:11
  63.8 10.2 %all-gather.3 = f32[8,129,128]{2,1,0:T(8,128)S(1)} all-gather(f32[1,129,128]{2,1,0:T(8,128)S(1)} %maximum_bitcast_fusion.1), channel_id=3, replica_groups=mesh['outer'=4,'inner'=8] {'inner'}, dimensions={0}, use_global_device_ids=true | all-gather | bytes 594432 | tf_op jit(solution)/shard_map/all_gather | solution.py:117
  75.8 1.7 %collective-permute-start.5 = (f32[129,128]{1,0:T(8,128)S(1)}, f32[129,128]{1,0:T(8,128)S(1)}, u32[]{:S(2)}, u32[]{:S(2)}) collective-permute-start(f32[129,128]{1,0:T(8,128)S(1)} %pad_maximum_fusion.1), channel_id=1, source_target_pairs={{0,8},{8,16},{16,24},{24,0},{1,9},{9,17},{17,25},{25,1},{2,10},{10... | collective-permute-start | bytes 198152 | tf_op jit(solution)/shard_map/ppermute | solution.py:111
  77.6 0.9 collective-permute-start.4
  78.5 1.5 %collective-permute-start.3 = (f32[129,128]{1,0:T(8,128)S(1)}, f32[129,128]{1,0:T(8,128)S(1)}, u32[]{:S(2)}, u32[]{:S(2)}) collective-permute-start(f32[129,128]{1,0:T(8,128)S(1)} %pad_maximum_fusion.1), channel_id=1, source_target_pairs={{0,24},{8,0},{16,8},{24,16},{1,25},{9,1},{17,9},{25,17},{2,26},{10... | collective-permute-start | bytes 198152 | tf_op jit(solution)/shard_map/ppermute | solution.py:111
  81.0 1.8 %collective-permute-done.5 = f32[129,128]{1,0:T(8,128)S(1)} collective-permute-done((f32[129,128]{1,0:T(8,128)S(1)}, f32[129,128]{1,0:T(8,128)S(1)}, u32[]{:S(2)}, u32[]{:S(2)}) %collective-permute-start.5) | collective-permute-done | bytes 66080 | tf_op jit(solution)/shard_map/ppermute | solution.py:111
  82.9 2.3 %collective-permute-done.4 = f32[129,128]{1,0:T(8,128)S(1)} collective-permute-done((f32[129,128]{1,0:T(8,128)S(1)}, f32[129,128]{1,0:T(8,128)S(1)}, u32[]{:S(2)}, u32[]{:S(2)}) %collective-permute-start.4) | collective-permute-done | bytes 66080 | tf_op jit(solution)/shard_map/ppermute | solution.py:111
  87.5 1.2 %multiply_reduce_fusion.1 = f32[64,128]{1,0:T(8,128)S(1)} fusion(f32[64,128,128]{2,1,0:T(8,128)S(1)} %copy-done.1, f32[64,128]{1,0:T(8,128)S(1)} %bitcast.573), kind=kLoop, calls=%fused_computation.2 | loop fusion | flops 2088960 | bytes 4259840 | tf_op jit(solution)/shard_map/reduce_sum | solution.py:19
  88.7 1.2 %multiply_reduce_fusion = f32[64,128]{1,0:T(8,128)S(1)} fusion(f32[64,128,128]{2,1,0:T(8,128)S(1)} %copy-done.1, f32[64,128]{1,0:T(8,128)S(1)} %bitcast.571), kind=kLoop, calls=%fused_computation.1 | loop fusion | flops 2088960 | bytes 4259840 | tf_op jit(solution)/shard_map/reduce_sum | solution.py:19
  (197 shorter events, 16.6 us)
Async XLA Ops:
  0.6 4.2 %copy-start = (f32[128,128]{1,0:T(8,128)S(1)}, f32[128,128]{1,0:T(8,128)}, u32[]{:S(2)}) copy-start(f32[128,128]{1,0:T(8,128)} %param.10) | copy-start | bytes 196612
  0.6 4.1 %copy-start.8 = (f32[128,128]{1,0:T(8,128)S(1)}, f32[128,128]{1,0:T(8,128)}, u32[]{:S(2)}) copy-start(f32[128,128]{1,0:T(8,128)} %param.9) | copy-start | bytes 196612
  11.1 3.7 %copy-start.2 = (f32[64,128,128]{1,2,0:T(8,128)}, f32[64,128,128]{1,2,0:T(8,128)S(1)}, u32[]{:S(2)}) copy-start(f32[64,128,128]{1,2,0:T(8,128)S(1)} %get-tuple-element.63) | copy-start | bytes 12582916
  13.5 15.4 %copy-start.6 = (f32[128,128]{1,0:T(8,128)S(1)}, f32[128,128]{1,0:T(8,128)}, u32[]{:S(2)}) copy-start(f32[128,128]{1,0:T(8,128)} %fusion.36) | copy-start | bytes 196612
  15.5 0.8 copy-start.4
  17.0 11.9 %copy-start.5 = (f32[2,128,128]{1,2,0:T(8,128)}, f32[2,128,128]{1,2,0:T(8,128)S(1)}, u32[]{:S(2)}) copy-start(f32[2,128,128]{1,2,0:T(8,128)S(1)} %get-tuple-element.73) | copy-start | bytes 393220
  31.3 8.5 %collective-permute-start.2 = (f32[129,128]{1,0:T(8,128)}, f32[129,128]{1,0:T(8,128)}, u32[]{:S(2)}, u32[]{:S(2)}) collective-permute-start(f32[129,128]{1,0:T(8,128)} %pad_maximum_fusion), channel_id=1, source_target_pairs={{0,24},{8,0},{16,8},{24,16},{1,25},{9,1},{17,9},{25,17},{2,26},{10... | collective-permute-start | bytes 198152 | tf_op jit(solution)/shard_map/ppermute | solution.py:111
  34.9 7.6 %collective-permute-start.1 = (f32[129,128]{1,0:T(8,128)}, f32[129,128]{1,0:T(8,128)}, u32[]{:S(2)}, u32[]{:S(2)}) collective-permute-start(f32[129,128]{1,0:T(8,128)} %pad_maximum_fusion), channel_id=1, source_target_pairs={{0,16},{8,24},{16,0},{24,8},{1,17},{9,25},{17,1},{25,9},{2,18},{10... | collective-permute-start | bytes 198152 | tf_op jit(solution)/shard_map/ppermute | solution.py:111
  34.9 9.3 %collective-permute-start = (f32[129,128]{1,0:T(8,128)}, f32[129,128]{1,0:T(8,128)}, u32[]{:S(2)}, u32[]{:S(2)}) collective-permute-start(f32[129,128]{1,0:T(8,128)} %pad_maximum_fusion), channel_id=1, source_target_pairs={{0,8},{8,16},{16,24},{24,0},{1,9},{9,17},{17,25},{25,1},{2,10},{10... | collective-permute-start | bytes 198152 | tf_op jit(solution)/shard_map/ppermute | solution.py:111
  39.7 11.1 %copy-start.3 = (f32[64,128,128]{1,2,0:T(8,128)S(1)}, f32[64,128,128]{1,2,0:T(8,128)}, u32[]{:S(2)}) copy-start(f32[64,128,128]{1,2,0:T(8,128)} %copy-done.2) | copy-start | bytes 12582916
  50.8 3.1 %copy-start.9 = (f32[128,128]{1,0:T(8,128)S(1)}, f32[128,128]{1,0:T(8,128)}, u32[]{:S(2)}) copy-start(f32[128,128]{1,0:T(8,128)} %param.9) | copy-start | bytes 196612
  50.8 3.3 %copy-start.1 = (f32[64,128,128]{2,1,0:T(8,128)S(1)}, f32[64,128,128]{2,1,0:T(8,128)}, u32[]{:S(2)}) copy-start(f32[64,128,128]{2,1,0:T(8,128)} %param.8) | copy-start | bytes 12582916
  53.9 36.0 %copy-start.10 = (f32[64,128]{1,0:T(8,128)}, f32[64,128]{1,0:T(8,128)S(1)}, u32[]{:S(2)}) copy-start(f32[64,128]{1,0:T(8,128)S(1)} %add.391) | copy-start | bytes 98308
  60.6 13.4 %copy-start.11 = (pred[4,2]{1,0:T(4,128)(4,1)S(1)}, pred[4,2]{1,0:T(4,128)(4,1)}, u32[]{:S(2)}) copy-start(pred[4,2]{1,0:T(4,128)(4,1)} %fusion.37) | copy-start | bytes 28
  60.6 13.5 %copy-start.7 = (f32[128,128]{1,0:T(8,128)S(1)}, f32[128,128]{1,0:T(8,128)}, u32[]{:S(2)}) copy-start(f32[128,128]{1,0:T(8,128)} %fusion.36) | copy-start | bytes 196612
  75.8 6.9 %collective-permute-start.5 = (f32[129,128]{1,0:T(8,128)S(1)}, f32[129,128]{1,0:T(8,128)S(1)}, u32[]{:S(2)}, u32[]{:S(2)}) collective-permute-start(f32[129,128]{1,0:T(8,128)S(1)} %pad_maximum_fusion.1), channel_id=1, source_target_pairs={{0,8},{8,16},{16,24},{24,0},{1,9},{9,17},{17,25},{25,1},{2,10},{10... | collective-permute-start | bytes 198152 | tf_op jit(solution)/shard_map/ppermute | solution.py:111
  77.6 7.6 %collective-permute-start.4 = (f32[129,128]{1,0:T(8,128)S(1)}, f32[129,128]{1,0:T(8,128)S(1)}, u32[]{:S(2)}, u32[]{:S(2)}) collective-permute-start(f32[129,128]{1,0:T(8,128)S(1)} %pad_maximum_fusion.1), channel_id=1, source_target_pairs={{0,16},{8,24},{16,0},{24,8},{1,17},{9,25},{17,1},{25,9},{2,18},{10... | collective-permute-start | bytes 198152 | tf_op jit(solution)/shard_map/ppermute | solution.py:111
  78.5 6.9 %collective-permute-start.3 = (f32[129,128]{1,0:T(8,128)S(1)}, f32[129,128]{1,0:T(8,128)S(1)}, u32[]{:S(2)}, u32[]{:S(2)}) collective-permute-start(f32[129,128]{1,0:T(8,128)S(1)} %pad_maximum_fusion.1), channel_id=1, source_target_pairs={{0,24},{8,0},{16,8},{24,16},{1,25},{9,1},{17,9},{25,17},{2,26},{10... | collective-permute-start | bytes 198152 | tf_op jit(solution)/shard_map/ppermute | solution.py:111

commit v7 on v6

--- a/solution.py
+++ b/solution.py
@@ -125,7 +125,9 @@
     eye = jnp.eye(mat.shape[-1], dtype=jnp.float32)
     state = start
     for block, kept in zip(received, keep):
-        state = mv_whole(jnp.where(kept, block[:-1], eye), state) + jnp.where(kept, block[-1], 0.0)
+        mat = jnp.where(kept, block[:-1], eye)
+        shift = jnp.where(kept, block[-1], 0.0) / mat.shape[-1]
+        state = jnp.sum(mat * state[None, :] + shift[:, None], axis=-1)
     return mv_whole(pm, state) + pv
 
 

time: 91 us -> 93.8 us (1.031)
  other arithmetic: 26 us -> 28 us
  waiting for transfers between devices: 4.93 us -> 3.23 us
  matrix products: 26.1 us -> 27.2 us
    reduce_sum x0 -> x6, other arithmetic: none -> 3.74 us  [across(): state = jnp.sum(mat * state[None, :] + shift[:, None], axis=-1)]
    reduce_sum x25 -> x19, other arithmetic: 20.2 us -> 17.4 us  [mv_whole(): return jnp.sum(a * v[..., None, :], axis=-1)]
    div x0 -> x6, other arithmetic: none -> 2.21 us  [across(): shift = jnp.where(kept, block[-1], 0.0) / mat.shape[-1]]
    ppermute x6, waiting for transfers between devices: 4.93 us -> 3.23 us  [from_other_groups(): received.append(lax.ppermute(packed, 'outer', pairs))]
    mul x13 -> x7, other arithmetic: 2.34 us -> 0.71 us  [mv_whole(): return jnp.sum(a * v[..., None, :], axis=-1)]
    dot_general x25, matrix products: 20 us -> 21 us  [mm(): return jnp.matmul(a, b, precision=exact, preferred_element_type=jnp.float32)]
  transfers between devices with their start and end apart: 6 -> 6, of which waited for: 3 -> 2; matrix products, arithmetic and copies ran while one was open for 9% -> 12% of each run, Pallas kernels for 0% -> 0%
where the time goes in v7:
time: 93.8 us; the launch traced here: 93.2 us
  other arithmetic  28 us (30%)
  matrix products  27.2 us (29%)
  blocking collectives  21.6 us (23%)
  starting transfers between devices  9.6 us (10%)
  waiting for transfers between devices  3.23 us (3%)
  between operations  1.9 us (2%)
  local copies, waits for them, and re-layouts  1.7 us (2%)
    all_gather x2, blocking collectives, across(): gathered = lax.all_gather(pack(mat, vec), 'inner')  21.6 us
    dot_general x25, matrix products, mm(): return jnp.matmul(a, b, precision=exact, preferred_element_type=jnp.float32)  21 us
    reduce_sum x19, other arithmetic, mv_whole(): return jnp.sum(a * v[..., None, :], axis=-1)  17.4 us
    ppermute x6, starting transfers between devices, from_other_groups(): received.append(lax.ppermute(packed, 'outer', pairs))  9.6 us
    dot_general x1, matrix products, on_device(): jnp.einsum('tij,jk->tik', gains, mapped, precision=exact, preferred_eleme...  5.92 us
    reduce_sum x6, other arithmetic, across(): state = jnp.sum(mat * state[None, :] + shift[:, None], axis=-1)  3.74 us
    ppermute x6, waiting for transfers between devices, from_other_groups(): received.append(lax.ppermute(packed, 'outer', pairs))  3.23 us
    div x6, other arithmetic, across(): shift = jnp.where(kept, block[-1], 0.0) / mat.shape[-1]  2.21 us
  transfers between devices with their start and end apart: 6, of which 2 were waited for; matrix products, arithmetic and copies ran while one was open for 12% of the time, Pallas kernels for 0%

profile of v7, /device:TPU:0, one launch (start us, length us, event | category | flops | bytes accessed | tf_op | source)
XLA Modules:
  0.0 93.2 jit_solution(8420584449290627223)
XLA Ops:
  1.8 3.3 %multiply_reduce_fusion.7 = f32[64,128]{1,0:T(8,128)S(1)} fusion(f32[64,128,128]{2,1,0:T(8,128)} %param.7, f32[64,128]{1,0:T(8,128)} %param.6), kind=kLoop, calls=%fused_computation.8 | loop fusion | flops 2088960 | bytes 4259840 | tf_op jit(solution)/shard_map/reduce_sum | solution.py:19
  5.7 5.9 %multiply_reduce_fusion.6 = (f32[64,128]{1,0:T(8,128)S(1)}, f32[64,128,128]{1,2,0:T(8,128)S(1)}) fusion(f32[64,128]{1,0:T(8,128)S(1)} %bitcast.548, f32[128,128,1]{0,1,2:T(8,128)S(1)} %convolution_bitcast_fusion, f32[64,128,128]{2,1,0:T(8,128)} %param.7, f32[128,128]{0,1:T(8,128)S(1)} %copy.409), kind=kOutput, calls=%fused_computation.7 | convolution fusion | flops 1613750272 | bytes 8585216 | tf_op jit(solution)/shard_map/tij,jk->tik/dot_general | solution.py:138
  11.7 2.3 %multiply_reduce_fusion.11 = (f32[32,128]{1,0:T(8,128)S(1)}, f32[32,128,128]{1,2,0:T(8,128)S(1)}) fusion(f32[32,128]{1,0:T(8,128)S(1)} %bitcast.568, f32[32,2,128,128]{2,3,1,0:T(8,128)S(1)} %bitcast.506), kind=kOutput, calls=%fused_computation.18 | convolution fusion | flops 806350848 | bytes 6324224 | tf_op jit(solution)/shard_map/dot_general | solution.py:11
  14.1 1.2 %multiply_reduce_fusion.15 = (f32[16,128]{1,0:T(8,128)S(1)}, f32[16,128,128]{1,2,0:T(8,128)S(1)}) fusion(f32[16,128]{1,0:T(8,128)S(1)} %bitcast.592, f32[16,2,128,128]{2,3,1,0:T(8,128)S(1)} %bitcast.507), kind=kOutput, calls=%fused_computation.33 | convolution fusion | flops 403175424 | bytes 3162112 | tf_op jit(solution)/shard_map/dot_general | solution.py:11
  17.8 11.4 %all-gather.2 = f32[8,129,128]{2,1,0:T(8,128)S(1)} all-gather(f32[1,129,128]{2,1,0:T(8,128)S(1)} %maximum_bitcast_fusion), channel_id=2, replica_groups=mesh['outer'=4,'inner'=8] {'inner'}, dimensions={0}, use_global_device_ids=true | all-gather | bytes 594432 | tf_op jit(solution)/shard_map/all_gather | solution.py:117
  29.4 0.9 %multiply_reduce_fusion.21 = (f32[8,128]{1,0:T(8,128)S(1)}, f32[8,128,128]{2,1,0:T(8,128)}, f32[8,128]{1,0:T(8,128)S(1)}, f32[8,128,128]{2,1,0:T(8,128)S(1)}) fusion(f32[8,128]{1,0:T(8,128)S(1)} %bitcast.607, f32[128,128]{1,0:T(8,128)S(1)} %copy-done.6, f32[8,129,128]{2,1,0:T(8,128)S(1)} %all-gather.2, pred[8]{0:T(512)(128)(4,1)S(1)} %iota_compare_fusion.2, ...), kind=kLoop, calls=%fused_computation.45 | loop fusion | flops 653312 | bytes 1654792 | tf_op jit(solution)/shard_map/reduce_sum | solution.py:19
  32.3 3.6 %collective-permute-start.2 = (f32[129,128]{1,0:T(8,128)}, f32[129,128]{1,0:T(8,128)}, u32[]{:S(2)}, u32[]{:S(2)}) collective-permute-start(f32[129,128]{1,0:T(8,128)} %pad_maximum_fusion), channel_id=1, source_target_pairs={{0,24},{8,0},{16,8},{24,16},{1,25},{9,1},{17,9},{25,17},{2,26},{10... | collective-permute-start | bytes 198152 | tf_op jit(solution)/shard_map/ppermute | solution.py:111
  35.9 1.0 %collective-permute-start = (f32[129,128]{1,0:T(8,128)}, f32[129,128]{1,0:T(8,128)}, u32[]{:S(2)}, u32[]{:S(2)}) collective-permute-start(f32[129,128]{1,0:T(8,128)} %pad_maximum_fusion), channel_id=1, source_target_pairs={{0,8},{8,16},{16,24},{24,0},{1,9},{9,17},{17,25},{25,1},{2,10},{10... | collective-permute-start | bytes 198152 | tf_op jit(solution)/shard_map/ppermute | solution.py:111
  37.5 2.3 %multiply_reduce_fusion.29 = (f32[4,128]{1,0:T(4,128)S(1)}, f32[4,128,128]{1,2,0:T(8,128)}) fusion(f32[4,128]{1,0:T(4,128)S(1)} %bitcast.637, f32[4,2,128,128]{3,2,1,0:T(8,128)} %bitcast.515), kind=kOutput, calls=%fused_computation.71 | convolution fusion | flops 100793856 | bytes 790528 | tf_op jit(solution)/shard_map/dot_general | solution.py:11
  41.0 1.9 %multiply_reduce_fusion.37 = (f32[2,128]{1,0:T(2,128)S(1)}, f32[2,128,128]{1,2,0:T(8,128)}) fusion(f32[2,128]{1,0:T(2,128)S(1)} %maximum_bitcast_fusion.4, f32[2,2,128,128]{2,3,1,0:T(8,128)} %bitcast.521), kind=kOutput, calls=%fused_computation.105 | convolution fusion | flops 50396928 | bytes 395264 | tf_op jit(solution)/shard_map/dot_general | solution.py:11
  42.9 0.8 fusion.46
  43.8 1.2 %fusion.28 = f32[128]{0:T(128)S(1)} fusion(f32[129,128]{1,0:T(8,128)} %collective-permute-done.2, f32[128]{0:T(128)S(1)} %fusion.46, f32[128]{0:T(128)} %param.11, pred[]{:T(512)S(6)} %ge.11), kind=kLoop, calls=%fused_computation.120 | loop fusion | flops 98176 | bytes 67073 | tf_op jit(solution)/shard_map/reduce_sum | solution.py:130
  45.7 1.0 %fusion.25 = f32[128]{0:T(128)S(1)} fusion(f32[129,128]{1,0:T(8,128)} %collective-permute-done.1, f32[128]{0:T(128)S(1)} %fusion.48, f32[128]{0:T(128)S(1)} %fusion.28, pred[]{:T(512)S(6)} %ge.10), kind=kLoop, calls=%fused_computation.117 | loop fusion | flops 98176 | bytes 67073 | tf_op jit(solution)/shard_map/reduce_sum | solution.py:130
  47.4 1.0 %fusion.22 = f32[128]{0:T(128)S(1)} fusion(f32[129,128]{1,0:T(8,128)} %collective-permute-done, f32[128]{0:T(128)S(1)} %fusion.50, f32[128]{0:T(128)S(1)} %fusion.25, pred[]{:T(512)S(6)} %ge.9), kind=kLoop, calls=%fused_computation.114 | loop fusion | flops 98176 | bytes 67073 | tf_op jit(solution)/shard_map/reduce_sum | solution.py:130
  48.4 1.1 %fusion.2 = f32[128]{0:T(128)S(1)} fusion(f32[1,2,128,128]{2,3,1,0:T(8,128)} %bitcast.529, f32[128]{0:T(128)S(1)} %fusion.22), kind=kOutput, calls=%fused_computation.22 | convolution fusion | flops 25198464 | bytes 132096 | tf_op jit(solution)/shard_map/dot_general | solution.py:11
  49.5 1.0 %multiply_reduce_fusion.36 = f32[2,128]{1,0:T(2,128)S(1)} fusion(f32[2,128,128]{1,2,0:T(8,128)} %copy-done.5, f32[128]{0:T(128)S(1)} %bitcast.658), kind=kLoop, calls=%fused_computation.104 | loop fusion | flops 65280 | bytes 132608 | tf_op jit(solution)/shard_map/reduce_sum | solution.py:19
  50.7 1.3 %multiply_reduce_fusion.20 = f32[8,128]{1,0:T(8,128)S(1)} fusion(f32[8,128,128]{1,2,0:T(8,128)} %copy-done.4, f32[8,128]{1,0:T(8,128)S(1)} %bitcast.610), kind=kLoop, calls=%fused_computation.44 | loop fusion | flops 261120 | bytes 532480 | tf_op jit(solution)/shard_map/reduce_sum | solution.py:19
  52.4 0.9 multiply_reduce_fusion.10
  53.4 1.5 %multiply_reduce_fusion.5 = f32[64,128]{1,0:T(8,128)S(1)} fusion(f32[64,128,128]{1,2,0:T(8,128)S(1)} %copy-done.3, f32[64,128]{1,0:T(8,128)S(1)} %bitcast.552), kind=kLoop, calls=%fused_computation.6 | loop fusion | flops 2088960 | bytes 4259840 | tf_op jit(solution)/shard_map/reduce_sum | solution.py:19
  55.0 1.5 %multiply_reduce_fusion.4 = f32[64,128]{1,0:T(8,128)S(1)} fusion(f32[64,128,128]{1,2,0:T(8,128)S(1)} %copy-done.3, f32[64,128]{1,0:T(8,128)S(1)} %bitcast.549), kind=kLoop, calls=%fused_computation.5 | loop fusion | flops 2088960 | bytes 4259840 | tf_op jit(solution)/shard_map/reduce_sum | solution.py:19
  56.7 1.2 %multiply_reduce_fusion.3 = f32[64,128]{1,0:T(8,128)S(1)} fusion(f32[64,128,128]{2,1,0:T(8,128)S(1)} %copy-done.1, f32[64,128]{1,0:T(8,128)S(1)} %fusion.85), kind=kLoop, calls=%fused_computation.4 | loop fusion | flops 2088960 | bytes 4259840 | tf_op jit(solution)/shard_map/reduce_sum | solution.py:19
  58.0 1.2 %multiply_reduce_fusion.2 = f32[64,128]{1,0:T(8,128)S(1)} fusion(f32[64,128,128]{2,1,0:T(8,128)S(1)} %copy-done.1, f32[64,128]{1,0:T(8,128)S(1)} %bitcast.550), kind=kLoop, calls=%fused_computation.3 | loop fusion | flops 2088960 | bytes 4259840 | tf_op jit(solution)/shard_map/reduce_sum | solution.py:19
  59.2 3.9 %multiply_reduce_fusion.9 = (f32[32,128]{1,0:T(8,128)S(1)}, f32[32,128,128]{1,2,0:T(8,128)S(1)}) fusion(f32[32,128]{1,0:T(8,128)S(1)} %bitcast.569, f32[32,2,128,128]{3,2,1,0:T(8,128)S(1)} %bitcast.505), kind=kOutput, calls=%fused_computation.16 | convolution fusion | flops 806350848 | bytes 6324224 | tf_op jit(solution)/shard_map/dot_general | solution.py:11
  63.2 1.2 %multiply_reduce_fusion.13 = (f32[16,128]{1,0:T(8,128)S(1)}, f32[16,128,128]{1,2,0:T(8,128)S(1)}) fusion(f32[16,128]{1,0:T(8,128)S(1)} %bitcast.593, f32[16,2,128,128]{2,3,1,0:T(8,128)S(1)} %bitcast.508), kind=kOutput, calls=%fused_computation.31 | convolution fusion | flops 403175424 | bytes 3162112 | tf_op jit(solution)/shard_map/dot_general | solution.py:11
  66.3 10.2 %all-gather.3 = f32[8,129,128]{2,1,0:T(8,128)S(1)} all-gather(f32[1,129,128]{2,1,0:T(8,128)S(1)} %maximum_bitcast_fusion.1), channel_id=3, replica_groups=mesh['outer'=4,'inner'=8] {'inner'}, dimensions={0}, use_global_device_ids=true | all-gather | bytes 594432 | tf_op jit(solution)/shard_map/all_gather | solution.py:117
  78.4 2.5 %collective-permute-start.5 = (f32[129,128]{1,0:T(8,128)S(1)}, f32[129,128]{1,0:T(8,128)S(1)}, u32[]{:S(2)}, u32[]{:S(2)}) collective-permute-start(f32[129,128]{1,0:T(8,128)S(1)} %pad_maximum_fusion.1), channel_id=1, source_target_pairs={{0,8},{8,16},{16,24},{24,0},{1,9},{9,17},{17,25},{25,1},{2,10},{10... | collective-permute-start | bytes 198152 | tf_op jit(solution)/shard_map/ppermute | solution.py:111
  80.9 0.9 collective-permute-start.4
  81.8 1.5 %collective-permute-start.3 = (f32[129,128]{1,0:T(8,128)S(1)}, f32[129,128]{1,0:T(8,128)S(1)}, u32[]{:S(2)}, u32[]{:S(2)}) collective-permute-start(f32[129,128]{1,0:T(8,128)S(1)} %pad_maximum_fusion.1), channel_id=1, source_target_pairs={{0,24},{8,0},{16,8},{24,16},{1,25},{9,1},{17,9},{25,17},{2,26},{10... | collective-permute-start | bytes 198152 | tf_op jit(solution)/shard_map/ppermute | solution.py:111
  84.4 0.9 collective-permute-done.5
  85.4 2.3 %collective-permute-done.4 = f32[129,128]{1,0:T(8,128)S(1)} collective-permute-done((f32[129,128]{1,0:T(8,128)S(1)}, f32[129,128]{1,0:T(8,128)S(1)}, u32[]{:S(2)}, u32[]{:S(2)}) %collective-permute-start.4) | collective-permute-done | bytes 66080 | tf_op jit(solution)/shard_map/ppermute | solution.py:111
  90.2 1.2 %multiply_reduce_fusion.1 = f32[64,128]{1,0:T(8,128)S(1)} fusion(f32[64,128,128]{2,1,0:T(8,128)S(1)} %copy-done.1, f32[64,128]{1,0:T(8,128)S(1)} %bitcast.553), kind=kLoop, calls=%fused_computation.2 | loop fusion | flops 2088960 | bytes 4259840 | tf_op jit(solution)/shard_map/reduce_sum | solution.py:19
  91.4 1.2 %multiply_reduce_fusion = f32[64,128]{1,0:T(8,128)S(1)} fusion(f32[64,128,128]{2,1,0:T(8,128)S(1)} %copy-done.1, f32[64,128]{1,0:T(8,128)S(1)} %bitcast.551), kind=kLoop, calls=%fused_computation.1 | loop fusion | flops 2088960 | bytes 4259840 | tf_op jit(solution)/shard_map/reduce_sum | solution.py:19
  (199 shorter events, 18.0 us)
Async XLA Ops:
  0.6 4.7 %copy-start = (f32[128,128]{1,0:T(8,128)S(1)}, f32[128,128]{1,0:T(8,128)}, u32[]{:S(2)}) copy-start(f32[128,128]{1,0:T(8,128)} %param.10) | copy-start | bytes 196612
  0.6 4.6 %copy-start.8 = (f32[128,128]{1,0:T(8,128)S(1)}, f32[128,128]{1,0:T(8,128)}, u32[]{:S(2)}) copy-start(f32[128,128]{1,0:T(8,128)} %param.9) | copy-start | bytes 196612
  11.6 3.7 %copy-start.2 = (f32[64,128,128]{1,2,0:T(8,128)}, f32[64,128,128]{1,2,0:T(8,128)S(1)}, u32[]{:S(2)}) copy-start(f32[64,128,128]{1,2,0:T(8,128)S(1)} %get-tuple-element.63) | copy-start | bytes 12582916
  14.0 15.3 %copy-start.12 = (pred[4,2]{1,0:T(4,128)(4,1)S(1)}, pred[4,2]{1,0:T(4,128)(4,1)}, u32[]{:S(2)}) copy-start(pred[4,2]{1,0:T(4,128)(4,1)} %fusion.44) | copy-start | bytes 28
  14.0 15.4 %copy-start.6 = (f32[128,128]{1,0:T(8,128)S(1)}, f32[128,128]{1,0:T(8,128)}, u32[]{:S(2)}) copy-start(f32[128,128]{1,0:T(8,128)} %fusion.42) | copy-start | bytes 196612
  16.0 0.8 copy-start.4
  17.5 11.9 %copy-start.5 = (f32[2,128,128]{1,2,0:T(8,128)}, f32[2,128,128]{1,2,0:T(8,128)S(1)}, u32[]{:S(2)}) copy-start(f32[2,128,128]{1,2,0:T(8,128)S(1)} %get-tuple-element.73) | copy-start | bytes 393220
  32.3 10.6 %collective-permute-start.2 = (f32[129,128]{1,0:T(8,128)}, f32[129,128]{1,0:T(8,128)}, u32[]{:S(2)}, u32[]{:S(2)}) collective-permute-start(f32[129,128]{1,0:T(8,128)} %pad_maximum_fusion), channel_id=1, source_target_pairs={{0,24},{8,0},{16,8},{24,16},{1,25},{9,1},{17,9},{25,17},{2,26},{10... | collective-permute-start | bytes 198152 | tf_op jit(solution)/shard_map/ppermute | solution.py:111
  35.9 9.1 %collective-permute-start.1 = (f32[129,128]{1,0:T(8,128)}, f32[129,128]{1,0:T(8,128)}, u32[]{:S(2)}, u32[]{:S(2)}) collective-permute-start(f32[129,128]{1,0:T(8,128)} %pad_maximum_fusion), channel_id=1, source_target_pairs={{0,16},{8,24},{16,0},{24,8},{1,17},{9,25},{17,1},{25,9},{2,18},{10... | collective-permute-start | bytes 198152 | tf_op jit(solution)/shard_map/ppermute | solution.py:111
  35.9 10.8 %collective-permute-start = (f32[129,128]{1,0:T(8,128)}, f32[129,128]{1,0:T(8,128)}, u32[]{:S(2)}, u32[]{:S(2)}) collective-permute-start(f32[129,128]{1,0:T(8,128)} %pad_maximum_fusion), channel_id=1, source_target_pairs={{0,8},{8,16},{16,24},{24,0},{1,9},{9,17},{17,25},{25,1},{2,10},{10... | collective-permute-start | bytes 198152 | tf_op jit(solution)/shard_map/ppermute | solution.py:111
  42.9 10.5 %copy-start.3 = (f32[64,128,128]{1,2,0:T(8,128)S(1)}, f32[64,128,128]{1,2,0:T(8,128)}, u32[]{:S(2)}) copy-start(f32[64,128,128]{1,2,0:T(8,128)} %copy-done.2) | copy-start | bytes 12582916
  53.4 3.1 %copy-start.9 = (f32[128,128]{1,0:T(8,128)S(1)}, f32[128,128]{1,0:T(8,128)}, u32[]{:S(2)}) copy-start(f32[128,128]{1,0:T(8,128)} %param.9) | copy-start | bytes 196612
  53.4 3.3 %copy-start.1 = (f32[64,128,128]{2,1,0:T(8,128)S(1)}, f32[64,128,128]{2,1,0:T(8,128)}, u32[]{:S(2)}) copy-start(f32[64,128,128]{2,1,0:T(8,128)} %param.8) | copy-start | bytes 12582916
  56.5 36.1 %copy-start.10 = (f32[64,128]{1,0:T(8,128)}, f32[64,128]{1,0:T(8,128)S(1)}, u32[]{:S(2)}) copy-start(f32[64,128]{1,0:T(8,128)S(1)} %add.418) | copy-start | bytes 98308
  63.2 13.4 %copy-start.11 = (pred[4,2]{1,0:T(4,128)(4,1)S(1)}, pred[4,2]{1,0:T(4,128)(4,1)}, u32[]{:S(2)}) copy-start(pred[4,2]{1,0:T(4,128)(4,1)} %fusion.43) | copy-start | bytes 28
  63.2 13.5 %copy-start.7 = (f32[128,128]{1,0:T(8,128)S(1)}, f32[128,128]{1,0:T(8,128)}, u32[]{:S(2)}) copy-start(f32[128,128]{1,0:T(8,128)} %fusion.42) | copy-start | bytes 196612
  78.4 6.8 %collective-permute-start.5 = (f32[129,128]{1,0:T(8,128)S(1)}, f32[129,128]{1,0:T(8,128)S(1)}, u32[]{:S(2)}, u32[]{:S(2)}) collective-permute-start(f32[129,128]{1,0:T(8,128)S(1)} %pad_maximum_fusion.1), channel_id=1, source_target_pairs={{0,8},{8,16},{16,24},{24,0},{1,9},{9,17},{17,25},{25,1},{2,10},{10... | collective-permute-start | bytes 198152 | tf_op jit(solution)/shard_map/ppermute | solution.py:111
  80.9 6.8 %collective-permute-start.4 = (f32[129,128]{1,0:T(8,128)S(1)}, f32[129,128]{1,0:T(8,128)S(1)}, u32[]{:S(2)}, u32[]{:S(2)}) collective-permute-start(f32[129,128]{1,0:T(8,128)S(1)} %pad_maximum_fusion.1), channel_id=1, source_target_pairs={{0,16},{8,24},{16,0},{24,8},{1,17},{9,25},{17,1},{25,9},{2,18},{10... | collective-permute-start | bytes 198152 | tf_op jit(solution)/shard_map/ppermute | solution.py:111
  81.8 6.1 %collective-permute-start.3 = (f32[129,128]{1,0:T(8,128)S(1)}, f32[129,128]{1,0:T(8,128)S(1)}, u32[]{:S(2)}, u32[]{:S(2)}) collective-permute-start(f32[129,128]{1,0:T(8,128)S(1)} %pad_maximum_fusion.1), channel_id=1, source_target_pairs={{0,24},{8,0},{16,8},{24,16},{1,25},{9,1},{17,9},{25,17},{2,26},{10... | collective-permute-start | bytes 198152 | tf_op jit(solution)/shard_map/ppermute | solution.py:111

commit v8 on v6

--- a/solution.py
+++ b/solution.py
@@ -40,8 +40,15 @@
     return mm(m2, m1), mv(m2, v1) + v2
 
 
-def local_tiers(mats, vecs, backward):
+def local_tiers(mats, vecs, backward, joined=None):
     tiers = [(mats, vecs)]
+    if joined is not None:
+        count, width = mats.shape[0], mats.shape[-1]
+        pv = vecs.reshape(count // 2, 2, width)
+        partner = jnp.stack((pv[:, 1], pv[:, 0]), axis=1).reshape(count, width)
+        crossed = mv_whole(mats, partner).reshape(count // 2, 2, width)
+        second = 0 if backward else 1
+        tiers.append((joined, crossed[:, second] + pv[:, second]))
     while tiers[-1][0].shape[0] > 1:
         tiers.append(local_pair(tiers[-1][0], tiers[-1][1], backward))
     return tiers
@@ -132,6 +139,9 @@
 def on_device(observations, gains, smoother_gains, transition, observation_map, initial_mean):
     me = lax.axis_index(AXES)
     devices = lax.axis_size(AXES)
+    width = smoother_gains.shape[-1]
+    paired = smoother_gains.reshape(smoother_gains.shape[0] // 2, 2, width, width)
+    back_joined = lax.optimization_barrier(mm(paired[:, 0], paired[:, 1]))
     mapped = mm(observation_map, transition)
     forward_maps = transition[None] - jnp.einsum(
         "tij,jk->tik", gains, mapped, precision=exact, preferred_element_type=jnp.float32
@@ -146,7 +156,7 @@
         filtered, transition.T, precision=exact, preferred_element_type=jnp.float32
     )
     offsets = filtered - mv_whole(smoother_gains, predicted_all)
-    backward = local_tiers(smoother_gains, offsets, True)
+    backward = local_tiers(smoother_gains, offsets, True, back_joined)
     bm, bv = backward[-1][0][0], backward[-1][1][0]
     last = me == devices - 1
     extra = jnp.where(last, predicted_all[-1], 0.0)

time: 91 us -> 92.2 us (1.013)
  waiting for transfers between devices: 4.93 us -> 3.31 us
  other arithmetic: 26 us -> 27.5 us
  matrix products: 26.1 us -> 27.4 us
    ppermute x6, waiting for transfers between devices: 4.93 us -> 3.31 us  [from_other_groups(): received.append(lax.ppermute(packed, 'outer', pairs))]
    reduce_sum x25 -> x26, other arithmetic: 20.2 us -> 21.8 us  [mv_whole(): return jnp.sum(a * v[..., None, :], axis=-1)]
    dot_general x25, matrix products: 20 us -> 21.2 us  [mm(): return jnp.matmul(a, b, precision=exact, preferred_element_type=jnp.float32)]
  transfers between devices with their start and end apart: 6 -> 6, of which waited for: 3 -> 2; matrix products, arithmetic and copies ran while one was open for 9% -> 14% of each run, Pallas kernels for 0% -> 0%
where the time goes in v8:
time: 92.2 us; the launch traced here: 91.6 us
  other arithmetic  27.5 us (30%)
  matrix products  27.4 us (30%)
  blocking collectives  21.4 us (23%)
  starting transfers between devices  9.58 us (10%)
  waiting for transfers between devices  3.31 us (4%)
  between operations  1.97 us (2%)
    reduce_sum x26, other arithmetic, mv_whole(): return jnp.sum(a * v[..., None, :], axis=-1)  21.8 us
    all_gather x2, blocking collectives, across(): gathered = lax.all_gather(pack(mat, vec), 'inner')  21.4 us
    dot_general x25, matrix products, mm(): return jnp.matmul(a, b, precision=exact, preferred_element_type=jnp.float32)  21.2 us
    ppermute x6, starting transfers between devices, from_other_groups(): received.append(lax.ppermute(packed, 'outer', pairs))  9.58 us
    dot_general x1, matrix products, on_device(): jnp.einsum('tij,jk->tik', gains, mapped, precision=exact, preferred_eleme...  5.93 us
    ppermute x6, waiting for transfers between devices, from_other_groups(): received.append(lax.ppermute(packed, 'outer', pairs))  3.31 us
    mul x13, other arithmetic, mv_whole(): return jnp.sum(a * v[..., None, :], axis=-1)  2.3 us
  transfers between devices with their start and end apart: 6, of which 2 were waited for; matrix products, arithmetic and copies ran while one was open for 14% of the time, Pallas kernels for 0%

profile of v8, /device:TPU:0, one launch (start us, length us, event | category | flops | bytes accessed | tf_op | source)
XLA Modules:
  0.0 91.6 jit_solution(6171737737926912397)
XLA Ops:
  1.3 3.3 %multiply_reduce_fusion.7 = f32[64,128]{1,0:T(8,128)S(1)} fusion(f32[64,128,128]{2,1,0:T(8,128)} %param.7, f32[64,128]{1,0:T(8,128)} %param.6), kind=kLoop, calls=%fused_computation.8 | loop fusion | flops 2088960 | bytes 4259840 | tf_op jit(solution)/shard_map/reduce_sum | solution.py:19
  5.2 5.9 %multiply_reduce_fusion.6 = (f32[64,128]{1,0:T(8,128)S(1)}, f32[64,128,128]{1,2,0:T(8,128)S(1)}) fusion(f32[64,128]{1,0:T(8,128)S(1)} %bitcast.565, f32[128,128,1]{0,1,2:T(8,128)S(1)} %convolution_bitcast_fusion, f32[64,128,128]{2,1,0:T(8,128)} %param.7, f32[128,128]{0,1:T(8,128)S(1)} %copy.408), kind=kOutput, calls=%fused_computation.7 | convolution fusion | flops 1613750272 | bytes 8585216 | tf_op jit(solution)/shard_map/tij,jk->tik/dot_general | solution.py:146
  11.2 2.3 %multiply_reduce_fusion.11 = (f32[32,128]{1,0:T(8,128)S(1)}, f32[32,128,128]{1,2,0:T(8,128)S(1)}) fusion(f32[32,128]{1,0:T(8,128)S(1)} %bitcast.585, f32[32,2,128,128]{2,3,1,0:T(8,128)S(1)} %bitcast.523), kind=kOutput, calls=%fused_computation.18 | convolution fusion | flops 806350848 | bytes 6324224 | tf_op jit(solution)/shard_map/dot_general | solution.py:11
  13.6 1.2 %multiply_reduce_fusion.15 = (f32[16,128]{1,0:T(8,128)S(1)}, f32[16,128,128]{1,2,0:T(8,128)S(1)}) fusion(f32[16,128]{1,0:T(8,128)S(1)} %bitcast.609, f32[16,2,128,128]{2,3,1,0:T(8,128)S(1)} %bitcast.525), kind=kOutput, calls=%fused_computation.29 | convolution fusion | flops 403175424 | bytes 3162112 | tf_op jit(solution)/shard_map/dot_general | solution.py:11
  16.6 11.4 %all-gather.2 = f32[8,129,128]{2,1,0:T(8,128)S(1)} all-gather(f32[1,129,128]{2,1,0:T(8,128)S(1)} %maximum_bitcast_fusion), channel_id=2, replica_groups=mesh['outer'=4,'inner'=8] {'inner'}, dimensions={0}, use_global_device_ids=true | all-gather | bytes 594432 | tf_op jit(solution)/shard_map/all_gather | solution.py:124
  30.6 3.6 %collective-permute-start.2 = (f32[129,128]{1,0:T(8,128)}, f32[129,128]{1,0:T(8,128)}, u32[]{:S(2)}, u32[]{:S(2)}) collective-permute-start(f32[129,128]{1,0:T(8,128)} %pad_maximum_fusion), channel_id=1, source_target_pairs={{0,24},{8,0},{16,8},{24,16},{1,25},{9,1},{17,9},{25,17},{2,26},{10... | collective-permute-start | bytes 198152 | tf_op jit(solution)/shard_map/ppermute | solution.py:118
  34.2 1.0 %collective-permute-start = (f32[129,128]{1,0:T(8,128)}, f32[129,128]{1,0:T(8,128)}, u32[]{:S(2)}, u32[]{:S(2)}) collective-permute-start(f32[129,128]{1,0:T(8,128)} %pad_maximum_fusion), channel_id=1, source_target_pairs={{0,8},{8,16},{16,24},{24,0},{1,9},{9,17},{17,25},{25,1},{2,10},{10... | collective-permute-start | bytes 198152 | tf_op jit(solution)/shard_map/ppermute | solution.py:118
  35.8 1.3 %multiply_reduce_fusion.29 = (f32[4,128]{1,0:T(4,128)S(1)}, f32[4,128,128]{1,2,0:T(8,128)}) fusion(f32[4,128]{1,0:T(4,128)S(1)} %bitcast.654, f32[4,2,128,128]{3,2,1,0:T(8,128)S(1)} %bitcast.532), kind=kOutput, calls=%fused_computation.67 | convolution fusion | flops 100793856 | bytes 790528 | tf_op jit(solution)/shard_map/dot_general | solution.py:11
  37.1 4.4 %fusion = f32[32,128,128]{2,1,0:T(8,128)S(1)} fusion(f32[32,2,128,128]{3,2,1,0:T(8,128)} %bitcast.522), kind=kOutput, calls=%fused_computation.10 | convolution fusion | flops 805306368 | bytes 6291456 | tf_op jit(solution)/shard_map/dot_general | solution.py:11
  41.5 1.9 %multiply_reduce_fusion.37 = (f32[2,128]{1,0:T(2,128)S(1)}, f32[2,128,128]{1,2,0:T(8,128)}) fusion(f32[2,128]{1,0:T(2,128)S(1)} %maximum_bitcast_fusion.4, f32[2,2,128,128]{2,3,1,0:T(8,128)} %bitcast.538), kind=kOutput, calls=%fused_computation.101 | convolution fusion | flops 50396928 | bytes 395264 | tf_op jit(solution)/shard_map/dot_general | solution.py:11
  43.4 1.1 %fusion.23 = f32[128]{0:T(128)S(1)} fusion(f32[129,128]{1,0:T(8,128)} %collective-permute-done.2, f32[128]{0:T(128)} %param.11, pred[]{:T(512)S(6)} %ge.11), kind=kLoop, calls=%fused_computation.113 | loop fusion | flops 81792 | bytes 66561 | tf_op jit(solution)/shard_map/reduce_sum | solution.py:19
  44.6 0.9 fusion.40
  45.4 0.9 %fusion.21 = f32[128]{0:T(128)S(1)} fusion(f32[129,128]{1,0:T(8,128)} %collective-permute-done.1, f32[128]{0:T(128)S(1)} %fusion.40, pred[]{:T(512)S(6)} %ge.10), kind=kLoop, calls=%fused_computation.111 | loop fusion | flops 81792 | bytes 66561 | tf_op jit(solution)/shard_map/reduce_sum | solution.py:19
  46.4 0.7 fusion.42
  47.1 0.9 %fusion.19 = f32[128]{0:T(128)S(1)} fusion(f32[129,128]{1,0:T(8,128)} %collective-permute-done, f32[128]{0:T(128)S(1)} %fusion.42, pred[]{:T(512)S(6)} %ge.9), kind=kLoop, calls=%fused_computation.109 | loop fusion | flops 81792 | bytes 66561 | tf_op jit(solution)/shard_map/reduce_sum | solution.py:19
  48.7 1.1 %multiply_reduce_fusion.42 = f32[128]{0:T(128)S(1)} fusion(f32[128]{0:T(128)S(1)} %fusion.44, f32[1,2,128,128]{2,3,1,0:T(8,128)} %bitcast.546), kind=kOutput, calls=%fused_computation.140 | convolution fusion | flops 25198464 | bytes 132096 | tf_op jit(solution)/shard_map/dot_general | solution.py:11
  49.8 1.0 %multiply_reduce_fusion.36 = f32[2,128]{1,0:T(2,128)S(1)} fusion(f32[2,128,128]{1,2,0:T(8,128)} %copy-done.6, f32[128]{0:T(128)S(1)} %bitcast.675), kind=kLoop, calls=%fused_computation.100 | loop fusion | flops 65280 | bytes 132608 | tf_op jit(solution)/shard_map/reduce_sum | solution.py:19
  51.0 1.3 %multiply_reduce_fusion.20 = f32[8,128]{1,0:T(8,128)S(1)} fusion(f32[8,128,128]{1,2,0:T(8,128)} %copy-done.5, f32[8,128]{1,0:T(8,128)S(1)} %bitcast.627), kind=kLoop, calls=%fused_computation.40 | loop fusion | flops 261120 | bytes 532480 | tf_op jit(solution)/shard_map/reduce_sum | solution.py:19
  52.7 1.9 %multiply_reduce_fusion.10 = f32[32,128]{1,0:T(8,128)S(1)} fusion(f32[32,128,128]{1,2,0:T(8,128)} %copy-done.4, f32[32,128]{1,0:T(8,128)S(1)} %bitcast.587), kind=kLoop, calls=%fused_computation.17 | loop fusion | flops 1044480 | bytes 2129920 | tf_op jit(solution)/shard_map/reduce_sum | solution.py:19
  54.7 1.5 %multiply_reduce_fusion.5 = f32[64,128]{1,0:T(8,128)S(1)} fusion(f32[64,128,128]{1,2,0:T(8,128)S(1)} %copy-done.3, f32[64,128]{1,0:T(8,128)S(1)} %bitcast.569), kind=kLoop, calls=%fused_computation.6 | loop fusion | flops 2088960 | bytes 4259840 | tf_op jit(solution)/shard_map/reduce_sum | solution.py:19
  56.3 1.5 %multiply_reduce_fusion.4 = f32[64,128]{1,0:T(8,128)S(1)} fusion(f32[64,128,128]{1,2,0:T(8,128)S(1)} %copy-done.3, f32[64,128]{1,0:T(8,128)S(1)} %bitcast.566), kind=kLoop, calls=%fused_computation.5 | loop fusion | flops 2088960 | bytes 4259840 | tf_op jit(solution)/shard_map/reduce_sum | solution.py:19
  58.1 1.2 %multiply_reduce_fusion.3 = f32[64,128]{1,0:T(8,128)S(1)} fusion(f32[64,128,128]{2,1,0:T(8,128)S(1)} %copy-done.1, f32[64,128]{1,0:T(8,128)S(1)} %fusion.79), kind=kLoop, calls=%fused_computation.4 | loop fusion | flops 2088960 | bytes 4259840 | tf_op jit(solution)/shard_map/reduce_sum | solution.py:19
  59.3 1.2 %multiply_reduce_fusion.2 = f32[64,128]{1,0:T(8,128)S(1)} fusion(f32[64,128,128]{2,1,0:T(8,128)S(1)} %copy-done.1, f32[64,128]{1,0:T(8,128)S(1)} %bitcast.567), kind=kLoop, calls=%fused_computation.3 | loop fusion | flops 2088960 | bytes 4259840 | tf_op jit(solution)/shard_map/reduce_sum | solution.py:19
  61.3 2.0 %multiply_reduce_fusion.13 = (f32[16,128]{1,0:T(8,128)S(1)}, f32[16,128,128]{1,2,0:T(8,128)S(1)}) fusion(f32[16,128]{1,0:T(8,128)S(1)} %bitcast.610, f32[16,2,128,128]{3,2,1,0:T(8,128)S(1)} %bitcast.524), kind=kOutput, calls=%fused_computation.27 | convolution fusion | flops 403175424 | bytes 3162112 | tf_op jit(solution)/shard_map/dot_general | solution.py:11
  65.2 10.0 %all-gather.3 = f32[8,129,128]{2,1,0:T(8,128)S(1)} all-gather(f32[1,129,128]{2,1,0:T(8,128)S(1)} %maximum_bitcast_fusion.1), channel_id=3, replica_groups=mesh['outer'=4,'inner'=8] {'inner'}, dimensions={0}, use_global_device_ids=true | all-gather | bytes 594432 | tf_op jit(solution)/shard_map/all_gather | solution.py:124
  77.0 2.5 %collective-permute-start.5 = (f32[129,128]{1,0:T(8,128)S(1)}, f32[129,128]{1,0:T(8,128)S(1)}, u32[]{:S(2)}, u32[]{:S(2)}) collective-permute-start(f32[129,128]{1,0:T(8,128)S(1)} %pad_maximum_fusion.1), channel_id=1, source_target_pairs={{0,8},{8,16},{16,24},{24,0},{1,9},{9,17},{17,25},{25,1},{2,10},{10... | collective-permute-start | bytes 198152 | tf_op jit(solution)/shard_map/ppermute | solution.py:118
  79.6 0.9 collective-permute-start.4
  80.5 1.5 %collective-permute-start.3 = (f32[129,128]{1,0:T(8,128)S(1)}, f32[129,128]{1,0:T(8,128)S(1)}, u32[]{:S(2)}, u32[]{:S(2)}) collective-permute-start(f32[129,128]{1,0:T(8,128)S(1)} %pad_maximum_fusion.1), channel_id=1, source_target_pairs={{0,24},{8,0},{16,8},{24,16},{1,25},{9,1},{17,9},{25,17},{2,26},{10... | collective-permute-start | bytes 198152 | tf_op jit(solution)/shard_map/ppermute | solution.py:118
  83.0 0.8 collective-permute-done.5
  83.9 2.5 %collective-permute-done.4 = f32[129,128]{1,0:T(8,128)S(1)} collective-permute-done((f32[129,128]{1,0:T(8,128)S(1)}, f32[129,128]{1,0:T(8,128)S(1)}, u32[]{:S(2)}, u32[]{:S(2)}) %collective-permute-start.4) | collective-permute-done | bytes 66080 | tf_op jit(solution)/shard_map/ppermute | solution.py:118
  88.6 1.2 %multiply_reduce_fusion.1 = f32[64,128]{1,0:T(8,128)S(1)} fusion(f32[64,128,128]{2,1,0:T(8,128)S(1)} %copy-done.1, f32[64,128]{1,0:T(8,128)S(1)} %bitcast.570), kind=kLoop, calls=%fused_computation.2 | loop fusion | flops 2088960 | bytes 4259840 | tf_op jit(solution)/shard_map/reduce_sum | solution.py:19
  89.9 1.2 %multiply_reduce_fusion = f32[64,128]{1,0:T(8,128)S(1)} fusion(f32[64,128,128]{2,1,0:T(8,128)S(1)} %copy-done.1, f32[64,128]{1,0:T(8,128)S(1)} %bitcast.568), kind=kLoop, calls=%fused_computation.1 | loop fusion | flops 2088960 | bytes 4259840 | tf_op jit(solution)/shard_map/reduce_sum | solution.py:19
  (200 shorter events, 15.6 us)
Async XLA Ops:
  0.6 4.2 %copy-start = (f32[128,128]{1,0:T(8,128)S(1)}, f32[128,128]{1,0:T(8,128)}, u32[]{:S(2)}) copy-start(f32[128,128]{1,0:T(8,128)} %param.10) | copy-start | bytes 196612
  0.6 4.1 %copy-start.9 = (f32[128,128]{1,0:T(8,128)S(1)}, f32[128,128]{1,0:T(8,128)}, u32[]{:S(2)}) copy-start(f32[128,128]{1,0:T(8,128)} %param.9) | copy-start | bytes 196612
  11.1 3.7 %copy-start.2 = (f32[64,128,128]{1,2,0:T(8,128)}, f32[64,128,128]{1,2,0:T(8,128)S(1)}, u32[]{:S(2)}) copy-start(f32[64,128,128]{1,2,0:T(8,128)S(1)} %get-tuple-element.63) | copy-start | bytes 12582916
  13.5 15.1 %copy-start.4 = (f32[32,128,128]{1,2,0:T(8,128)}, f32[32,128,128]{1,2,0:T(8,128)S(1)}, u32[]{:S(2)}) copy-start(f32[32,128,128]{1,2,0:T(8,128)S(1)} %get-tuple-element.65) | copy-start | bytes 6291460
  13.5 14.7 %copy-start.7 = (f32[128,128]{1,0:T(8,128)S(1)}, f32[128,128]{1,0:T(8,128)}, u32[]{:S(2)}) copy-start(f32[128,128]{1,0:T(8,128)} %fusion.36) | copy-start | bytes 196612
  15.5 13.2 %copy-start.5 = (f32[8,128,128]{1,2,0:T(8,128)}, f32[8,128,128]{1,2,0:T(8,128)S(1)}, u32[]{:S(2)}) copy-start(f32[8,128,128]{1,2,0:T(8,128)S(1)} %get-tuple-element.69) | copy-start | bytes 1572868
  16.3 11.9 %copy-start.6 = (f32[2,128,128]{1,2,0:T(8,128)}, f32[2,128,128]{1,2,0:T(8,128)S(1)}, u32[]{:S(2)}) copy-start(f32[2,128,128]{1,2,0:T(8,128)S(1)} %get-tuple-element.73) | copy-start | bytes 393220
  30.6 12.8 %collective-permute-start.2 = (f32[129,128]{1,0:T(8,128)}, f32[129,128]{1,0:T(8,128)}, u32[]{:S(2)}, u32[]{:S(2)}) collective-permute-start(f32[129,128]{1,0:T(8,128)} %pad_maximum_fusion), channel_id=1, source_target_pairs={{0,24},{8,0},{16,8},{24,16},{1,25},{9,1},{17,9},{25,17},{2,26},{10... | collective-permute-start | bytes 198152 | tf_op jit(solution)/shard_map/ppermute | solution.py:118
  34.2 11.2 %collective-permute-start.1 = (f32[129,128]{1,0:T(8,128)}, f32[129,128]{1,0:T(8,128)}, u32[]{:S(2)}, u32[]{:S(2)}) collective-permute-start(f32[129,128]{1,0:T(8,128)} %pad_maximum_fusion), channel_id=1, source_target_pairs={{0,16},{8,24},{16,0},{24,8},{1,17},{9,25},{17,1},{25,9},{2,18},{10... | collective-permute-start | bytes 198152 | tf_op jit(solution)/shard_map/ppermute | solution.py:118
  34.2 12.8 %collective-permute-start = (f32[129,128]{1,0:T(8,128)}, f32[129,128]{1,0:T(8,128)}, u32[]{:S(2)}, u32[]{:S(2)}) collective-permute-start(f32[129,128]{1,0:T(8,128)} %pad_maximum_fusion), channel_id=1, source_target_pairs={{0,8},{8,16},{16,24},{24,0},{1,9},{9,17},{17,25},{25,1},{2,10},{10... | collective-permute-start | bytes 198152 | tf_op jit(solution)/shard_map/ppermute | solution.py:118
  43.4 11.3 %copy-start.3 = (f32[64,128,128]{1,2,0:T(8,128)S(1)}, f32[64,128,128]{1,2,0:T(8,128)}, u32[]{:S(2)}) copy-start(f32[64,128,128]{1,2,0:T(8,128)} %copy-done.2) | copy-start | bytes 12582916
  54.7 3.1 %copy-start.10 = (f32[128,128]{1,0:T(8,128)S(1)}, f32[128,128]{1,0:T(8,128)}, u32[]{:S(2)}) copy-start(f32[128,128]{1,0:T(8,128)} %param.9) | copy-start | bytes 196612
  54.7 3.3 %copy-start.1 = (f32[64,128,128]{2,1,0:T(8,128)S(1)}, f32[64,128,128]{2,1,0:T(8,128)}, u32[]{:S(2)}) copy-start(f32[64,128,128]{2,1,0:T(8,128)} %param.8) | copy-start | bytes 12582916
  57.8 33.2 %copy-start.11 = (f32[64,128]{1,0:T(8,128)}, f32[64,128]{1,0:T(8,128)S(1)}, u32[]{:S(2)}) copy-start(f32[64,128]{1,0:T(8,128)S(1)} %add.391) | copy-start | bytes 98308
  60.6 14.6 %copy-start.12 = (pred[4,2]{1,0:T(4,128)(4,1)S(1)}, pred[4,2]{1,0:T(4,128)(4,1)}, u32[]{:S(2)}) copy-start(pred[4,2]{1,0:T(4,128)(4,1)} %fusion.37) | copy-start | bytes 28
  60.6 14.7 %copy-start.8 = (f32[128,128]{1,0:T(8,128)S(1)}, f32[128,128]{1,0:T(8,128)}, u32[]{:S(2)}) copy-start(f32[128,128]{1,0:T(8,128)} %fusion.36) | copy-start | bytes 196612
  77.0 6.8 %collective-permute-start.5 = (f32[129,128]{1,0:T(8,128)S(1)}, f32[129,128]{1,0:T(8,128)S(1)}, u32[]{:S(2)}, u32[]{:S(2)}) collective-permute-start(f32[129,128]{1,0:T(8,128)S(1)} %pad_maximum_fusion.1), channel_id=1, source_target_pairs={{0,8},{8,16},{16,24},{24,0},{1,9},{9,17},{17,25},{25,1},{2,10},{10... | collective-permute-start | bytes 198152 | tf_op jit(solution)/shard_map/ppermute | solution.py:118
  79.6 6.8 %collective-permute-start.4 = (f32[129,128]{1,0:T(8,128)S(1)}, f32[129,128]{1,0:T(8,128)S(1)}, u32[]{:S(2)}, u32[]{:S(2)}) collective-permute-start(f32[129,128]{1,0:T(8,128)S(1)} %pad_maximum_fusion.1), channel_id=1, source_target_pairs={{0,16},{8,24},{16,0},{24,8},{1,17},{9,25},{17,1},{25,9},{2,18},{10... | collective-permute-start | bytes 198152 | tf_op jit(solution)/shard_map/ppermute | solution.py:118
  80.5 6.1 %collective-permute-start.3 = (f32[129,128]{1,0:T(8,128)S(1)}, f32[129,128]{1,0:T(8,128)S(1)}, u32[]{:S(2)}, u32[]{:S(2)}) collective-permute-start(f32[129,128]{1,0:T(8,128)S(1)} %pad_maximum_fusion.1), channel_id=1, source_target_pairs={{0,24},{8,0},{16,8},{24,16},{1,25},{9,1},{17,9},{25,17},{2,26},{10... | collective-permute-start | bytes 198152 | tf_op jit(solution)/shard_map/ppermute | solution.py:118

commit v9 on v6

--- a/solution.py
+++ b/solution.py
@@ -54,13 +54,12 @@
         mats, vecs = tiers[height]
         half = mats.shape[0] // 2
         pv = vecs.reshape(half, 2, width)
-        both = jnp.broadcast_to(states[:, None, :], (half, 2, width)).reshape(-1, width)
-        applied = mv_whole(mats, both).reshape(half, 2, width)
+        rows = mats.reshape(half, 2 * width, width)
         if backward:
-            other = applied[:, 1] + pv[:, 1]
+            other = mv_whole(rows[:, width:], states) + pv[:, 1]
             states = jnp.stack((other, states), axis=1)
         else:
-            other = applied[:, 0] + pv[:, 0]
+            other = mv_whole(rows[:, :width], states) + pv[:, 0]
             states = jnp.stack((states, other), axis=1)
         states = states.reshape(-1, width)
     return mv_whole(tiers[0][0], states) + tiers[0][1]

time: 91 us -> 87 us (0.956)
  matrix products: 26.1 us -> 24.2 us
  other arithmetic: 26 us -> 24.2 us
    dot_general x1, matrix products: 5.92 us -> 4.06 us  [on_device(): jnp.einsum('tij,jk->tik', gains, mapped, precision=exact, preferred_eleme...]
    reduce_sum x25, other arithmetic: 20.2 us -> 19.1 us  [mv_whole(): return jnp.sum(a * v[..., None, :], axis=-1)]
    mul x13 -> x14, other arithmetic: 2.34 us -> 2.34 us  [mv_whole(): return jnp.sum(a * v[..., None, :], axis=-1)]
  transfers between devices with their start and end apart: 6 -> 6, of which waited for: 3 -> 3; matrix products, arithmetic and copies ran while one was open for 9% -> 10% of each run, Pallas kernels for 0% -> 0%
where the time goes in v9:
time: 87 us; the launch traced here: 86.6 us
  other arithmetic  24.2 us (28%)
  matrix products  24.2 us (28%)
  blocking collectives  21.6 us (25%)
  starting transfers between devices  8.78 us (10%)
  waiting for transfers between devices  4.94 us (6%)
  between operations  1.87 us (2%)
  local copies, waits for them, and re-layouts  1.04 us (1%)
    all_gather x2, blocking collectives, across(): gathered = lax.all_gather(pack(mat, vec), 'inner')  21.6 us
    dot_general x25, matrix products, mm(): return jnp.matmul(a, b, precision=exact, preferred_element_type=jnp.float32)  19.9 us
    reduce_sum x25, other arithmetic, mv_whole(): return jnp.sum(a * v[..., None, :], axis=-1)  19.1 us
    ppermute x6, starting transfers between devices, from_other_groups(): received.append(lax.ppermute(packed, 'outer', pairs))  8.78 us
    ppermute x6, waiting for transfers between devices, from_other_groups(): received.append(lax.ppermute(packed, 'outer', pairs))  4.94 us
    dot_general x1, matrix products, on_device(): jnp.einsum('tij,jk->tik', gains, mapped, precision=exact, preferred_eleme...  4.06 us
    mul x14, other arithmetic, mv_whole(): return jnp.sum(a * v[..., None, :], axis=-1)  2.34 us
  transfers between devices with their start and end apart: 6, of which 3 were waited for; matrix products, arithmetic and copies ran while one was open for 10% of the time, Pallas kernels for 0%

profile of v9, /device:TPU:0, one launch (start us, length us, event | category | flops | bytes accessed | tf_op | source)
XLA Modules:
  0.0 86.6 jit_solution(16311213104107674817)
XLA Ops:
  0.7 3.5 %multiply_reduce_fusion.5 = f32[64,128]{1,0:T(8,128)S(1)} fusion(f32[64,128,128]{2,1,0:T(8,128)} %param.7, f32[64,128]{1,0:T(8,128)} %param.6), kind=kLoop, calls=%fused_computation.6 | loop fusion | flops 2088960 | bytes 4259840 | tf_op jit(solution)/shard_map/reduce_sum | solution.py:19
  4.5 4.1 %multiply_reduce_fusion.4 = (f32[64,128]{1,0:T(8,128)S(1)}, f32[64,128,128]{2,1,0:T(8,128)S(1)}) fusion(f32[64,128]{1,0:T(8,128)S(1)} %bitcast.594, f32[128,128,1]{1,0,2:T(8,128)S(1)} %convolution_bitcast_fusion, f32[64,128,128]{2,1,0:T(8,128)S(1)} %copy-done.4, f32[128,128]{1,0:T(8,128)S(1)} %copy-done.7), kind=kOutput, calls=%fused_computation.5 | convolution fusion | flops 1613750272 | bytes 8585216 | tf_op jit(solution)/shard_map/tij,jk->tik/dot_general | solution.py:135
  8.7 2.6 %multiply_reduce_fusion.7 = (f32[32,128]{1,0:T(8,128)S(1)}, f32[32,128,128]{2,1,0:T(8,128)S(1)}) fusion(f32[32,128]{1,0:T(8,128)S(1)} %bitcast.612, f32[32,2,128,128]{3,2,1,0:T(8,128)S(1)} %bitcast.541), kind=kOutput, calls=%fused_computation.18 | convolution fusion | flops 806350848 | bytes 6324224 | tf_op jit(solution)/shard_map/dot_general | solution.py:11
  11.4 1.4 %multiply_reduce_fusion.9 = (f32[16,128]{1,0:T(8,128)S(1)}, f32[16,128,128]{2,1,0:T(8,128)S(1)}) fusion(f32[16,128]{1,0:T(8,128)S(1)} %bitcast.634, f32[16,2,128,128]{3,2,1,0:T(8,128)S(1)} %bitcast.543), kind=kOutput, calls=%fused_computation.31 | convolution fusion | flops 403175424 | bytes 3162112 | tf_op jit(solution)/shard_map/dot_general | solution.py:11
  12.8 0.8 multiply_reduce_fusion.15
  15.6 11.6 %all-gather.2 = f32[8,129,128]{2,1,0:T(8,128)S(1)} all-gather(f32[1,129,128]{2,1,0:T(8,128)S(1)} %maximum_bitcast_fusion), channel_id=2, replica_groups=mesh['outer'=4,'inner'=8] {'inner'}, dimensions={0}, use_global_device_ids=true | all-gather | bytes 594432 | tf_op jit(solution)/shard_map/all_gather | solution.py:116
  29.7 3.6 %collective-permute-start.2 = (f32[129,128]{1,0:T(8,128)}, f32[129,128]{1,0:T(8,128)}, u32[]{:S(2)}, u32[]{:S(2)}) collective-permute-start(f32[129,128]{1,0:T(8,128)} %pad_maximum_fusion), channel_id=1, source_target_pairs={{0,24},{8,0},{16,8},{24,16},{1,25},{9,1},{17,9},{25,17},{2,26},{10... | collective-permute-start | bytes 198152 | tf_op jit(solution)/shard_map/ppermute | solution.py:110
  33.3 1.0 %collective-permute-start = (f32[129,128]{1,0:T(8,128)}, f32[129,128]{1,0:T(8,128)}, u32[]{:S(2)}, u32[]{:S(2)}) collective-permute-start(f32[129,128]{1,0:T(8,128)} %pad_maximum_fusion), channel_id=1, source_target_pairs={{0,8},{8,16},{16,24},{24,0},{1,9},{9,17},{17,25},{25,1},{2,10},{10... | collective-permute-start | bytes 198152 | tf_op jit(solution)/shard_map/ppermute | solution.py:110
  34.9 1.3 %multiply_reduce_fusion.19 = (f32[4,128]{1,0:T(4,128)S(1)}, f32[4,128,128]{1,2,0:T(8,128)}) fusion(f32[4,128]{1,0:T(4,128)S(1)} %bitcast.675, f32[4,2,128,128]{3,2,1,0:T(8,128)S(1)} %bitcast.555), kind=kOutput, calls=%fused_computation.73 | convolution fusion | flops 100793856 | bytes 790528 | tf_op jit(solution)/shard_map/dot_general | solution.py:11
  36.3 1.9 %multiply_reduce_fusion.25 = (f32[2,128]{1,0:T(2,128)S(1)}, f32[2,128,128]{1,2,0:T(8,128)}) fusion(f32[2,128]{1,0:T(2,128)S(1)} %maximum_bitcast_fusion.4, f32[2,2,128,128]{2,3,1,0:T(8,128)} %bitcast.563), kind=kOutput, calls=%fused_computation.109 | convolution fusion | flops 50396928 | bytes 395264 | tf_op jit(solution)/shard_map/dot_general | solution.py:11
  38.2 1.1 %fusion.33 = f32[128]{0:T(128)S(1)} fusion(f32[129,128]{1,0:T(8,128)} %collective-permute-done.2, f32[128]{0:T(128)} %param.11, pred[]{:T(512)S(6)} %ge.11), kind=kLoop, calls=%fused_computation.121 | loop fusion | flops 81792 | bytes 66561 | tf_op jit(solution)/shard_map/reduce_sum | solution.py:19
  39.3 0.9 %fusion.52 = f32[128]{0:T(128)S(1)} fusion(pred[]{:T(512)S(6)} %ge.11, f32[129,128]{1,0:T(8,128)} %collective-permute-done.2, f32[128]{0:T(128)S(1)} %fusion.33), kind=kLoop, calls=%fused_computation.225 | loop fusion | flops 256 | bytes 1537 | tf_op jit(solution)/shard_map/mul | solution.py:19
  40.2 0.8 collective-permute-done.1
  41.0 0.9 %fusion.31 = f32[128]{0:T(128)S(1)} fusion(f32[129,128]{1,0:T(8,128)} %collective-permute-done.1, f32[128]{0:T(128)S(1)} %fusion.52, pred[]{:T(512)S(6)} %ge.10), kind=kLoop, calls=%fused_computation.119 | loop fusion | flops 81792 | bytes 66561 | tf_op jit(solution)/shard_map/reduce_sum | solution.py:19
  42.6 0.9 %fusion.29 = f32[128]{0:T(128)S(1)} fusion(f32[129,128]{1,0:T(8,128)} %collective-permute-done, f32[128]{0:T(128)S(1)} %fusion.54, pred[]{:T(512)S(6)} %ge.9), kind=kLoop, calls=%fused_computation.117 | loop fusion | flops 81792 | bytes 66561 | tf_op jit(solution)/shard_map/reduce_sum | solution.py:19
  44.3 1.1 %multiply_reduce_fusion.30 = f32[128]{0:T(128)S(1)} fusion(f32[128]{0:T(128)S(1)} %fusion.56, f32[1,2,128,128]{2,3,1,0:T(8,128)} %bitcast.575), kind=kOutput, calls=%fused_computation.152 | convolution fusion | flops 25198464 | bytes 132096 | tf_op jit(solution)/shard_map/dot_general | solution.py:11
  45.4 0.9 %fusion.44 = f32[128]{0:T(128)S(1)} fusion(f32[1,256,128]{2,1,0:T(8,128)} %bitcast.572, f32[128]{0:T(128)S(1)} %bitcast.692), kind=kLoop, calls=%fused_computation.140 | loop fusion | flops 32640 | bytes 66560 | tf_op jit(solution)/shard_map/reduce_sum | solution.py:19
  46.5 1.1 %fusion.16 = f32[4,128]{1,0:T(4,128)S(1)} fusion(f32[4,256,128]{2,1,0:T(8,128)} %bitcast.552, f32[4,128]{1,0:T(4,128)S(1)} %bitcast.638), kind=kLoop, calls=%fused_computation.60 | loop fusion | flops 130560 | bytes 266240 | tf_op jit(solution)/shard_map/reduce_sum | solution.py:19
  48.3 2.5 %fusion.2 = f32[32,128]{1,0:T(8,128)S(1)} fusion(f32[32,256,128]{2,1,0:T(8,128)} %bitcast.542, f32[32,128]{1,0:T(8,128)S(1)} %bitcast.586), kind=kLoop, calls=%fused_computation.13 | loop fusion | flops 1044480 | bytes 2129920 | tf_op jit(solution)/shard_map/reduce_sum | solution.py:19
  50.9 1.2 %multiply_reduce_fusion.3 = f32[64,128]{1,0:T(8,128)S(1)} fusion(f32[64,128,128]{2,1,0:T(8,128)S(1)} %copy-done.3, f32[64,128]{1,0:T(8,128)S(1)} %bitcast.595), kind=kLoop, calls=%fused_computation.4 | loop fusion | flops 2088960 | bytes 4259840 | tf_op jit(solution)/shard_map/reduce_sum | solution.py:19
  52.4 1.2 %multiply_reduce_fusion.2 = f32[64,128]{1,0:T(8,128)S(1)} fusion(f32[64,128,128]{2,1,0:T(8,128)S(1)} %copy-done.1, f32[64,128]{1,0:T(8,128)S(1)} %fusion.91), kind=kLoop, calls=%fused_computation.3 | loop fusion | flops 2088960 | bytes 4259840 | tf_op jit(solution)/shard_map/reduce_sum | solution.py:19
  53.6 1.2 %multiply_reduce_fusion.1 = f32[64,128]{1,0:T(8,128)S(1)} fusion(f32[64,128,128]{2,1,0:T(8,128)S(1)} %copy-done.1, f32[64,128]{1,0:T(8,128)S(1)} %bitcast.596), kind=kLoop, calls=%fused_computation.2 | loop fusion | flops 2088960 | bytes 4259840 | tf_op jit(solution)/shard_map/reduce_sum | solution.py:19
  54.9 2.5 %multiply_reduce_fusion.6 = (f32[32,128]{1,0:T(8,128)S(1)}, f32[32,128,128]{2,1,0:T(8,128)S(1)}) fusion(f32[32,128]{1,0:T(8,128)S(1)} %bitcast.613, f32[32,2,128,128]{3,2,1,0:T(8,128)S(1)} %bitcast.539), kind=kOutput, calls=%fused_computation.17 | convolution fusion | flops 806350848 | bytes 6324224 | tf_op jit(solution)/shard_map/dot_general | solution.py:11
  57.5 1.4 %multiply_reduce_fusion.8 = (f32[16,128]{1,0:T(8,128)S(1)}, f32[16,128,128]{2,1,0:T(8,128)S(1)}) fusion(f32[16,128]{1,0:T(8,128)S(1)} %bitcast.635, f32[16,2,128,128]{3,2,1,0:T(8,128)S(1)} %bitcast.545), kind=kOutput, calls=%fused_computation.30 | convolution fusion | flops 403175424 | bytes 3162112 | tf_op jit(solution)/shard_map/dot_general | solution.py:11
  58.9 0.8 multiply_reduce_fusion.12
  61.3 10.0 %all-gather.3 = f32[8,129,128]{2,1,0:T(8,128)S(1)} all-gather(f32[1,129,128]{2,1,0:T(8,128)S(1)} %maximum_bitcast_fusion.1), channel_id=3, replica_groups=mesh['outer'=4,'inner'=8] {'inner'}, dimensions={0}, use_global_device_ids=true | all-gather | bytes 594432 | tf_op jit(solution)/shard_map/all_gather | solution.py:116
  73.1 1.7 %collective-permute-start.5 = (f32[129,128]{1,0:T(8,128)S(1)}, f32[129,128]{1,0:T(8,128)S(1)}, u32[]{:S(2)}, u32[]{:S(2)}) collective-permute-start(f32[129,128]{1,0:T(8,128)S(1)} %pad_maximum_fusion.1), channel_id=1, source_target_pairs={{0,8},{8,16},{16,24},{24,0},{1,9},{9,17},{17,25},{25,1},{2,10},{10... | collective-permute-start | bytes 198152 | tf_op jit(solution)/shard_map/ppermute | solution.py:110
  74.8 0.9 %collective-permute-start.4 = (f32[129,128]{1,0:T(8,128)S(1)}, f32[129,128]{1,0:T(8,128)S(1)}, u32[]{:S(2)}, u32[]{:S(2)}) collective-permute-start(f32[129,128]{1,0:T(8,128)S(1)} %pad_maximum_fusion.1), channel_id=1, source_target_pairs={{0,16},{8,24},{16,0},{24,8},{1,17},{9,25},{17,1},{25,9},{2,18},{10... | collective-permute-start | bytes 198152 | tf_op jit(solution)/shard_map/ppermute | solution.py:110
  75.7 1.5 %collective-permute-start.3 = (f32[129,128]{1,0:T(8,128)S(1)}, f32[129,128]{1,0:T(8,128)S(1)}, u32[]{:S(2)}, u32[]{:S(2)}) collective-permute-start(f32[129,128]{1,0:T(8,128)S(1)} %pad_maximum_fusion.1), channel_id=1, source_target_pairs={{0,24},{8,0},{16,8},{24,16},{1,25},{9,1},{17,9},{25,17},{2,26},{10... | collective-permute-start | bytes 198152 | tf_op jit(solution)/shard_map/ppermute | solution.py:110
  78.2 1.8 %collective-permute-done.5 = f32[129,128]{1,0:T(8,128)S(1)} collective-permute-done((f32[129,128]{1,0:T(8,128)S(1)}, f32[129,128]{1,0:T(8,128)S(1)}, u32[]{:S(2)}, u32[]{:S(2)}) %collective-permute-start.5) | collective-permute-done | bytes 66080 | tf_op jit(solution)/shard_map/ppermute | solution.py:110
  80.2 2.3 %collective-permute-done.4 = f32[129,128]{1,0:T(8,128)S(1)} collective-permute-done((f32[129,128]{1,0:T(8,128)S(1)}, f32[129,128]{1,0:T(8,128)S(1)}, u32[]{:S(2)}, u32[]{:S(2)}) %collective-permute-start.4) | collective-permute-done | bytes 66080 | tf_op jit(solution)/shard_map/ppermute | solution.py:110
  84.8 1.2 %multiply_reduce_fusion = f32[64,128]{1,0:T(8,128)S(1)} fusion(f32[64,128,128]{2,1,0:T(8,128)S(1)} %copy-done.1, f32[64,128]{1,0:T(8,128)S(1)} %bitcast.597), kind=kLoop, calls=%fused_computation.1 | loop fusion | flops 2088960 | bytes 4259840 | tf_op jit(solution)/shard_map/reduce_sum | solution.py:19
  (187 shorter events, 15.0 us)
Async XLA Ops:
  0.6 3.7 %copy-start = (f32[128,128]{1,0:T(8,128)S(1)}, f32[128,128]{1,0:T(8,128)}, u32[]{:S(2)}) copy-start(f32[128,128]{1,0:T(8,128)} %param.10) | copy-start | bytes 196612
  0.6 3.7 %copy-start.7 = (f32[128,128]{1,0:T(8,128)S(1)}, f32[128,128]{1,0:T(8,128)}, u32[]{:S(2)}) copy-start(f32[128,128]{1,0:T(8,128)} %param.9) | copy-start | bytes 196612
  0.7 3.9 %copy-start.4 = (f32[64,128,128]{2,1,0:T(8,128)S(1)}, f32[64,128,128]{2,1,0:T(8,128)}, u32[]{:S(2)}) copy-start(f32[64,128,128]{2,1,0:T(8,128)} %param.7) | copy-start | bytes 12582916
  0.7 26.6 %copy-start.9 = (f32[128,128]{1,0:T(8,128)}, f32[128,128]{1,0:T(8,128)S(1)}, u32[]{:S(2)}) copy-start(f32[128,128]{1,0:T(8,128)S(1)} %fusion.48) | copy-start | bytes 196612
  8.6 4.2 %copy-start.2 = (f32[64,128,128]{2,1,0:T(8,128)}, f32[64,128,128]{2,1,0:T(8,128)S(1)}, u32[]{:S(2)}) copy-start(f32[64,128,128]{2,1,0:T(8,128)S(1)} %get-tuple-element.63) | copy-start | bytes 12582916
  13.6 0.8 copy-start.5
  15.3 12.0 %copy-start.6 = (f32[2,128,128]{2,1,0:T(8,128)}, f32[2,128,128]{2,1,0:T(8,128)S(1)}, u32[]{:S(2)}) copy-start(f32[2,128,128]{2,1,0:T(8,128)S(1)} %get-tuple-element.73) | copy-start | bytes 393220
  29.7 8.5 %collective-permute-start.2 = (f32[129,128]{1,0:T(8,128)}, f32[129,128]{1,0:T(8,128)}, u32[]{:S(2)}, u32[]{:S(2)}) collective-permute-start(f32[129,128]{1,0:T(8,128)} %pad_maximum_fusion), channel_id=1, source_target_pairs={{0,24},{8,0},{16,8},{24,16},{1,25},{9,1},{17,9},{25,17},{2,26},{10... | collective-permute-start | bytes 198152 | tf_op jit(solution)/shard_map/ppermute | solution.py:110
  33.3 7.7 %collective-permute-start.1 = (f32[129,128]{1,0:T(8,128)}, f32[129,128]{1,0:T(8,128)}, u32[]{:S(2)}, u32[]{:S(2)}) collective-permute-start(f32[129,128]{1,0:T(8,128)} %pad_maximum_fusion), channel_id=1, source_target_pairs={{0,16},{8,24},{16,0},{24,8},{1,17},{9,25},{17,1},{25,9},{2,18},{10... | collective-permute-start | bytes 198152 | tf_op jit(solution)/shard_map/ppermute | solution.py:110
  33.3 9.3 %collective-permute-start = (f32[129,128]{1,0:T(8,128)}, f32[129,128]{1,0:T(8,128)}, u32[]{:S(2)}, u32[]{:S(2)}) collective-permute-start(f32[129,128]{1,0:T(8,128)} %pad_maximum_fusion), channel_id=1, source_target_pairs={{0,8},{8,16},{16,24},{24,0},{1,9},{9,17},{17,25},{25,1},{2,10},{10... | collective-permute-start | bytes 198152 | tf_op jit(solution)/shard_map/ppermute | solution.py:110
  38.2 12.8 %copy-start.3 = (f32[64,128,128]{2,1,0:T(8,128)S(1)}, f32[64,128,128]{2,1,0:T(8,128)}, u32[]{:S(2)}) copy-start(f32[64,128,128]{2,1,0:T(8,128)} %copy-done.2) | copy-start | bytes 12582916
  47.6 4.5 %copy-start.8 = (f32[128,128]{1,0:T(8,128)S(1)}, f32[128,128]{1,0:T(8,128)}, u32[]{:S(2)}) copy-start(f32[128,128]{1,0:T(8,128)} %param.9) | copy-start | bytes 196612
  47.6 4.7 %copy-start.1 = (f32[64,128,128]{2,1,0:T(8,128)S(1)}, f32[64,128,128]{2,1,0:T(8,128)}, u32[]{:S(2)}) copy-start(f32[64,128,128]{2,1,0:T(8,128)} %param.8) | copy-start | bytes 12582916
  52.1 33.8 %copy-start.11 = (f32[64,128]{1,0:T(8,128)}, f32[64,128]{1,0:T(8,128)S(1)}, u32[]{:S(2)}) copy-start(f32[64,128]{1,0:T(8,128)S(1)} %add.391) | copy-start | bytes 98308
  57.4 13.8 %copy-start.12 = (pred[4,2]{1,0:T(4,128)(4,1)S(1)}, pred[4,2]{1,0:T(4,128)(4,1)}, u32[]{:S(2)}) copy-start(pred[4,2]{1,0:T(4,128)(4,1)} %fusion.49) | copy-start | bytes 28
  57.4 13.9 %copy-start.10 = (f32[128,128]{1,0:T(8,128)S(1)}, f32[128,128]{1,0:T(8,128)}, u32[]{:S(2)}) copy-start(f32[128,128]{1,0:T(8,128)} %copy-done.9) | copy-start | bytes 196612
  73.1 7.0 %collective-permute-start.5 = (f32[129,128]{1,0:T(8,128)S(1)}, f32[129,128]{1,0:T(8,128)S(1)}, u32[]{:S(2)}, u32[]{:S(2)}) collective-permute-start(f32[129,128]{1,0:T(8,128)S(1)} %pad_maximum_fusion.1), channel_id=1, source_target_pairs={{0,8},{8,16},{16,24},{24,0},{1,9},{9,17},{17,25},{25,1},{2,10},{10... | collective-permute-start | bytes 198152 | tf_op jit(solution)/shard_map/ppermute | solution.py:110
  74.8 7.6 %collective-permute-start.4 = (f32[129,128]{1,0:T(8,128)S(1)}, f32[129,128]{1,0:T(8,128)S(1)}, u32[]{:S(2)}, u32[]{:S(2)}) collective-permute-start(f32[129,128]{1,0:T(8,128)S(1)} %pad_maximum_fusion.1), channel_id=1, source_target_pairs={{0,16},{8,24},{16,0},{24,8},{1,17},{9,25},{17,1},{25,9},{2,18},{10... | collective-permute-start | bytes 198152 | tf_op jit(solution)/shard_map/ppermute | solution.py:110
  75.7 6.9 %collective-permute-start.3 = (f32[129,128]{1,0:T(8,128)S(1)}, f32[129,128]{1,0:T(8,128)S(1)}, u32[]{:S(2)}, u32[]{:S(2)}) collective-permute-start(f32[129,128]{1,0:T(8,128)S(1)} %pad_maximum_fusion.1), channel_id=1, source_target_pairs={{0,24},{8,0},{16,8},{24,16},{1,25},{9,1},{17,9},{25,17},{2,26},{10... | collective-permute-start | bytes 198152 | tf_op jit(solution)/shard_map/ppermute | solution.py:110

commit v10 on v9

--- a/solution.py
+++ b/solution.py
@@ -25,9 +25,9 @@
     pv = vecs.reshape(count // 2, 2, width)
     first, second = (1, 0) if backward else (0, 1)
     joined = mm(pm[:, second], pm[:, first])
-    partner = jnp.stack((pv[:, 1], pv[:, 0]), axis=1).reshape(count, width)
-    crossed = mv_whole(mats, partner).reshape(count // 2, 2, width)
-    return joined, crossed[:, second] + pv[:, second]
+    rows = mats.reshape(count // 2, 2 * width, width)
+    later = rows[:, width:] if second == 1 else rows[:, :width]
+    return joined, mv_whole(later, pv[:, first]) + pv[:, second]
 
 
 def pair_up(mats, vecs, backward):

time: 87 us -> 93.9 us (1.079)
  other arithmetic: 24.2 us -> 30.1 us
  local copies, waits for them, and re-layouts: 1.04 us -> 4.59 us
  matrix products: 24.2 us -> 22.3 us
  waiting for transfers between devices: 4.94 us -> 3.09 us
    reduce_sum x25 -> x46, other arithmetic: 19.1 us -> 25.3 us  [mv_whole(): return jnp.sum(a * v[..., None, :], axis=-1)]
    unnamed x26 -> x42, local copies, waits for them, and re-layouts: 0.8 us -> 3.89 us
    ppermute x6, waiting for transfers between devices: 4.94 us -> 3.09 us  [from_other_groups(): received.append(lax.ppermute(packed, 'outer', pairs))]
    dot_general x25, matrix products: 19.9 us -> 18.1 us  [mm(): return jnp.matmul(a, b, precision=exact, preferred_element_type=jnp.float32)]
    mul x14 -> x8, other arithmetic: 2.34 us -> 2.1 us  [mv_whole(): return jnp.sum(a * v[..., None, :], axis=-1)]
  transfers between devices with their start and end apart: 6 -> 6, of which waited for: 3 -> 2; matrix products, arithmetic and copies ran while one was open for 10% -> 17% of each run, Pallas kernels for 0% -> 0%
where the time goes in v10:
time: 93.9 us; the launch traced here: 93.2 us
  other arithmetic  30.1 us (32%)
  matrix products  22.3 us (24%)
  blocking collectives  21.6 us (23%)
  starting transfers between devices  9.61 us (10%)
  local copies, waits for them, and re-layouts  4.59 us (5%)
  waiting for transfers between devices  3.09 us (3%)
  between operations  1.94 us (2%)
    reduce_sum x46, other arithmetic, mv_whole(): return jnp.sum(a * v[..., None, :], axis=-1)  25.3 us
    all_gather x2, blocking collectives, across(): gathered = lax.all_gather(pack(mat, vec), 'inner')  21.6 us
    dot_general x25, matrix products, mm(): return jnp.matmul(a, b, precision=exact, preferred_element_type=jnp.float32)  18.1 us
    ppermute x6, starting transfers between devices, from_other_groups(): received.append(lax.ppermute(packed, 'outer', pairs))  9.61 us
    dot_general x1, matrix products, on_device(): jnp.einsum('tij,jk->tik', gains, mapped, precision=exact, preferred_eleme...  3.92 us
    unnamed x42, local copies, waits for them, and re-layouts  3.89 us
    ppermute x6, waiting for transfers between devices, from_other_groups(): received.append(lax.ppermute(packed, 'outer', pairs))  3.09 us
    mul x8, other arithmetic, mv_whole(): return jnp.sum(a * v[..., None, :], axis=-1)  2.1 us
  transfers between devices with their start and end apart: 6, of which 2 were waited for; matrix products, arithmetic and copies ran while one was open for 17% of the time, Pallas kernels for 0%

profile of v10, /device:TPU:0, one launch (start us, length us, event | category | flops | bytes accessed | tf_op | source)
XLA Modules:
  0.0 93.2 jit_solution(13793981215549077647)
XLA Ops:
  0.7 3.5 %multiply_reduce_fusion.3 = f32[64,128]{1,0:T(8,128)S(1)} fusion(f32[64,128,128]{2,1,0:T(8,128)} %param.7, f32[64,128]{1,0:T(8,128)} %param.6), kind=kLoop, calls=%fused_computation.4 | loop fusion | flops 2088960 | bytes 4259840 | tf_op jit(solution)/shard_map/reduce_sum | solution.py:19
  4.5 3.9 %bitcast_subtract_fusion = f32[64,128,128]{2,1,0:T(8,128)S(1)} fusion(f32[128,128,1]{1,0,2:T(8,128)S(1)} %convolution_bitcast_fusion, f32[64,128,128]{2,1,0:T(8,128)S(1)} %copy-done.5, f32[128,128]{1,0:T(8,128)S(1)} %copy-done.13), kind=kOutput, calls=%fused_computation | convolution fusion | flops 1611661312 | bytes 8519680 | tf_op jit(solution)/shard_map/tij,jk->tik/dot_general | solution.py:135
  9.1 2.3 %fusion.5 = f32[32,128,128]{2,1,0:T(8,128)S(1)} fusion(f32[32,2,128,128]{3,2,1,0:T(8,128)S(1)} %bitcast.500), kind=kOutput, calls=%fused_computation.17 | convolution fusion | flops 805306368 | bytes 6291456 | tf_op jit(solution)/shard_map/dot_general | solution.py:11
  11.8 1.2 %fusion.11 = f32[16,128,128]{2,1,0:T(8,128)S(1)} fusion(f32[16,2,128,128]{3,2,1,0:T(8,128)S(1)} %bitcast.509), kind=kOutput, calls=%fused_computation.32 | convolution fusion | flops 402653184 | bytes 3145728 | tf_op jit(solution)/shard_map/dot_general | solution.py:11
  17.5 11.4 %all-gather.2 = f32[8,129,128]{2,1,0:T(8,128)S(1)} all-gather(f32[1,129,128]{2,1,0:T(8,128)S(1)} %maximum_bitcast_fusion), channel_id=2, replica_groups=mesh['outer'=4,'inner'=8] {'inner'}, dimensions={0}, use_global_device_ids=true | all-gather | bytes 594432 | tf_op jit(solution)/shard_map/all_gather | solution.py:116
  31.0 3.6 %collective-permute-start.2 = (f32[129,128]{1,0:T(8,128)}, f32[129,128]{1,0:T(8,128)}, u32[]{:S(2)}, u32[]{:S(2)}) collective-permute-start(f32[129,128]{1,0:T(8,128)} %pad_maximum_fusion), channel_id=1, source_target_pairs={{0,24},{8,0},{16,8},{24,16},{1,25},{9,1},{17,9},{25,17},{2,26},{10... | collective-permute-start | bytes 198152 | tf_op jit(solution)/shard_map/ppermute | solution.py:110
  34.6 1.0 %collective-permute-start = (f32[129,128]{1,0:T(8,128)}, f32[129,128]{1,0:T(8,128)}, u32[]{:S(2)}, u32[]{:S(2)}) collective-permute-start(f32[129,128]{1,0:T(8,128)} %pad_maximum_fusion), channel_id=1, source_target_pairs={{0,8},{8,16},{16,24},{24,0},{1,9},{9,17},{17,25},{25,1},{2,10},{10... | collective-permute-start | bytes 198152 | tf_op jit(solution)/shard_map/ppermute | solution.py:110
  36.6 0.9 fusion.43
  38.4 4.4 %fusion.1 = f32[32,128,128]{2,1,0:T(8,128)S(1)} fusion(f32[32,2,128,128]{3,2,1,0:T(8,128)} %bitcast.502), kind=kOutput, calls=%fused_computation.8 | convolution fusion | flops 805306368 | bytes 6291456 | tf_op jit(solution)/shard_map/dot_general | solution.py:11
  42.8 1.1 %fusion.7 = f32[16,128,128]{2,1,0:T(8,128)S(1)} fusion(f32[16,2,128,128]{3,2,1,0:T(8,128)S(1)} %bitcast.505), kind=kOutput, calls=%fused_computation.23 | convolution fusion | flops 402653184 | bytes 3145728 | tf_op jit(solution)/shard_map/dot_general | solution.py:11
  44.6 0.8 copy-done.7
  45.8 0.9 fusion.37
  46.7 0.9 %fusion.66 = f32[128]{0:T(128)S(1)} fusion(f32[1,256,128]{2,1,0:T(8,128)} %bitcast.555, f32[128]{0:T(128)} %slice_bitcast_fusion.104), kind=kLoop, calls=%fused_computation.160 | loop fusion | flops 32640 | bytes 66560 | tf_op jit(solution)/shard_map/reduce_sum | solution.py:19
  47.7 0.9 %fusion.51 = f32[128]{0:T(128)S(1)} fusion(f32[129,128]{1,0:T(8,128)} %collective-permute-done.2, f32[128]{0:T(128)S(1)} %copy-done.18, pred[]{:T(512)S(6)} %ge.11), kind=kLoop, calls=%fused_computation.133 | loop fusion | flops 81792 | bytes 66561 | tf_op jit(solution)/shard_map/reduce_sum | solution.py:19
  49.4 0.9 %fusion.49 = f32[128]{0:T(128)S(1)} fusion(f32[129,128]{1,0:T(8,128)} %collective-permute-done.1, f32[128]{0:T(128)S(1)} %fusion.78, pred[]{:T(512)S(6)} %ge.10), kind=kLoop, calls=%fused_computation.131 | loop fusion | flops 81792 | bytes 66561 | tf_op jit(solution)/shard_map/reduce_sum | solution.py:19
  51.0 0.9 %fusion.47 = f32[128]{0:T(128)S(1)} fusion(f32[129,128]{1,0:T(8,128)} %collective-permute-done, f32[128]{0:T(128)S(1)} %fusion.80, pred[]{:T(512)S(6)} %ge.9), kind=kLoop, calls=%fused_computation.129 | loop fusion | flops 81792 | bytes 66561 | tf_op jit(solution)/shard_map/reduce_sum | solution.py:19
  52.7 1.2 %multiply_reduce_fusion.6 = f32[128]{0:T(128)S(1)} fusion(f32[128]{0:T(128)S(1)} %fusion.82, f32[1,2,128,128]{3,2,1,0:T(8,128)} %bitcast.556), kind=kOutput, calls=%fused_computation.176 | convolution fusion | flops 25198464 | bytes 132096 | tf_op jit(solution)/shard_map/dot_general | solution.py:11
  53.8 0.9 %fusion.65 = f32[128]{0:T(128)S(1)} fusion(f32[1,256,128]{2,1,0:T(8,128)} %bitcast.550, f32[128]{0:T(128)S(1)} %bitcast.635), kind=kLoop, calls=%fused_computation.158 | loop fusion | flops 32640 | bytes 66560 | tf_op jit(solution)/shard_map/reduce_sum | solution.py:19
  54.8 1.0 %fusion.39 = f32[2,128]{1,0:T(2,128)S(1)} fusion(f32[2,256,128]{2,1,0:T(8,128)} %bitcast.536, f32[2,128]{1,0:T(2,128)S(1)} %get-tuple-element.41), kind=kLoop, calls=%fused_computation.108 | loop fusion | flops 65280 | bytes 133120 | tf_op jit(solution)/shard_map/reduce_sum | solution.py:19
  55.9 1.3 %fusion.25 = f32[4,128]{1,0:T(4,128)S(1)} fusion(f32[4,256,128]{2,1,0:T(8,128)} %bitcast.522, f32[4,128]{1,0:T(4,128)S(1)} %bitcast.600), kind=kLoop, calls=%fused_computation.66 | loop fusion | flops 130560 | bytes 266240 | tf_op jit(solution)/shard_map/reduce_sum | solution.py:19
  57.2 1.3 %fusion.15 = f32[8,128]{1,0:T(8,128)S(1)} fusion(f32[8,256,128]{2,1,0:T(8,128)} %bitcast.516, f32[8,128]{1,0:T(8,128)S(1)} %bitcast.584), kind=kLoop, calls=%fused_computation.42 | loop fusion | flops 261120 | bytes 532480 | tf_op jit(solution)/shard_map/reduce_sum | solution.py:19
  58.5 1.6 %fusion.9 = f32[16,128]{1,0:T(8,128)S(1)} fusion(f32[16,256,128]{2,1,0:T(8,128)} %bitcast.510, f32[16,128]{1,0:T(8,128)S(1)} %bitcast.572), kind=kLoop, calls=%fused_computation.28 | loop fusion | flops 522240 | bytes 1064960 | tf_op jit(solution)/shard_map/reduce_sum | solution.py:19
  60.1 2.2 %fusion.3 = f32[32,128]{1,0:T(8,128)S(1)} fusion(f32[32,256,128]{2,1,0:T(8,128)} %bitcast.501, f32[32,128]{1,0:T(8,128)S(1)} %bitcast.568), kind=kLoop, calls=%fused_computation.13 | loop fusion | flops 1044480 | bytes 2129920 | tf_op jit(solution)/shard_map/reduce_sum | solution.py:19
  62.5 1.2 %multiply_reduce_fusion.2 = f32[64,128]{1,0:T(8,128)S(1)} fusion(f32[64,128,128]{2,1,0:T(8,128)S(1)} %copy-done.2, f32[64,128]{1,0:T(8,128)S(1)} %bitcast.570), kind=kLoop, calls=%fused_computation.3 | loop fusion | flops 2088960 | bytes 4259840 | tf_op jit(solution)/shard_map/reduce_sum | solution.py:19
  63.9 0.8 copy-done.3
  64.7 1.2 %multiply_reduce_fusion.1 = f32[64,128]{1,0:T(8,128)S(1)} fusion(f32[64,128,128]{2,1,0:T(8,128)S(1)} %copy-done.3, f32[64,128]{1,0:T(8,128)S(1)} %fusion.112), kind=kLoop, calls=%fused_computation.2 | loop fusion | flops 2088960 | bytes 4259840 | tf_op jit(solution)/shard_map/reduce_sum | solution.py:19
  68.0 10.2 %all-gather.3 = f32[8,129,128]{2,1,0:T(8,128)S(1)} all-gather(f32[1,129,128]{2,1,0:T(8,128)S(1)} %maximum_bitcast_fusion.1), channel_id=3, replica_groups=mesh['outer'=4,'inner'=8] {'inner'}, dimensions={0}, use_global_device_ids=true | all-gather | bytes 594432 | tf_op jit(solution)/shard_map/all_gather | solution.py:116
  79.7 2.5 %collective-permute-start.5 = (f32[129,128]{1,0:T(8,128)S(1)}, f32[129,128]{1,0:T(8,128)S(1)}, u32[]{:S(2)}, u32[]{:S(2)}) collective-permute-start(f32[129,128]{1,0:T(8,128)S(1)} %pad_maximum_fusion.1), channel_id=1, source_target_pairs={{0,8},{8,16},{16,24},{24,0},{1,9},{9,17},{17,25},{25,1},{2,10},{10... | collective-permute-start | bytes 198152 | tf_op jit(solution)/shard_map/ppermute | solution.py:110
  82.2 0.9 collective-permute-start.4
  83.1 1.5 %collective-permute-start.3 = (f32[129,128]{1,0:T(8,128)S(1)}, f32[129,128]{1,0:T(8,128)S(1)}, u32[]{:S(2)}, u32[]{:S(2)}) collective-permute-start(f32[129,128]{1,0:T(8,128)S(1)} %pad_maximum_fusion.1), channel_id=1, source_target_pairs={{0,24},{8,0},{16,8},{24,16},{1,25},{9,1},{17,9},{25,17},{2,26},{10... | collective-permute-start | bytes 198152 | tf_op jit(solution)/shard_map/ppermute | solution.py:110
  86.6 2.5 %collective-permute-done.4 = f32[129,128]{1,0:T(8,128)S(1)} collective-permute-done((f32[129,128]{1,0:T(8,128)S(1)}, f32[129,128]{1,0:T(8,128)S(1)}, u32[]{:S(2)}, u32[]{:S(2)}) %collective-permute-start.4) | collective-permute-done | bytes 66080 | tf_op jit(solution)/shard_map/ppermute | solution.py:110
  91.4 1.2 %multiply_reduce_fusion = f32[64,128]{1,0:T(8,128)S(1)} fusion(f32[64,128,128]{2,1,0:T(8,128)S(1)} %copy-done.3, f32[64,128]{1,0:T(8,128)S(1)} %bitcast.571), kind=kLoop, calls=%fused_computation.1 | loop fusion | flops 2088960 | bytes 4259840 | tf_op jit(solution)/shard_map/reduce_sum | solution.py:19
  (196 shorter events, 21.1 us)
Async XLA Ops:
  0.6 3.6 %copy-start = (f32[128,128]{1,0:T(8,128)S(1)}, f32[128,128]{1,0:T(8,128)}, u32[]{:S(2)}) copy-start(f32[128,128]{1,0:T(8,128)} %param.10) | copy-start | bytes 196612
  0.7 28.3 %copy-start.15 = (f32[128,128]{1,0:T(8,128)}, f32[128,128]{1,0:T(8,128)S(1)}, u32[]{:S(2)}) copy-start(f32[128,128]{1,0:T(8,128)S(1)} %fusion.72) | copy-start | bytes 196612
  0.7 3.6 %copy-start.13 = (f32[128,128]{1,0:T(8,128)S(1)}, f32[128,128]{1,0:T(8,128)}, u32[]{:S(2)}) copy-start(f32[128,128]{1,0:T(8,128)} %param.9) | copy-start | bytes 196612
  0.7 3.8 %copy-start.5 = (f32[64,128,128]{2,1,0:T(8,128)S(1)}, f32[64,128,128]{2,1,0:T(8,128)}, u32[]{:S(2)}) copy-start(f32[64,128,128]{2,1,0:T(8,128)} %param.7) | copy-start | bytes 12582916
  8.4 3.0 %copy-start.1 = (f32[64,128,128]{2,1,0:T(8,128)}, f32[64,128,128]{2,1,0:T(8,128)S(1)}, u32[]{:S(2)}) copy-start(f32[64,128,128]{2,1,0:T(8,128)S(1)} %bitcast_subtract_fusion) | copy-start | bytes 12582916
  11.4 1.6 %copy-start.4 = (f32[32,128,128]{2,1,0:T(8,128)}, f32[32,128,128]{2,1,0:T(8,128)S(1)}, u32[]{:S(2)}) copy-start(f32[32,128,128]{2,1,0:T(8,128)S(1)} %fusion.5) | copy-start | bytes 6291460
  13.0 1.0 %copy-start.6 = (f32[16,128,128]{2,1,0:T(8,128)}, f32[16,128,128]{2,1,0:T(8,128)S(1)}, u32[]{:S(2)}) copy-start(f32[16,128,128]{2,1,0:T(8,128)S(1)} %fusion.11) | copy-start | bytes 3145732
  14.6 0.8 copy-start.9
  15.8 0.7 copy-start.10
  16.8 0.6 copy-start.12
  31.0 16.7 %collective-permute-start.2 = (f32[129,128]{1,0:T(8,128)}, f32[129,128]{1,0:T(8,128)}, u32[]{:S(2)}, u32[]{:S(2)}) collective-permute-start(f32[129,128]{1,0:T(8,128)} %pad_maximum_fusion), channel_id=1, source_target_pairs={{0,24},{8,0},{16,8},{24,16},{1,25},{9,1},{17,9},{25,17},{2,26},{10... | collective-permute-start | bytes 198152 | tf_op jit(solution)/shard_map/ppermute | solution.py:110
  34.6 14.8 %collective-permute-start.1 = (f32[129,128]{1,0:T(8,128)}, f32[129,128]{1,0:T(8,128)}, u32[]{:S(2)}, u32[]{:S(2)}) collective-permute-start(f32[129,128]{1,0:T(8,128)} %pad_maximum_fusion), channel_id=1, source_target_pairs={{0,16},{8,24},{16,0},{24,8},{1,17},{9,25},{17,1},{25,9},{2,18},{10... | collective-permute-start | bytes 198152 | tf_op jit(solution)/shard_map/ppermute | solution.py:110
  34.6 16.4 %collective-permute-start = (f32[129,128]{1,0:T(8,128)}, f32[129,128]{1,0:T(8,128)}, u32[]{:S(2)}, u32[]{:S(2)}) collective-permute-start(f32[129,128]{1,0:T(8,128)} %pad_maximum_fusion), channel_id=1, source_target_pairs={{0,8},{8,16},{16,24},{24,0},{1,9},{9,17},{17,25},{25,1},{2,10},{10... | collective-permute-start | bytes 198152 | tf_op jit(solution)/shard_map/ppermute | solution.py:110
  43.9 3.8 %copy-start.18 = (f32[128]{0:T(128)S(1)}, f32[128]{0:T(128)}, u32[]{:S(2)}) copy-start(f32[128]{0:T(128)} %param.11) | copy-start | bytes 1540
  44.6 0.8 copy-start.7
  55.9 6.6 %copy-start.2 = (f32[64,128,128]{2,1,0:T(8,128)S(1)}, f32[64,128,128]{2,1,0:T(8,128)}, u32[]{:S(2)}) copy-start(f32[64,128,128]{2,1,0:T(8,128)} %copy-done.1) | copy-start | bytes 12582916
  62.4 1.2 %copy-start.14 = (f32[128,128]{1,0:T(8,128)S(1)}, f32[128,128]{1,0:T(8,128)}, u32[]{:S(2)}) copy-start(f32[128,128]{1,0:T(8,128)} %param.9) | copy-start | bytes 196612
  62.4 2.2 %copy-start.3 = (f32[64,128,128]{2,1,0:T(8,128)S(1)}, f32[64,128,128]{2,1,0:T(8,128)}, u32[]{:S(2)}) copy-start(f32[64,128,128]{2,1,0:T(8,128)} %param.8) | copy-start | bytes 12582916
  63.6 29.0 %copy-start.17 = (f32[64,128]{1,0:T(8,128)}, f32[64,128]{1,0:T(8,128)S(1)}, u32[]{:S(2)}) copy-start(f32[64,128]{1,0:T(8,128)S(1)} %add.314) | copy-start | bytes 98308
  65.8 1.4 %copy-start.8 = (f32[8,128,128]{2,1,0:T(8,128)S(1)}, f32[8,128,128]{2,1,0:T(8,128)}, u32[]{:S(2)}) copy-start(f32[8,128,128]{2,1,0:T(8,128)} %copy-done.7) | copy-start | bytes 1572868
  65.9 1.7 %copy-start.11 = (f32[2,128,128]{2,1,0:T(8,128)S(1)}, f32[2,128,128]{2,1,0:T(8,128)}, u32[]{:S(2)}) copy-start(f32[2,128,128]{2,1,0:T(8,128)} %fusion.37) | copy-start | bytes 393220
  66.5 11.7 %copy-start.16 = (f32[128,128]{1,0:T(8,128)S(1)}, f32[128,128]{1,0:T(8,128)}, u32[]{:S(2)}) copy-start(f32[128,128]{1,0:T(8,128)} %copy-done.15) | copy-start | bytes 196612
  66.5 11.7 %copy-start.19 = (pred[8]{0:T(512)(128)(4,1)S(1)}, pred[8]{0:T(512)(128)(4,1)}, u32[]{:S(2)}) copy-start(pred[8]{0:T(512)(128)(4,1)} %iota_compare_fusion.1) | copy-start | bytes 28
  79.7 6.8 %collective-permute-start.5 = (f32[129,128]{1,0:T(8,128)S(1)}, f32[129,128]{1,0:T(8,128)S(1)}, u32[]{:S(2)}, u32[]{:S(2)}) collective-permute-start(f32[129,128]{1,0:T(8,128)S(1)} %pad_maximum_fusion.1), channel_id=1, source_target_pairs={{0,8},{8,16},{16,24},{24,0},{1,9},{9,17},{17,25},{25,1},{2,10},{10... | collective-permute-start | bytes 198152 | tf_op jit(solution)/shard_map/ppermute | solution.py:110
  82.2 6.8 %collective-permute-start.4 = (f32[129,128]{1,0:T(8,128)S(1)}, f32[129,128]{1,0:T(8,128)S(1)}, u32[]{:S(2)}, u32[]{:S(2)}) collective-permute-start(f32[129,128]{1,0:T(8,128)S(1)} %pad_maximum_fusion.1), channel_id=1, source_target_pairs={{0,16},{8,24},{16,0},{24,8},{1,17},{9,25},{17,1},{25,9},{2,18},{10... | collective-permute-start | bytes 198152 | tf_op jit(solution)/shard_map/ppermute | solution.py:110
  83.1 6.0 %collective-permute-start.3 = (f32[129,128]{1,0:T(8,128)S(1)}, f32[129,128]{1,0:T(8,128)S(1)}, u32[]{:S(2)}, u32[]{:S(2)}) collective-permute-start(f32[129,128]{1,0:T(8,128)S(1)} %pad_maximum_fusion.1), channel_id=1, source_target_pairs={{0,24},{8,0},{16,8},{24,16},{1,25},{9,1},{17,9},{25,17},{2,26},{10... | collective-permute-start | bytes 198152 | tf_op jit(solution)/shard_map/ppermute | solution.py:110

commit v11 on v9

--- a/solution.py
+++ b/solution.py
@@ -19,12 +19,16 @@
     return jnp.sum(a * v[..., None, :], axis=-1)
 
 
-def local_pair(mats, vecs, backward):
+def local_pair(mats, vecs, backward, whole=True):
     count, width = mats.shape[0], mats.shape[-1]
     pm = mats.reshape(count // 2, 2, width, width)
     pv = vecs.reshape(count // 2, 2, width)
     first, second = (1, 0) if backward else (0, 1)
     joined = mm(pm[:, second], pm[:, first])
+    if not whole:
+        rows = mats.reshape(count // 2, 2 * width, width)
+        later = rows[:, width:] if second == 1 else rows[:, :width]
+        return joined, mv_whole(later, pv[:, first]) + pv[:, second]
     partner = jnp.stack((pv[:, 1], pv[:, 0]), axis=1).reshape(count, width)
     crossed = mv_whole(mats, partner).reshape(count // 2, 2, width)
     return joined, crossed[:, second] + pv[:, second]
@@ -84,7 +88,7 @@
 def reduce_maps(mats, vecs, backward):
     mats, vecs = pad_pow2(mats, vecs)
     while mats.shape[-3] > 1:
-        mats, vecs = local_pair(mats, vecs, backward)
+        mats, vecs = local_pair(mats, vecs, backward, whole=False)
     return mats[..., 0, :, :], vecs[..., 0, :]
 
 

time: 87 us -> 92 us (1.057)
  other arithmetic: 24.2 us -> 29.3 us
  waiting for transfers between devices: 4.94 us -> 3.1 us
  matrix products: 24.2 us -> 22.7 us
  local copies, waits for them, and re-layouts: 1.04 us -> 2.43 us
    reduce_sum x25 -> x35, other arithmetic: 19.1 us -> 21.7 us  [mv_whole(): return jnp.sum(a * v[..., None, :], axis=-1)]
    slice x0 -> x2, other arithmetic: none -> 2.07 us  [across(): mats, vecs = (gathered[:, :-1], gathered[:, -1])]
    ppermute x6, waiting for transfers between devices: 4.94 us -> 3.1 us  [from_other_groups(): received.append(lax.ppermute(packed, 'outer', pairs))]
    dot_general x25, matrix products: 19.9 us -> 18.3 us  [mm(): return jnp.matmul(a, b, precision=exact, preferred_element_type=jnp.float32)]
    mul x14 -> x10, other arithmetic: 2.34 us -> 2.28 us  [mv_whole(): return jnp.sum(a * v[..., None, :], axis=-1)]
  transfers between devices with their start and end apart: 6 -> 6, of which waited for: 3 -> 2; matrix products, arithmetic and copies ran while one was open for 10% -> 11% of each run, Pallas kernels for 0% -> 0%
where the time goes in v11:
time: 92 us; the launch traced here: 91.4 us
  other arithmetic  29.3 us (32%)
  matrix products  22.7 us (25%)
  blocking collectives  22.4 us (24%)
  starting transfers between devices  9.58 us (10%)
  waiting for transfers between devices  3.1 us (3%)
  local copies, waits for them, and re-layouts  2.43 us (3%)
  between operations  1.87 us (2%)
    all_gather x2, blocking collectives, across(): gathered = lax.all_gather(pack(mat, vec), 'inner')  22.4 us
    reduce_sum x35, other arithmetic, mv_whole(): return jnp.sum(a * v[..., None, :], axis=-1)  21.7 us
    dot_general x25, matrix products, mm(): return jnp.matmul(a, b, precision=exact, preferred_element_type=jnp.float32)  18.3 us
    ppermute x6, starting transfers between devices, from_other_groups(): received.append(lax.ppermute(packed, 'outer', pairs))  9.58 us
    dot_general x1, matrix products, on_device(): jnp.einsum('tij,jk->tik', gains, mapped, precision=exact, preferred_eleme...  4.11 us
    ppermute x6, waiting for transfers between devices, from_other_groups(): received.append(lax.ppermute(packed, 'outer', pairs))  3.1 us
    mul x10, other arithmetic, mv_whole(): return jnp.sum(a * v[..., None, :], axis=-1)  2.28 us
    slice x2, other arithmetic, across(): mats, vecs = (gathered[:, :-1], gathered[:, -1])  2.07 us
  transfers between devices with their start and end apart: 6, of which 2 were waited for; matrix products, arithmetic and copies ran while one was open for 11% of the time, Pallas kernels for 0%

profile of v11, /device:TPU:0, one launch (start us, length us, event | category | flops | bytes accessed | tf_op | source)
XLA Modules:
  0.0 91.4 jit_solution(17746250923283559746)
XLA Ops:
  1.3 3.7 %multiply_reduce_fusion.5 = f32[64,128]{1,0:T(8,128)S(1)} fusion(f32[64,128,128]{2,1,0:T(8,128)} %param.7, f32[64,128]{1,0:T(8,128)} %param.6), kind=kLoop, calls=%fused_computation.6 | loop fusion | flops 2088960 | bytes 4259840 | tf_op jit(solution)/shard_map/reduce_sum | solution.py:19
  5.4 4.1 %multiply_reduce_fusion.4 = (f32[64,128]{1,0:T(8,128)S(1)}, f32[64,128,128]{2,1,0:T(8,128)S(1)}) fusion(f32[64,128]{1,0:T(8,128)S(1)} %bitcast.608, f32[128,128,1]{1,0,2:T(8,128)S(1)} %convolution_bitcast_fusion, f32[64,128,128]{2,1,0:T(8,128)S(1)} %copy-done.4, f32[128,128]{1,0:T(8,128)S(1)} %copy-done.7), kind=kOutput, calls=%fused_computation.5 | convolution fusion | flops 1613750272 | bytes 8585216 | tf_op jit(solution)/shard_map/tij,jk->tik/dot_general | solution.py:139
  9.6 2.6 %multiply_reduce_fusion.7 = (f32[32,128]{1,0:T(8,128)S(1)}, f32[32,128,128]{2,1,0:T(8,128)S(1)}) fusion(f32[32,128]{1,0:T(8,128)S(1)} %bitcast.626, f32[32,2,128,128]{3,2,1,0:T(8,128)S(1)} %bitcast.543), kind=kOutput, calls=%fused_computation.18 | convolution fusion | flops 806350848 | bytes 6324224 | tf_op jit(solution)/shard_map/dot_general | solution.py:11
  12.3 1.4 %multiply_reduce_fusion.9 = (f32[16,128]{1,0:T(8,128)S(1)}, f32[16,128,128]{2,1,0:T(8,128)S(1)}) fusion(f32[16,128]{1,0:T(8,128)S(1)} %bitcast.646, f32[16,2,128,128]{3,2,1,0:T(8,128)S(1)} %bitcast.545), kind=kOutput, calls=%fused_computation.31 | convolution fusion | flops 403175424 | bytes 3162112 | tf_op jit(solution)/shard_map/dot_general | solution.py:11
  17.1 12.5 %all-gather.2 = f32[8,129,128]{2,1,0:T(8,128)} all-gather(f32[1,129,128]{2,1,0:T(8,128)S(1)} %maximum_bitcast_fusion), channel_id=2, replica_groups=mesh['outer'=4,'inner'=8] {'inner'}, dimensions={0}, use_global_device_ids=true | all-gather | bytes 594432 | tf_op jit(solution)/shard_map/all_gather | solution.py:120
  30.4 2.0 %fusion.84 = (f32[8,128,128]{2,1,0:T(8,128)S(1)}, f32[8,128,128]{2,1,0:T(8,128)}) fusion(f32[8,129,128]{2,1,0:T(8,128)} %all-gather.2, f32[128,128]{1,0:T(8,128)} %fusion.60, pred[8]{0:T(512)(128)(4,1)S(1)} %iota_compare_fusion.2), kind=kLoop, calls=%fused_computation.271 | loop fusion | flops 131072 | bytes 1638408 | tf_op jit(solution)/shard_map/slice | solution.py:121
  34.3 3.6 %collective-permute-start.2 = (f32[129,128]{1,0:T(8,128)}, f32[129,128]{1,0:T(8,128)}, u32[]{:S(2)}, u32[]{:S(2)}) collective-permute-start(f32[129,128]{1,0:T(8,128)} %pad_maximum_fusion), channel_id=1, source_target_pairs={{0,24},{8,0},{16,8},{24,16},{1,25},{9,1},{17,9},{25,17},{2,26},{10... | collective-permute-start | bytes 198152 | tf_op jit(solution)/shard_map/ppermute | solution.py:114
  37.9 1.0 %collective-permute-start = (f32[129,128]{1,0:T(8,128)}, f32[129,128]{1,0:T(8,128)}, u32[]{:S(2)}, u32[]{:S(2)}) collective-permute-start(f32[129,128]{1,0:T(8,128)} %pad_maximum_fusion), channel_id=1, source_target_pairs={{0,8},{8,16},{16,24},{24,0},{1,9},{9,17},{17,25},{25,1},{2,10},{10... | collective-permute-start | bytes 198152 | tf_op jit(solution)/shard_map/ppermute | solution.py:114
  39.4 1.4 %fusion.22 = f32[4,128,128]{2,1,0:T(8,128)S(1)} fusion(f32[4,2,128,128]{3,2,1,0:T(8,128)} %bitcast.557), kind=kOutput, calls=%fused_computation.69 | convolution fusion | flops 100663296 | bytes 786432 | tf_op jit(solution)/shard_map/dot_general | solution.py:11
  40.9 0.9 %fusion.34 = f32[2,128,128]{2,1,0:T(8,128)} fusion(f32[2,2,128,128]{3,2,1,0:T(8,128)S(1)} %bitcast.569), kind=kOutput, calls=%fused_computation.109 | convolution fusion | flops 50331648 | bytes 393216 | tf_op jit(solution)/shard_map/dot_general | solution.py:11
  41.9 1.1 %fusion.19 = f32[4,128]{1,0:T(4,128)S(1)} fusion(f32[4,256,128]{2,1,0:T(8,128)} %bitcast.558, f32[4,128]{1,0:T(4,128)S(1)} %get-tuple-element.26), kind=kLoop, calls=%fused_computation.62 | loop fusion | flops 130560 | bytes 266240 | tf_op jit(solution)/shard_map/reduce_sum | solution.py:19
  43.1 0.9 %fusion.55 = f32[128]{0:T(128)S(1)} fusion(f32[1,256,128]{2,1,0:T(8,128)} %bitcast.589, f32[128]{0:T(128)S(1)} %slice_bitcast_fusion.104), kind=kLoop, calls=%fused_computation.150 | loop fusion | flops 32640 | bytes 66560 | tf_op jit(solution)/shard_map/reduce_sum | solution.py:19
  44.1 1.1 %fusion.41 = f32[128]{0:T(128)S(1)} fusion(f32[129,128]{1,0:T(8,128)} %collective-permute-done.2, f32[128]{0:T(128)} %param.11, pred[]{:T(512)S(6)} %ge.11), kind=kLoop, calls=%fused_computation.125 | loop fusion | flops 81792 | bytes 66561 | tf_op jit(solution)/shard_map/reduce_sum | solution.py:19
  45.2 0.8 fusion.66
  46.1 0.9 %fusion.39 = f32[128]{0:T(128)S(1)} fusion(f32[129,128]{1,0:T(8,128)} %collective-permute-done.1, f32[128]{0:T(128)S(1)} %fusion.66, pred[]{:T(512)S(6)} %ge.10), kind=kLoop, calls=%fused_computation.123 | loop fusion | flops 81792 | bytes 66561 | tf_op jit(solution)/shard_map/reduce_sum | solution.py:19
  47.7 0.9 %fusion.37 = f32[128]{0:T(128)S(1)} fusion(f32[129,128]{1,0:T(8,128)} %collective-permute-done, f32[128]{0:T(128)S(1)} %fusion.68, pred[]{:T(512)S(6)} %ge.9), kind=kLoop, calls=%fused_computation.121 | loop fusion | flops 81792 | bytes 66561 | tf_op jit(solution)/shard_map/reduce_sum | solution.py:19
  49.4 1.2 %multiply_reduce_fusion.18 = f32[128]{0:T(128)S(1)} fusion(f32[128]{0:T(128)S(1)} %fusion.70, f32[1,2,128,128]{3,2,1,0:T(8,128)} %bitcast.590), kind=kOutput, calls=%fused_computation.164 | convolution fusion | flops 25198464 | bytes 132096 | tf_op jit(solution)/shard_map/dot_general | solution.py:11
  50.6 0.9 %fusion.54 = f32[128]{0:T(128)S(1)} fusion(f32[1,256,128]{2,1,0:T(8,128)} %bitcast.582, f32[128]{0:T(128)S(1)} %bitcast.688), kind=kLoop, calls=%fused_computation.148 | loop fusion | flops 32640 | bytes 66560 | tf_op jit(solution)/shard_map/reduce_sum | solution.py:19
  51.7 1.1 %fusion.18 = f32[4,128]{1,0:T(4,128)S(1)} fusion(f32[4,256,128]{2,1,0:T(8,128)} %bitcast.554, f32[4,128]{1,0:T(4,128)S(1)} %bitcast.650), kind=kLoop, calls=%fused_computation.60 | loop fusion | flops 130560 | bytes 266240 | tf_op jit(solution)/shard_map/reduce_sum | solution.py:19
  53.5 2.5 %fusion.2 = f32[32,128]{1,0:T(8,128)S(1)} fusion(f32[32,256,128]{2,1,0:T(8,128)} %bitcast.544, f32[32,128]{1,0:T(8,128)S(1)} %bitcast.600), kind=kLoop, calls=%fused_computation.13 | loop fusion | flops 1044480 | bytes 2129920 | tf_op jit(solution)/shard_map/reduce_sum | solution.py:19
  56.1 1.2 %multiply_reduce_fusion.3 = f32[64,128]{1,0:T(8,128)S(1)} fusion(f32[64,128,128]{2,1,0:T(8,128)S(1)} %copy-done.3, f32[64,128]{1,0:T(8,128)S(1)} %bitcast.609), kind=kLoop, calls=%fused_computation.4 | loop fusion | flops 2088960 | bytes 4259840 | tf_op jit(solution)/shard_map/reduce_sum | solution.py:19
  57.6 1.2 %multiply_reduce_fusion.2 = f32[64,128]{1,0:T(8,128)S(1)} fusion(f32[64,128,128]{2,1,0:T(8,128)S(1)} %copy-done.1, f32[64,128]{1,0:T(8,128)S(1)} %fusion.101), kind=kLoop, calls=%fused_computation.3 | loop fusion | flops 2088960 | bytes 4259840 | tf_op jit(solution)/shard_map/reduce_sum | solution.py:19
  58.8 1.2 %multiply_reduce_fusion.1 = f32[64,128]{1,0:T(8,128)S(1)} fusion(f32[64,128,128]{2,1,0:T(8,128)S(1)} %copy-done.1, f32[64,128]{1,0:T(8,128)S(1)} %bitcast.610), kind=kLoop, calls=%fused_computation.2 | loop fusion | flops 2088960 | bytes 4259840 | tf_op jit(solution)/shard_map/reduce_sum | solution.py:19
  60.1 2.5 %multiply_reduce_fusion.6 = (f32[32,128]{1,0:T(8,128)S(1)}, f32[32,128,128]{2,1,0:T(8,128)S(1)}) fusion(f32[32,128]{1,0:T(8,128)S(1)} %bitcast.627, f32[32,2,128,128]{3,2,1,0:T(8,128)S(1)} %bitcast.541), kind=kOutput, calls=%fused_computation.17 | convolution fusion | flops 806350848 | bytes 6324224 | tf_op jit(solution)/shard_map/dot_general | solution.py:11
  62.7 1.4 %multiply_reduce_fusion.8 = (f32[16,128]{1,0:T(8,128)S(1)}, f32[16,128,128]{2,1,0:T(8,128)S(1)}) fusion(f32[16,128]{1,0:T(8,128)S(1)} %bitcast.647, f32[16,2,128,128]{3,2,1,0:T(8,128)S(1)} %bitcast.547), kind=kOutput, calls=%fused_computation.30 | convolution fusion | flops 403175424 | bytes 3162112 | tf_op jit(solution)/shard_map/dot_general | solution.py:11
  64.1 0.8 multiply_reduce_fusion.10
  66.4 9.9 %all-gather.3 = f32[8,129,128]{2,1,0:T(8,128)S(1)} all-gather(f32[1,129,128]{2,1,0:T(8,128)S(1)} %maximum_bitcast_fusion.1), channel_id=3, replica_groups=mesh['outer'=4,'inner'=8] {'inner'}, dimensions={0}, use_global_device_ids=true | all-gather | bytes 594432 | tf_op jit(solution)/shard_map/all_gather | solution.py:120
  77.8 2.5 %collective-permute-start.5 = (f32[129,128]{1,0:T(8,128)S(1)}, f32[129,128]{1,0:T(8,128)S(1)}, u32[]{:S(2)}, u32[]{:S(2)}) collective-permute-start(f32[129,128]{1,0:T(8,128)S(1)} %pad_maximum_fusion.1), channel_id=1, source_target_pairs={{0,8},{8,16},{16,24},{24,0},{1,9},{9,17},{17,25},{25,1},{2,10},{10... | collective-permute-start | bytes 198152 | tf_op jit(solution)/shard_map/ppermute | solution.py:114
  80.3 0.9 collective-permute-start.4
  81.2 1.5 %collective-permute-start.3 = (f32[129,128]{1,0:T(8,128)S(1)}, f32[129,128]{1,0:T(8,128)S(1)}, u32[]{:S(2)}, u32[]{:S(2)}) collective-permute-start(f32[129,128]{1,0:T(8,128)S(1)} %pad_maximum_fusion.1), channel_id=1, source_target_pairs={{0,24},{8,0},{16,8},{24,16},{1,25},{9,1},{17,9},{25,17},{2,26},{10... | collective-permute-start | bytes 198152 | tf_op jit(solution)/shard_map/ppermute | solution.py:114
  84.7 2.5 %collective-permute-done.4 = f32[129,128]{1,0:T(8,128)S(1)} collective-permute-done((f32[129,128]{1,0:T(8,128)S(1)}, f32[129,128]{1,0:T(8,128)S(1)}, u32[]{:S(2)}, u32[]{:S(2)}) %collective-permute-start.4) | collective-permute-done | bytes 66080 | tf_op jit(solution)/shard_map/ppermute | solution.py:114
  89.6 1.2 %multiply_reduce_fusion = f32[64,128]{1,0:T(8,128)S(1)} fusion(f32[64,128,128]{2,1,0:T(8,128)S(1)} %copy-done.1, f32[64,128]{1,0:T(8,128)S(1)} %bitcast.611), kind=kLoop, calls=%fused_computation.1 | loop fusion | flops 2088960 | bytes 4259840 | tf_op jit(solution)/shard_map/reduce_sum | solution.py:19
  (183 shorter events, 18.0 us)
Async XLA Ops:
  0.6 4.5 %copy-start = (f32[128,128]{1,0:T(8,128)S(1)}, f32[128,128]{1,0:T(8,128)}, u32[]{:S(2)}) copy-start(f32[128,128]{1,0:T(8,128)} %param.10) | copy-start | bytes 196612
  0.6 4.7 %copy-start.4 = (f32[64,128,128]{2,1,0:T(8,128)S(1)}, f32[64,128,128]{2,1,0:T(8,128)}, u32[]{:S(2)}) copy-start(f32[64,128,128]{2,1,0:T(8,128)} %param.7) | copy-start | bytes 12582916
  0.7 4.5 %copy-start.7 = (f32[128,128]{1,0:T(8,128)S(1)}, f32[128,128]{1,0:T(8,128)}, u32[]{:S(2)}) copy-start(f32[128,128]{1,0:T(8,128)} %param.9) | copy-start | bytes 196612
  9.5 4.2 %copy-start.2 = (f32[64,128,128]{2,1,0:T(8,128)}, f32[64,128,128]{2,1,0:T(8,128)S(1)}, u32[]{:S(2)}) copy-start(f32[64,128,128]{2,1,0:T(8,128)S(1)} %get-tuple-element.47) | copy-start | bytes 12582916
  14.5 0.8 copy-start.5
  16.2 0.7 copy-start.6
  34.3 9.8 %collective-permute-start.2 = (f32[129,128]{1,0:T(8,128)}, f32[129,128]{1,0:T(8,128)}, u32[]{:S(2)}, u32[]{:S(2)}) collective-permute-start(f32[129,128]{1,0:T(8,128)} %pad_maximum_fusion), channel_id=1, source_target_pairs={{0,24},{8,0},{16,8},{24,16},{1,25},{9,1},{17,9},{25,17},{2,26},{10... | collective-permute-start | bytes 198152 | tf_op jit(solution)/shard_map/ppermute | solution.py:114
  37.9 8.2 %collective-permute-start.1 = (f32[129,128]{1,0:T(8,128)}, f32[129,128]{1,0:T(8,128)}, u32[]{:S(2)}, u32[]{:S(2)}) collective-permute-start(f32[129,128]{1,0:T(8,128)} %pad_maximum_fusion), channel_id=1, source_target_pairs={{0,16},{8,24},{16,0},{24,8},{1,17},{9,25},{17,1},{25,9},{2,18},{10... | collective-permute-start | bytes 198152 | tf_op jit(solution)/shard_map/ppermute | solution.py:114
  37.9 9.8 %collective-permute-start = (f32[129,128]{1,0:T(8,128)}, f32[129,128]{1,0:T(8,128)}, u32[]{:S(2)}, u32[]{:S(2)}) collective-permute-start(f32[129,128]{1,0:T(8,128)} %pad_maximum_fusion), channel_id=1, source_target_pairs={{0,8},{8,16},{16,24},{24,0},{1,9},{9,17},{17,25},{25,1},{2,10},{10... | collective-permute-start | bytes 198152 | tf_op jit(solution)/shard_map/ppermute | solution.py:114
  44.1 12.0 %copy-start.3 = (f32[64,128,128]{2,1,0:T(8,128)S(1)}, f32[64,128,128]{2,1,0:T(8,128)}, u32[]{:S(2)}) copy-start(f32[64,128,128]{2,1,0:T(8,128)} %copy-done.2) | copy-start | bytes 12582916
  52.8 4.5 %copy-start.8 = (f32[128,128]{1,0:T(8,128)S(1)}, f32[128,128]{1,0:T(8,128)}, u32[]{:S(2)}) copy-start(f32[128,128]{1,0:T(8,128)} %param.9) | copy-start | bytes 196612
  52.8 4.7 %copy-start.1 = (f32[64,128,128]{2,1,0:T(8,128)S(1)}, f32[64,128,128]{2,1,0:T(8,128)}, u32[]{:S(2)}) copy-start(f32[64,128,128]{2,1,0:T(8,128)} %param.8) | copy-start | bytes 12582916
  57.3 33.5 %copy-start.10 = (f32[64,128]{1,0:T(8,128)}, f32[64,128]{1,0:T(8,128)S(1)}, u32[]{:S(2)}) copy-start(f32[64,128]{1,0:T(8,128)S(1)} %add.356) | copy-start | bytes 98308
  62.6 13.7 %copy-start.9 = (f32[128,128]{1,0:T(8,128)S(1)}, f32[128,128]{1,0:T(8,128)}, u32[]{:S(2)}) copy-start(f32[128,128]{1,0:T(8,128)} %fusion.60) | copy-start | bytes 196612
  62.6 13.7 %copy-start.11 = (pred[8]{0:T(512)(128)(4,1)S(1)}, pred[8]{0:T(512)(128)(4,1)}, u32[]{:S(2)}) copy-start(pred[8]{0:T(512)(128)(4,1)} %iota_compare_fusion.1) | copy-start | bytes 28
  77.8 6.8 %collective-permute-start.5 = (f32[129,128]{1,0:T(8,128)S(1)}, f32[129,128]{1,0:T(8,128)S(1)}, u32[]{:S(2)}, u32[]{:S(2)}) collective-permute-start(f32[129,128]{1,0:T(8,128)S(1)} %pad_maximum_fusion.1), channel_id=1, source_target_pairs={{0,8},{8,16},{16,24},{24,0},{1,9},{9,17},{17,25},{25,1},{2,10},{10... | collective-permute-start | bytes 198152 | tf_op jit(solution)/shard_map/ppermute | solution.py:114
  80.3 6.8 %collective-permute-start.4 = (f32[129,128]{1,0:T(8,128)S(1)}, f32[129,128]{1,0:T(8,128)S(1)}, u32[]{:S(2)}, u32[]{:S(2)}) collective-permute-start(f32[129,128]{1,0:T(8,128)S(1)} %pad_maximum_fusion.1), channel_id=1, source_target_pairs={{0,16},{8,24},{16,0},{24,8},{1,17},{9,25},{17,1},{25,9},{2,18},{10... | collective-permute-start | bytes 198152 | tf_op jit(solution)/shard_map/ppermute | solution.py:114
  81.2 6.1 %collective-permute-start.3 = (f32[129,128]{1,0:T(8,128)S(1)}, f32[129,128]{1,0:T(8,128)S(1)}, u32[]{:S(2)}, u32[]{:S(2)}) collective-permute-start(f32[129,128]{1,0:T(8,128)S(1)} %pad_maximum_fusion.1), channel_id=1, source_target_pairs={{0,24},{8,0},{16,8},{24,16},{1,25},{9,1},{17,9},{25,17},{2,26},{10... | collective-permute-start | bytes 198152 | tf_op jit(solution)/shard_map/ppermute | solution.py:114

commit v12 on v9

--- a/solution.py
+++ b/solution.py
@@ -141,9 +141,7 @@
     entry_state = across(fm, fv, initial_mean, False)
     filtered = spread(forward, entry_state, False)
 
-    predicted_all = jnp.dot(
-        filtered, transition.T, precision=exact, preferred_element_type=jnp.float32
-    )
+    predicted_all = mv_whole(transition[None], filtered)
     offsets = filtered - mv_whole(smoother_gains, predicted_all)
     backward = local_tiers(smoother_gains, offsets, True)
     bm, bv = backward[-1][0][0], backward[-1][1][0]

time: 87 us -> 87.9 us (1.010)
  other arithmetic: 24.2 us -> 25.3 us
    reduce_sum x25 -> x26, other arithmetic: 19.1 us -> 20.2 us  [mv_whole(): return jnp.sum(a * v[..., None, :], axis=-1)]
where the time goes in v12:
time: 87.9 us; the launch traced here: 87.5 us
  other arithmetic  25.3 us (29%)
  matrix products  24 us (27%)
  blocking collectives  21.6 us (25%)
  starting transfers between devices  8.78 us (10%)
  waiting for transfers between devices  4.94 us (6%)
  between operations  1.86 us (2%)
  local copies, waits for them, and re-layouts  1.04 us (1%)
    all_gather x2, blocking collectives, across(): gathered = lax.all_gather(pack(mat, vec), 'inner')  21.6 us
    reduce_sum x26, other arithmetic, mv_whole(): return jnp.sum(a * v[..., None, :], axis=-1)  20.2 us
    dot_general x25, matrix products, mm(): return jnp.matmul(a, b, precision=exact, preferred_element_type=jnp.float32)  19.9 us
    ppermute x6, starting transfers between devices, from_other_groups(): received.append(lax.ppermute(packed, 'outer', pairs))  8.78 us
    ppermute x6, waiting for transfers between devices, from_other_groups(): received.append(lax.ppermute(packed, 'outer', pairs))  4.94 us
    dot_general x1, matrix products, on_device(): jnp.einsum('tij,jk->tik', gains, mapped, precision=exact, preferred_eleme...  4.06 us
    mul x14, other arithmetic, mv_whole(): return jnp.sum(a * v[..., None, :], axis=-1)  2.34 us
  transfers between devices with their start and end apart: 6, of which 3 were waited for; matrix products, arithmetic and copies ran while one was open for 10% of the time, Pallas kernels for 0%

profile of v12, /device:TPU:0, one launch (start us, length us, event | category | flops | bytes accessed | tf_op | source)
XLA Modules:
  0.0 87.5 jit_solution(14018284828299373195)
XLA Ops:
  0.7 3.5 %multiply_reduce_fusion.6 = f32[64,128]{1,0:T(8,128)S(1)} fusion(f32[64,128,128]{2,1,0:T(8,128)} %param.7, f32[64,128]{1,0:T(8,128)} %param.6), kind=kLoop, calls=%fused_computation.7 | loop fusion | flops 2088960 | bytes 4259840 | tf_op jit(solution)/shard_map/reduce_sum | solution.py:19
  4.5 4.1 %multiply_reduce_fusion.5 = (f32[64,128]{1,0:T(8,128)S(1)}, f32[64,128,128]{2,1,0:T(8,128)S(1)}) fusion(f32[64,128]{1,0:T(8,128)S(1)} %bitcast.592, f32[128,128,1]{1,0,2:T(8,128)S(1)} %convolution_bitcast_fusion, f32[64,128,128]{2,1,0:T(8,128)S(1)} %copy-done.4, f32[128,128]{1,0:T(8,128)S(1)} %copy-done.7), kind=kOutput, calls=%fused_computation.6 | convolution fusion | flops 1613750272 | bytes 8585216 | tf_op jit(solution)/shard_map/tij,jk->tik/dot_general | solution.py:135
  8.7 2.6 %multiply_reduce_fusion.8 = (f32[32,128]{1,0:T(8,128)S(1)}, f32[32,128,128]{2,1,0:T(8,128)S(1)}) fusion(f32[32,128]{1,0:T(8,128)S(1)} %bitcast.610, f32[32,2,128,128]{3,2,1,0:T(8,128)S(1)} %bitcast.539), kind=kOutput, calls=%fused_computation.19 | convolution fusion | flops 806350848 | bytes 6324224 | tf_op jit(solution)/shard_map/dot_general | solution.py:11
  11.4 1.4 %multiply_reduce_fusion.10 = (f32[16,128]{1,0:T(8,128)S(1)}, f32[16,128,128]{2,1,0:T(8,128)S(1)}) fusion(f32[16,128]{1,0:T(8,128)S(1)} %bitcast.632, f32[16,2,128,128]{3,2,1,0:T(8,128)S(1)} %bitcast.541), kind=kOutput, calls=%fused_computation.32 | convolution fusion | flops 403175424 | bytes 3162112 | tf_op jit(solution)/shard_map/dot_general | solution.py:11
  15.6 11.6 %all-gather.2 = f32[8,129,128]{2,1,0:T(8,128)S(1)} all-gather(f32[1,129,128]{2,1,0:T(8,128)S(1)} %maximum_bitcast_fusion), channel_id=2, replica_groups=mesh['outer'=4,'inner'=8] {'inner'}, dimensions={0}, use_global_device_ids=true | all-gather | bytes 594432 | tf_op jit(solution)/shard_map/all_gather | solution.py:116
  29.7 3.6 %collective-permute-start.2 = (f32[129,128]{1,0:T(8,128)}, f32[129,128]{1,0:T(8,128)}, u32[]{:S(2)}, u32[]{:S(2)}) collective-permute-start(f32[129,128]{1,0:T(8,128)} %pad_maximum_fusion), channel_id=1, source_target_pairs={{0,24},{8,0},{16,8},{24,16},{1,25},{9,1},{17,9},{25,17},{2,26},{10... | collective-permute-start | bytes 198152 | tf_op jit(solution)/shard_map/ppermute | solution.py:110
  33.3 1.0 %collective-permute-start = (f32[129,128]{1,0:T(8,128)}, f32[129,128]{1,0:T(8,128)}, u32[]{:S(2)}, u32[]{:S(2)}) collective-permute-start(f32[129,128]{1,0:T(8,128)} %pad_maximum_fusion), channel_id=1, source_target_pairs={{0,8},{8,16},{16,24},{24,0},{1,9},{9,17},{17,25},{25,1},{2,10},{10... | collective-permute-start | bytes 198152 | tf_op jit(solution)/shard_map/ppermute | solution.py:110
  34.9 1.3 %multiply_reduce_fusion.20 = (f32[4,128]{1,0:T(4,128)S(1)}, f32[4,128,128]{1,2,0:T(8,128)}) fusion(f32[4,128]{1,0:T(4,128)S(1)} %bitcast.673, f32[4,2,128,128]{3,2,1,0:T(8,128)S(1)} %bitcast.553), kind=kOutput, calls=%fused_computation.74 | convolution fusion | flops 100793856 | bytes 790528 | tf_op jit(solution)/shard_map/dot_general | solution.py:11
  36.3 1.9 %multiply_reduce_fusion.26 = (f32[2,128]{1,0:T(2,128)S(1)}, f32[2,128,128]{1,2,0:T(8,128)}) fusion(f32[2,128]{1,0:T(2,128)S(1)} %maximum_bitcast_fusion.4, f32[2,2,128,128]{2,3,1,0:T(8,128)} %bitcast.561), kind=kOutput, calls=%fused_computation.110 | convolution fusion | flops 50396928 | bytes 395264 | tf_op jit(solution)/shard_map/dot_general | solution.py:11
  38.2 1.1 %fusion.33 = f32[128]{0:T(128)S(1)} fusion(f32[129,128]{1,0:T(8,128)} %collective-permute-done.2, f32[128]{0:T(128)} %param.11, pred[]{:T(512)S(6)} %ge.11), kind=kLoop, calls=%fused_computation.122 | loop fusion | flops 81792 | bytes 66561 | tf_op jit(solution)/shard_map/reduce_sum | solution.py:19
  39.3 0.9 fusion.52
  40.2 0.8 collective-permute-done.1
  41.0 0.9 %fusion.31 = f32[128]{0:T(128)S(1)} fusion(f32[129,128]{1,0:T(8,128)} %collective-permute-done.1, f32[128]{0:T(128)S(1)} %fusion.52, pred[]{:T(512)S(6)} %ge.10), kind=kLoop, calls=%fused_computation.120 | loop fusion | flops 81792 | bytes 66561 | tf_op jit(solution)/shard_map/reduce_sum | solution.py:19
  42.6 0.9 %fusion.29 = f32[128]{0:T(128)S(1)} fusion(f32[129,128]{1,0:T(8,128)} %collective-permute-done, f32[128]{0:T(128)S(1)} %fusion.54, pred[]{:T(512)S(6)} %ge.9), kind=kLoop, calls=%fused_computation.118 | loop fusion | flops 81792 | bytes 66561 | tf_op jit(solution)/shard_map/reduce_sum | solution.py:19
  44.3 1.1 %multiply_reduce_fusion.31 = f32[128]{0:T(128)S(1)} fusion(f32[128]{0:T(128)S(1)} %fusion.56, f32[1,2,128,128]{2,3,1,0:T(8,128)} %bitcast.573), kind=kOutput, calls=%fused_computation.153 | convolution fusion | flops 25198464 | bytes 132096 | tf_op jit(solution)/shard_map/dot_general | solution.py:11
  45.4 0.9 %fusion.44 = f32[128]{0:T(128)S(1)} fusion(f32[1,256,128]{2,1,0:T(8,128)} %bitcast.570, f32[128]{0:T(128)S(1)} %bitcast.690), kind=kLoop, calls=%fused_computation.141 | loop fusion | flops 32640 | bytes 66560 | tf_op jit(solution)/shard_map/reduce_sum | solution.py:19
  46.5 1.1 %fusion.16 = f32[4,128]{1,0:T(4,128)S(1)} fusion(f32[4,256,128]{2,1,0:T(8,128)} %bitcast.550, f32[4,128]{1,0:T(4,128)S(1)} %bitcast.636), kind=kLoop, calls=%fused_computation.61 | loop fusion | flops 130560 | bytes 266240 | tf_op jit(solution)/shard_map/reduce_sum | solution.py:19
  48.3 2.5 %fusion.2 = f32[32,128]{1,0:T(8,128)S(1)} fusion(f32[32,256,128]{2,1,0:T(8,128)} %bitcast.540, f32[32,128]{1,0:T(8,128)S(1)} %bitcast.584), kind=kLoop, calls=%fused_computation.14 | loop fusion | flops 1044480 | bytes 2129920 | tf_op jit(solution)/shard_map/reduce_sum | solution.py:19
  50.9 1.2 %multiply_reduce_fusion.4 = f32[64,128]{1,0:T(8,128)S(1)} fusion(f32[64,128,128]{2,1,0:T(8,128)S(1)} %copy-done.3, f32[64,128]{1,0:T(8,128)S(1)} %bitcast.593), kind=kLoop, calls=%fused_computation.5 | loop fusion | flops 2088960 | bytes 4259840 | tf_op jit(solution)/shard_map/reduce_sum | solution.py:19
  52.1 1.1 %multiply_reduce_fusion.3 = f32[64,128]{1,0:T(8,128)S(1)} fusion(f32[64,128]{1,0:T(8,128)S(1)} %add.395, f32[128,128]{1,0:T(8,128)S(1)} %copy-done.8), kind=kLoop, calls=%fused_computation.4 | loop fusion | flops 2088960 | bytes 131072 | tf_op jit(solution)/shard_map/reduce_sum | solution.py:19
  53.3 1.2 %multiply_reduce_fusion.2 = f32[64,128]{1,0:T(8,128)S(1)} fusion(f32[64,128,128]{2,1,0:T(8,128)S(1)} %copy-done.1, f32[64,128]{1,0:T(8,128)S(1)} %multiply_reduce_fusion.3), kind=kLoop, calls=%fused_computation.3 | loop fusion | flops 2088960 | bytes 4259840 | tf_op jit(solution)/shard_map/reduce_sum | solution.py:19
  54.5 1.2 %multiply_reduce_fusion.1 = f32[64,128]{1,0:T(8,128)S(1)} fusion(f32[64,128,128]{2,1,0:T(8,128)S(1)} %copy-done.1, f32[64,128]{1,0:T(8,128)S(1)} %bitcast.594), kind=kLoop, calls=%fused_computation.2 | loop fusion | flops 2088960 | bytes 4259840 | tf_op jit(solution)/shard_map/reduce_sum | solution.py:19
  55.8 2.5 %multiply_reduce_fusion.7 = (f32[32,128]{1,0:T(8,128)S(1)}, f32[32,128,128]{2,1,0:T(8,128)S(1)}) fusion(f32[32,128]{1,0:T(8,128)S(1)} %bitcast.611, f32[32,2,128,128]{3,2,1,0:T(8,128)S(1)} %bitcast.537), kind=kOutput, calls=%fused_computation.18 | convolution fusion | flops 806350848 | bytes 6324224 | tf_op jit(solution)/shard_map/dot_general | solution.py:11
  58.4 1.4 %multiply_reduce_fusion.9 = (f32[16,128]{1,0:T(8,128)S(1)}, f32[16,128,128]{2,1,0:T(8,128)S(1)}) fusion(f32[16,128]{1,0:T(8,128)S(1)} %bitcast.633, f32[16,2,128,128]{3,2,1,0:T(8,128)S(1)} %bitcast.543), kind=kOutput, calls=%fused_computation.31 | convolution fusion | flops 403175424 | bytes 3162112 | tf_op jit(solution)/shard_map/dot_general | solution.py:11
  59.8 1.0 %multiply_reduce_fusion.13 = (f32[8,128]{1,0:T(8,128)S(1)}, f32[8,128,128]{2,1,0:T(8,128)S(1)}) fusion(f32[8,128]{1,0:T(8,128)S(1)} %bitcast.647, f32[8,2,128,128]{3,2,1,0:T(8,128)S(1)} %bitcast.547), kind=kOutput, calls=%fused_computation.45 | convolution fusion | flops 201587712 | bytes 1581056 | tf_op jit(solution)/shard_map/dot_general | solution.py:11
  62.2 10.0 %all-gather.3 = f32[8,129,128]{2,1,0:T(8,128)S(1)} all-gather(f32[1,129,128]{2,1,0:T(8,128)S(1)} %maximum_bitcast_fusion.1), channel_id=3, replica_groups=mesh['outer'=4,'inner'=8] {'inner'}, dimensions={0}, use_global_device_ids=true | all-gather | bytes 594432 | tf_op jit(solution)/shard_map/all_gather | solution.py:116
  74.0 1.7 %collective-permute-start.5 = (f32[129,128]{1,0:T(8,128)S(1)}, f32[129,128]{1,0:T(8,128)S(1)}, u32[]{:S(2)}, u32[]{:S(2)}) collective-permute-start(f32[129,128]{1,0:T(8,128)S(1)} %pad_maximum_fusion.1), channel_id=1, source_target_pairs={{0,8},{8,16},{16,24},{24,0},{1,9},{9,17},{17,25},{25,1},{2,10},{10... | collective-permute-start | bytes 198152 | tf_op jit(solution)/shard_map/ppermute | solution.py:110
  75.7 0.9 %collective-permute-start.4 = (f32[129,128]{1,0:T(8,128)S(1)}, f32[129,128]{1,0:T(8,128)S(1)}, u32[]{:S(2)}, u32[]{:S(2)}) collective-permute-start(f32[129,128]{1,0:T(8,128)S(1)} %pad_maximum_fusion.1), channel_id=1, source_target_pairs={{0,16},{8,24},{16,0},{24,8},{1,17},{9,25},{17,1},{25,9},{2,18},{10... | collective-permute-start | bytes 198152 | tf_op jit(solution)/shard_map/ppermute | solution.py:110
  76.6 1.5 %collective-permute-start.3 = (f32[129,128]{1,0:T(8,128)S(1)}, f32[129,128]{1,0:T(8,128)S(1)}, u32[]{:S(2)}, u32[]{:S(2)}) collective-permute-start(f32[129,128]{1,0:T(8,128)S(1)} %pad_maximum_fusion.1), channel_id=1, source_target_pairs={{0,24},{8,0},{16,8},{24,16},{1,25},{9,1},{17,9},{25,17},{2,26},{10... | collective-permute-start | bytes 198152 | tf_op jit(solution)/shard_map/ppermute | solution.py:110
  79.1 1.8 %collective-permute-done.5 = f32[129,128]{1,0:T(8,128)S(1)} collective-permute-done((f32[129,128]{1,0:T(8,128)S(1)}, f32[129,128]{1,0:T(8,128)S(1)}, u32[]{:S(2)}, u32[]{:S(2)}) %collective-permute-start.5) | collective-permute-done | bytes 66080 | tf_op jit(solution)/shard_map/ppermute | solution.py:110
  81.1 2.3 %collective-permute-done.4 = f32[129,128]{1,0:T(8,128)S(1)} collective-permute-done((f32[129,128]{1,0:T(8,128)S(1)}, f32[129,128]{1,0:T(8,128)S(1)}, u32[]{:S(2)}, u32[]{:S(2)}) %collective-permute-start.4) | collective-permute-done | bytes 66080 | tf_op jit(solution)/shard_map/ppermute | solution.py:110
  85.7 1.2 %multiply_reduce_fusion = f32[64,128]{1,0:T(8,128)S(1)} fusion(f32[64,128,128]{2,1,0:T(8,128)S(1)} %copy-done.1, f32[64,128]{1,0:T(8,128)S(1)} %bitcast.595), kind=kLoop, calls=%fused_computation.1 | loop fusion | flops 2088960 | bytes 4259840 | tf_op jit(solution)/shard_map/reduce_sum | solution.py:19
  (187 shorter events, 15.4 us)
Async XLA Ops:
  0.6 3.7 %copy-start = (f32[128,128]{1,0:T(8,128)S(1)}, f32[128,128]{1,0:T(8,128)}, u32[]{:S(2)}) copy-start(f32[128,128]{1,0:T(8,128)} %param.10) | copy-start | bytes 196612
  0.6 3.7 %copy-start.7 = (f32[128,128]{1,0:T(8,128)S(1)}, f32[128,128]{1,0:T(8,128)}, u32[]{:S(2)}) copy-start(f32[128,128]{1,0:T(8,128)} %param.9) | copy-start | bytes 196612
  0.7 3.9 %copy-start.4 = (f32[64,128,128]{2,1,0:T(8,128)S(1)}, f32[64,128,128]{2,1,0:T(8,128)}, u32[]{:S(2)}) copy-start(f32[64,128,128]{2,1,0:T(8,128)} %param.7) | copy-start | bytes 12582916
  0.7 26.6 %copy-start.9 = (f32[128,128]{1,0:T(8,128)}, f32[128,128]{1,0:T(8,128)S(1)}, u32[]{:S(2)}) copy-start(f32[128,128]{1,0:T(8,128)S(1)} %fusion.48) | copy-start | bytes 196612
  8.6 4.2 %copy-start.2 = (f32[64,128,128]{2,1,0:T(8,128)}, f32[64,128,128]{2,1,0:T(8,128)S(1)}, u32[]{:S(2)}) copy-start(f32[64,128,128]{2,1,0:T(8,128)S(1)} %get-tuple-element.63) | copy-start | bytes 12582916
  13.6 0.8 copy-start.5
  15.3 12.0 %copy-start.6 = (f32[2,128,128]{2,1,0:T(8,128)}, f32[2,128,128]{2,1,0:T(8,128)S(1)}, u32[]{:S(2)}) copy-start(f32[2,128,128]{2,1,0:T(8,128)S(1)} %get-tuple-element.73) | copy-start | bytes 393220
  29.7 8.5 %collective-permute-start.2 = (f32[129,128]{1,0:T(8,128)}, f32[129,128]{1,0:T(8,128)}, u32[]{:S(2)}, u32[]{:S(2)}) collective-permute-start(f32[129,128]{1,0:T(8,128)} %pad_maximum_fusion), channel_id=1, source_target_pairs={{0,24},{8,0},{16,8},{24,16},{1,25},{9,1},{17,9},{25,17},{2,26},{10... | collective-permute-start | bytes 198152 | tf_op jit(solution)/shard_map/ppermute | solution.py:110
  33.3 7.7 %collective-permute-start.1 = (f32[129,128]{1,0:T(8,128)}, f32[129,128]{1,0:T(8,128)}, u32[]{:S(2)}, u32[]{:S(2)}) collective-permute-start(f32[129,128]{1,0:T(8,128)} %pad_maximum_fusion), channel_id=1, source_target_pairs={{0,16},{8,24},{16,0},{24,8},{1,17},{9,25},{17,1},{25,9},{2,18},{10... | collective-permute-start | bytes 198152 | tf_op jit(solution)/shard_map/ppermute | solution.py:110
  33.3 9.3 %collective-permute-start = (f32[129,128]{1,0:T(8,128)}, f32[129,128]{1,0:T(8,128)}, u32[]{:S(2)}, u32[]{:S(2)}) collective-permute-start(f32[129,128]{1,0:T(8,128)} %pad_maximum_fusion), channel_id=1, source_target_pairs={{0,8},{8,16},{16,24},{24,0},{1,9},{9,17},{17,25},{25,1},{2,10},{10... | collective-permute-start | bytes 198152 | tf_op jit(solution)/shard_map/ppermute | solution.py:110
  38.2 12.8 %copy-start.3 = (f32[64,128,128]{2,1,0:T(8,128)S(1)}, f32[64,128,128]{2,1,0:T(8,128)}, u32[]{:S(2)}) copy-start(f32[64,128,128]{2,1,0:T(8,128)} %copy-done.2) | copy-start | bytes 12582916
  47.6 4.5 %copy-start.8 = (f32[128,128]{1,0:T(8,128)S(1)}, f32[128,128]{1,0:T(8,128)}, u32[]{:S(2)}) copy-start(f32[128,128]{1,0:T(8,128)} %param.9) | copy-start | bytes 196612
  47.6 5.6 %copy-start.1 = (f32[64,128,128]{2,1,0:T(8,128)S(1)}, f32[64,128,128]{2,1,0:T(8,128)}, u32[]{:S(2)}) copy-start(f32[64,128,128]{2,1,0:T(8,128)} %param.8) | copy-start | bytes 12582916
  52.1 34.7 %copy-start.11 = (f32[64,128]{1,0:T(8,128)}, f32[64,128]{1,0:T(8,128)S(1)}, u32[]{:S(2)}) copy-start(f32[64,128]{1,0:T(8,128)S(1)} %add.395) | copy-start | bytes 98308
  58.3 13.8 %copy-start.12 = (pred[4,2]{1,0:T(4,128)(4,1)S(1)}, pred[4,2]{1,0:T(4,128)(4,1)}, u32[]{:S(2)}) copy-start(pred[4,2]{1,0:T(4,128)(4,1)} %fusion.49) | copy-start | bytes 28
  58.3 13.9 %copy-start.10 = (f32[128,128]{1,0:T(8,128)S(1)}, f32[128,128]{1,0:T(8,128)}, u32[]{:S(2)}) copy-start(f32[128,128]{1,0:T(8,128)} %copy-done.9) | copy-start | bytes 196612
  74.0 7.0 %collective-permute-start.5 = (f32[129,128]{1,0:T(8,128)S(1)}, f32[129,128]{1,0:T(8,128)S(1)}, u32[]{:S(2)}, u32[]{:S(2)}) collective-permute-start(f32[129,128]{1,0:T(8,128)S(1)} %pad_maximum_fusion.1), channel_id=1, source_target_pairs={{0,8},{8,16},{16,24},{24,0},{1,9},{9,17},{17,25},{25,1},{2,10},{10... | collective-permute-start | bytes 198152 | tf_op jit(solution)/shard_map/ppermute | solution.py:110
  75.7 7.6 %collective-permute-start.4 = (f32[129,128]{1,0:T(8,128)S(1)}, f32[129,128]{1,0:T(8,128)S(1)}, u32[]{:S(2)}, u32[]{:S(2)}) collective-permute-start(f32[129,128]{1,0:T(8,128)S(1)} %pad_maximum_fusion.1), channel_id=1, source_target_pairs={{0,16},{8,24},{16,0},{24,8},{1,17},{9,25},{17,1},{25,9},{2,18},{10... | collective-permute-start | bytes 198152 | tf_op jit(solution)/shard_map/ppermute | solution.py:110
  76.6 6.8 %collective-permute-start.3 = (f32[129,128]{1,0:T(8,128)S(1)}, f32[129,128]{1,0:T(8,128)S(1)}, u32[]{:S(2)}, u32[]{:S(2)}) collective-permute-start(f32[129,128]{1,0:T(8,128)S(1)} %pad_maximum_fusion.1), channel_id=1, source_target_pairs={{0,24},{8,0},{16,8},{24,16},{1,25},{9,1},{17,9},{25,17},{2,26},{10... | collective-permute-start | bytes 198152 | tf_op jit(solution)/shard_map/ppermute | solution.py:110

commit v13 on v9

--- a/solution.py
+++ b/solution.py
@@ -145,12 +145,11 @@
         filtered, transition.T, precision=exact, preferred_element_type=jnp.float32
     )
     offsets = filtered - mv_whole(smoother_gains, predicted_all)
+    final = (me == devices - 1) & (jnp.arange(offsets.shape[0]) == offsets.shape[0] - 1)
+    offsets = jnp.where(final[:, None], filtered, offsets)
     backward = local_tiers(smoother_gains, offsets, True)
     bm, bv = backward[-1][0][0], backward[-1][1][0]
-    last = me == devices - 1
-    extra = jnp.where(last, predicted_all[-1], 0.0)
-    bv = bv + mv_whole(bm, extra)
-    after_state = across(bm, bv, jnp.zeros_like(extra), True) + extra
+    after_state = across(bm, bv, jnp.zeros_like(bv), True)
     smoothed = spread(backward, after_state, True)
     return (filtered, smoothed)
 

time: 87 us -> 87.7 us (level)
  other arithmetic: 24.2 us -> 25.9 us
  waiting for transfers between devices: 4.94 us -> 3.27 us
  matrix products: 24.2 us -> 22.8 us
  local copies, waits for them, and re-layouts: 1.04 us -> 2.3 us
    ppermute x6, waiting for transfers between devices: 4.94 us -> 3.27 us  [from_other_groups(): received.append(lax.ppermute(packed, 'outer', pairs))]
    dot_general x25, matrix products: 19.9 us -> 18.5 us  [mm(): return jnp.matmul(a, b, precision=exact, preferred_element_type=jnp.float32)]
    mul x14 -> x13, other arithmetic: 2.34 us -> 2.95 us  [mv_whole(): return jnp.sum(a * v[..., None, :], axis=-1)]
  transfers between devices with their start and end apart: 6 -> 6, of which waited for: 3 -> 2; matrix products, arithmetic and copies ran while one was open for 10% -> 12% of each run, Pallas kernels for 0% -> 0%
where the time goes in v13:
time: 87.7 us; the launch traced here: 87.3 us
  other arithmetic  25.9 us (30%)
  matrix products  22.8 us (26%)
  blocking collectives  21.6 us (25%)
  starting transfers between devices  9.63 us (11%)
  waiting for transfers between devices  3.27 us (4%)
  local copies, waits for them, and re-layouts  2.3 us (3%)
  between operations  1.86 us (2%)
    all_gather x2, blocking collectives, across(): gathered = lax.all_gather(pack(mat, vec), 'inner')  21.6 us
    reduce_sum x25, other arithmetic, mv_whole(): return jnp.sum(a * v[..., None, :], axis=-1)  18.9 us
    dot_general x25, matrix products, mm(): return jnp.matmul(a, b, precision=exact, preferred_element_type=jnp.float32)  18.5 us
    ppermute x6, starting transfers between devices, from_other_groups(): received.append(lax.ppermute(packed, 'outer', pairs))  9.63 us
    dot_general x1, matrix products, on_device(): jnp.einsum('tij,jk->tik', gains, mapped, precision=exact, preferred_eleme...  4.06 us
    ppermute x6, waiting for transfers between devices, from_other_groups(): received.append(lax.ppermute(packed, 'outer', pairs))  3.27 us
    mul x13, other arithmetic, mv_whole(): return jnp.sum(a * v[..., None, :], axis=-1)  2.95 us
  transfers between devices with their start and end apart: 6, of which 2 were waited for; matrix products, arithmetic and copies ran while one was open for 12% of the time, Pallas kernels for 0%

profile of v13, /device:TPU:0, one launch (start us, length us, event | category | flops | bytes accessed | tf_op | source)
XLA Modules:
  0.0 87.3 jit_solution(4352456474575360561)
XLA Ops:
  0.7 3.5 %multiply_reduce_fusion.5 = f32[64,128]{1,0:T(8,128)S(1)} fusion(f32[64,128,128]{2,1,0:T(8,128)} %param.7, f32[64,128]{1,0:T(8,128)} %param.6), kind=kLoop, calls=%fused_computation.6 | loop fusion | flops 2088960 | bytes 4259840 | tf_op jit(solution)/shard_map/reduce_sum | solution.py:19
  4.5 4.1 %multiply_reduce_fusion.4 = (f32[64,128]{1,0:T(8,128)S(1)}, f32[64,128,128]{2,1,0:T(8,128)S(1)}) fusion(f32[64,128]{1,0:T(8,128)S(1)} %bitcast.575, f32[128,128,1]{1,0,2:T(8,128)S(1)} %convolution_bitcast_fusion, f32[64,128,128]{2,1,0:T(8,128)S(1)} %copy-done.4, f32[128,128]{1,0:T(8,128)S(1)} %copy-done.7), kind=kOutput, calls=%fused_computation.5 | convolution fusion | flops 1613750272 | bytes 8585216 | tf_op jit(solution)/shard_map/tij,jk->tik/dot_general | solution.py:135
  8.7 2.6 %multiply_reduce_fusion.7 = (f32[32,128]{1,0:T(8,128)S(1)}, f32[32,128,128]{2,1,0:T(8,128)S(1)}) fusion(f32[32,128]{1,0:T(8,128)S(1)} %bitcast.593, f32[32,2,128,128]{3,2,1,0:T(8,128)S(1)} %bitcast.525), kind=kOutput, calls=%fused_computation.18 | convolution fusion | flops 806350848 | bytes 6324224 | tf_op jit(solution)/shard_map/dot_general | solution.py:11
  11.4 1.4 %multiply_reduce_fusion.9 = (f32[16,128]{1,0:T(8,128)S(1)}, f32[16,128,128]{2,1,0:T(8,128)S(1)}) fusion(f32[16,128]{1,0:T(8,128)S(1)} %bitcast.615, f32[16,2,128,128]{3,2,1,0:T(8,128)S(1)} %bitcast.527), kind=kOutput, calls=%fused_computation.31 | convolution fusion | flops 403175424 | bytes 3162112 | tf_op jit(solution)/shard_map/dot_general | solution.py:11
  12.8 0.8 multiply_reduce_fusion.15
  13.7 0.7 copy-done.5
  15.6 11.6 %all-gather.2 = f32[8,129,128]{2,1,0:T(8,128)S(1)} all-gather(f32[1,129,128]{2,1,0:T(8,128)S(1)} %maximum_bitcast_fusion), channel_id=2, replica_groups=mesh['outer'=4,'inner'=8] {'inner'}, dimensions={0}, use_global_device_ids=true | all-gather | bytes 594432 | tf_op jit(solution)/shard_map/all_gather | solution.py:116
  29.7 3.6 %collective-permute-start.2 = (f32[129,128]{1,0:T(8,128)}, f32[129,128]{1,0:T(8,128)}, u32[]{:S(2)}, u32[]{:S(2)}) collective-permute-start(f32[129,128]{1,0:T(8,128)} %pad_maximum_fusion), channel_id=1, source_target_pairs={{0,24},{8,0},{16,8},{24,16},{1,25},{9,1},{17,9},{25,17},{2,26},{10... | collective-permute-start | bytes 198152 | tf_op jit(solution)/shard_map/ppermute | solution.py:110
  33.3 1.0 %collective-permute-start = (f32[129,128]{1,0:T(8,128)}, f32[129,128]{1,0:T(8,128)}, u32[]{:S(2)}, u32[]{:S(2)}) collective-permute-start(f32[129,128]{1,0:T(8,128)} %pad_maximum_fusion), channel_id=1, source_target_pairs={{0,8},{8,16},{16,24},{24,0},{1,9},{9,17},{17,25},{25,1},{2,10},{10... | collective-permute-start | bytes 198152 | tf_op jit(solution)/shard_map/ppermute | solution.py:110
  35.4 1.3 %multiply_reduce_fusion.19 = (f32[4,128]{1,0:T(4,128)S(1)}, f32[4,128,128]{1,2,0:T(8,128)}) fusion(f32[4,128]{1,0:T(4,128)S(1)} %bitcast.656, f32[4,2,128,128]{3,2,1,0:T(8,128)S(1)} %bitcast.539), kind=kOutput, calls=%fused_computation.73 | convolution fusion | flops 100793856 | bytes 790528 | tf_op jit(solution)/shard_map/dot_general | solution.py:11
  37.8 0.8 copy.491
  38.6 0.8 maximum_bitcast_fusion.4
  39.4 1.4 %multiply_reduce_fusion.25 = (f32[2,128]{1,0:T(2,128)S(1)}, f32[2,128,128]{1,2,0:T(8,128)S(1)}) fusion(f32[2,128]{1,0:T(2,128)S(1)} %maximum_bitcast_fusion.4, f32[2,2,128,128]{2,3,1,0:T(8,128)} %bitcast.547), kind=kOutput, calls=%fused_computation.109 | convolution fusion | flops 50396928 | bytes 395264 | tf_op jit(solution)/shard_map/dot_general | solution.py:11
  40.8 0.9 %fusion.33 = f32[128]{0:T(128)S(1)} fusion(f32[129,128]{1,0:T(8,128)} %collective-permute-done.2, f32[128]{0:T(128)} %param.11, pred[]{:T(512)S(6)} %ge.11), kind=kLoop, calls=%fused_computation.121 | loop fusion | flops 81792 | bytes 66561 | tf_op jit(solution)/shard_map/reduce_sum | solution.py:19
  42.5 0.9 %fusion.31 = f32[128]{0:T(128)S(1)} fusion(f32[129,128]{1,0:T(8,128)} %collective-permute-done.1, f32[128]{0:T(128)S(1)} %fusion.53, pred[]{:T(512)S(6)} %ge.10), kind=kLoop, calls=%fused_computation.119 | loop fusion | flops 81792 | bytes 66561 | tf_op jit(solution)/shard_map/reduce_sum | solution.py:19
  44.1 0.9 %fusion.29 = f32[128]{0:T(128)S(1)} fusion(f32[129,128]{1,0:T(8,128)} %collective-permute-done, f32[128]{0:T(128)S(1)} %fusion.55, pred[]{:T(512)S(6)} %ge.9), kind=kLoop, calls=%fused_computation.117 | loop fusion | flops 81792 | bytes 66561 | tf_op jit(solution)/shard_map/reduce_sum | solution.py:19
  46.0 0.9 %fusion.44 = f32[128]{0:T(128)S(1)} fusion(f32[1,256,128]{2,1,0:T(8,128)} %bitcast.556, f32[128]{0:T(128)S(1)} %bitcast.669), kind=kLoop, calls=%fused_computation.140 | loop fusion | flops 32640 | bytes 66560 | tf_op jit(solution)/shard_map/reduce_sum | solution.py:19
  47.1 1.1 %fusion.16 = f32[4,128]{1,0:T(4,128)S(1)} fusion(f32[4,256,128]{2,1,0:T(8,128)} %bitcast.536, f32[4,128]{1,0:T(4,128)S(1)} %bitcast.619), kind=kLoop, calls=%fused_computation.60 | loop fusion | flops 130560 | bytes 266240 | tf_op jit(solution)/shard_map/reduce_sum | solution.py:19
  48.9 2.5 %fusion.2 = f32[32,128]{1,0:T(8,128)S(1)} fusion(f32[32,256,128]{2,1,0:T(8,128)} %bitcast.526, f32[32,128]{1,0:T(8,128)S(1)} %bitcast.567), kind=kLoop, calls=%fused_computation.13 | loop fusion | flops 1044480 | bytes 2129920 | tf_op jit(solution)/shard_map/reduce_sum | solution.py:19
  51.5 1.2 %multiply_reduce_fusion.3 = f32[64,128]{1,0:T(8,128)S(1)} fusion(f32[64,128,128]{2,1,0:T(8,128)S(1)} %copy-done.3, f32[64,128]{1,0:T(8,128)S(1)} %bitcast.576), kind=kLoop, calls=%fused_computation.4 | loop fusion | flops 2088960 | bytes 4259840 | tf_op jit(solution)/shard_map/reduce_sum | solution.py:19
  53.0 1.2 %multiply_reduce_fusion.2 = f32[64,128]{1,0:T(8,128)S(1)} fusion(f32[64,128,128]{2,1,0:T(8,128)S(1)} %copy-done.1, f32[64,128]{1,0:T(8,128)S(1)} %fusion.91), kind=kLoop, calls=%fused_computation.3 | loop fusion | flops 2088960 | bytes 4259840 | tf_op jit(solution)/shard_map/reduce_sum | solution.py:19
  54.3 1.2 %multiply_reduce_fusion.1 = f32[64,128]{1,0:T(8,128)S(1)} fusion(f32[64,128,128]{2,1,0:T(8,128)S(1)} %copy-done.1, f32[64,128]{1,0:T(8,128)S(1)} %bitcast.577), kind=kLoop, calls=%fused_computation.2 | loop fusion | flops 2088960 | bytes 4259840 | tf_op jit(solution)/shard_map/reduce_sum | solution.py:19
  55.6 2.5 %multiply_reduce_fusion.6 = (f32[32,128]{1,0:T(8,128)S(1)}, f32[32,128,128]{2,1,0:T(8,128)S(1)}) fusion(f32[32,128]{1,0:T(8,128)S(1)} %bitcast.594, f32[32,2,128,128]{3,2,1,0:T(8,128)S(1)} %bitcast.523), kind=kOutput, calls=%fused_computation.17 | convolution fusion | flops 806350848 | bytes 6324224 | tf_op jit(solution)/shard_map/dot_general | solution.py:11
  58.2 1.4 %multiply_reduce_fusion.8 = (f32[16,128]{1,0:T(8,128)S(1)}, f32[16,128,128]{2,1,0:T(8,128)S(1)}) fusion(f32[16,128]{1,0:T(8,128)S(1)} %bitcast.616, f32[16,2,128,128]{3,2,1,0:T(8,128)S(1)} %bitcast.529), kind=kOutput, calls=%fused_computation.30 | convolution fusion | flops 403175424 | bytes 3162112 | tf_op jit(solution)/shard_map/dot_general | solution.py:11
  59.6 0.8 multiply_reduce_fusion.12
  61.9 10.0 %all-gather.3 = f32[8,129,128]{2,1,0:T(8,128)S(1)} all-gather(f32[1,129,128]{2,1,0:T(8,128)S(1)} %maximum_bitcast_fusion.1), channel_id=3, replica_groups=mesh['outer'=4,'inner'=8] {'inner'}, dimensions={0}, use_global_device_ids=true | all-gather | bytes 594432 | tf_op jit(solution)/shard_map/all_gather | solution.py:116
  73.7 2.6 %collective-permute-start.5 = (f32[129,128]{1,0:T(8,128)S(1)}, f32[129,128]{1,0:T(8,128)S(1)}, u32[]{:S(2)}, u32[]{:S(2)}) collective-permute-start(f32[129,128]{1,0:T(8,128)S(1)} %pad_maximum_fusion.1), channel_id=1, source_target_pairs={{0,8},{8,16},{16,24},{24,0},{1,9},{9,17},{17,25},{25,1},{2,10},{10... | collective-permute-start | bytes 198152 | tf_op jit(solution)/shard_map/ppermute | solution.py:110
  76.3 0.9 %collective-permute-start.4 = (f32[129,128]{1,0:T(8,128)S(1)}, f32[129,128]{1,0:T(8,128)S(1)}, u32[]{:S(2)}, u32[]{:S(2)}) collective-permute-start(f32[129,128]{1,0:T(8,128)S(1)} %pad_maximum_fusion.1), channel_id=1, source_target_pairs={{0,16},{8,24},{16,0},{24,8},{1,17},{9,25},{17,1},{25,9},{2,18},{10... | collective-permute-start | bytes 198152 | tf_op jit(solution)/shard_map/ppermute | solution.py:110
  77.2 1.5 %collective-permute-start.3 = (f32[129,128]{1,0:T(8,128)S(1)}, f32[129,128]{1,0:T(8,128)S(1)}, u32[]{:S(2)}, u32[]{:S(2)}) collective-permute-start(f32[129,128]{1,0:T(8,128)S(1)} %pad_maximum_fusion.1), channel_id=1, source_target_pairs={{0,24},{8,0},{16,8},{24,16},{1,25},{9,1},{17,9},{25,17},{2,26},{10... | collective-permute-start | bytes 198152 | tf_op jit(solution)/shard_map/ppermute | solution.py:110
  79.7 0.8 collective-permute-done.5
  80.7 2.4 %collective-permute-done.4 = f32[129,128]{1,0:T(8,128)S(1)} collective-permute-done((f32[129,128]{1,0:T(8,128)S(1)}, f32[129,128]{1,0:T(8,128)S(1)}, u32[]{:S(2)}, u32[]{:S(2)}) %collective-permute-start.4) | collective-permute-done | bytes 66080 | tf_op jit(solution)/shard_map/ppermute | solution.py:110
  85.4 1.2 %multiply_reduce_fusion = f32[64,128]{1,0:T(8,128)S(1)} fusion(f32[64,128,128]{2,1,0:T(8,128)S(1)} %copy-done.1, f32[64,128]{1,0:T(8,128)S(1)} %bitcast.578), kind=kLoop, calls=%fused_computation.1 | loop fusion | flops 2088960 | bytes 4259840 | tf_op jit(solution)/shard_map/reduce_sum | solution.py:19
  (191 shorter events, 16.8 us)
Async XLA Ops:
  0.6 3.7 %copy-start = (f32[128,128]{1,0:T(8,128)S(1)}, f32[128,128]{1,0:T(8,128)}, u32[]{:S(2)}) copy-start(f32[128,128]{1,0:T(8,128)} %param.10) | copy-start | bytes 196612
  0.6 3.7 %copy-start.7 = (f32[128,128]{1,0:T(8,128)S(1)}, f32[128,128]{1,0:T(8,128)}, u32[]{:S(2)}) copy-start(f32[128,128]{1,0:T(8,128)} %param.9) | copy-start | bytes 196612
  0.7 3.9 %copy-start.4 = (f32[64,128,128]{2,1,0:T(8,128)S(1)}, f32[64,128,128]{2,1,0:T(8,128)}, u32[]{:S(2)}) copy-start(f32[64,128,128]{2,1,0:T(8,128)} %param.7) | copy-start | bytes 12582916
  0.7 26.6 %copy-start.9 = (f32[128,128]{1,0:T(8,128)}, f32[128,128]{1,0:T(8,128)S(1)}, u32[]{:S(2)}) copy-start(f32[128,128]{1,0:T(8,128)S(1)} %fusion.48) | copy-start | bytes 196612
  8.6 4.2 %copy-start.2 = (f32[64,128,128]{2,1,0:T(8,128)}, f32[64,128,128]{2,1,0:T(8,128)S(1)}, u32[]{:S(2)}) copy-start(f32[64,128,128]{2,1,0:T(8,128)S(1)} %get-tuple-element.63) | copy-start | bytes 12582916
  13.6 0.8 copy-start.5
  15.3 12.0 %copy-start.6 = (f32[2,128,128]{2,1,0:T(8,128)}, f32[2,128,128]{2,1,0:T(8,128)S(1)}, u32[]{:S(2)}) copy-start(f32[2,128,128]{2,1,0:T(8,128)S(1)} %get-tuple-element.73) | copy-start | bytes 393220
  29.7 11.1 %collective-permute-start.2 = (f32[129,128]{1,0:T(8,128)}, f32[129,128]{1,0:T(8,128)}, u32[]{:S(2)}, u32[]{:S(2)}) collective-permute-start(f32[129,128]{1,0:T(8,128)} %pad_maximum_fusion), channel_id=1, source_target_pairs={{0,24},{8,0},{16,8},{24,16},{1,25},{9,1},{17,9},{25,17},{2,26},{10... | collective-permute-start | bytes 198152 | tf_op jit(solution)/shard_map/ppermute | solution.py:110
  33.3 9.2 %collective-permute-start.1 = (f32[129,128]{1,0:T(8,128)}, f32[129,128]{1,0:T(8,128)}, u32[]{:S(2)}, u32[]{:S(2)}) collective-permute-start(f32[129,128]{1,0:T(8,128)} %pad_maximum_fusion), channel_id=1, source_target_pairs={{0,16},{8,24},{16,0},{24,8},{1,17},{9,25},{17,1},{25,9},{2,18},{10... | collective-permute-start | bytes 198152 | tf_op jit(solution)/shard_map/ppermute | solution.py:110
  33.3 10.8 %collective-permute-start = (f32[129,128]{1,0:T(8,128)}, f32[129,128]{1,0:T(8,128)}, u32[]{:S(2)}, u32[]{:S(2)}) collective-permute-start(f32[129,128]{1,0:T(8,128)} %pad_maximum_fusion), channel_id=1, source_target_pairs={{0,8},{8,16},{16,24},{24,0},{1,9},{9,17},{17,25},{25,1},{2,10},{10... | collective-permute-start | bytes 198152 | tf_op jit(solution)/shard_map/ppermute | solution.py:110
  38.5 13.0 %copy-start.3 = (f32[64,128,128]{2,1,0:T(8,128)S(1)}, f32[64,128,128]{2,1,0:T(8,128)}, u32[]{:S(2)}) copy-start(f32[64,128,128]{2,1,0:T(8,128)} %copy-done.2) | copy-start | bytes 12582916
  48.2 4.5 %copy-start.8 = (f32[128,128]{1,0:T(8,128)S(1)}, f32[128,128]{1,0:T(8,128)}, u32[]{:S(2)}) copy-start(f32[128,128]{1,0:T(8,128)} %param.9) | copy-start | bytes 196612
  48.3 4.7 %copy-start.1 = (f32[64,128,128]{2,1,0:T(8,128)S(1)}, f32[64,128,128]{2,1,0:T(8,128)}, u32[]{:S(2)}) copy-start(f32[64,128,128]{2,1,0:T(8,128)} %param.8) | copy-start | bytes 12582916
  52.7 33.8 %copy-start.11 = (f32[64,128]{1,0:T(8,128)}, f32[64,128]{1,0:T(8,128)S(1)}, u32[]{:S(2)}) copy-start(f32[64,128]{1,0:T(8,128)S(1)} %add.376) | copy-start | bytes 98308
  58.1 13.7 %copy-start.13 = (pred[4,2]{1,0:T(4,128)(4,1)S(1)}, pred[4,2]{1,0:T(4,128)(4,1)}, u32[]{:S(2)}) copy-start(pred[4,2]{1,0:T(4,128)(4,1)} %fusion.50) | copy-start | bytes 28
  58.1 13.8 %copy-start.10 = (f32[128,128]{1,0:T(8,128)S(1)}, f32[128,128]{1,0:T(8,128)}, u32[]{:S(2)}) copy-start(f32[128,128]{1,0:T(8,128)} %copy-done.9) | copy-start | bytes 196612
  58.2 13.8 %copy-start.12 = (pred[8]{0:T(512)(128)(4,1)S(1)}, pred[8]{0:T(512)(128)(4,1)}, u32[]{:S(2)}) copy-start(pred[8]{0:T(512)(128)(4,1)} %iota_compare_fusion.1) | copy-start | bytes 28
  73.7 6.8 %collective-permute-start.5 = (f32[129,128]{1,0:T(8,128)S(1)}, f32[129,128]{1,0:T(8,128)S(1)}, u32[]{:S(2)}, u32[]{:S(2)}) collective-permute-start(f32[129,128]{1,0:T(8,128)S(1)} %pad_maximum_fusion.1), channel_id=1, source_target_pairs={{0,8},{8,16},{16,24},{24,0},{1,9},{9,17},{17,25},{25,1},{2,10},{10... | collective-permute-start | bytes 198152 | tf_op jit(solution)/shard_map/ppermute | solution.py:110
  76.3 6.8 %collective-permute-start.4 = (f32[129,128]{1,0:T(8,128)S(1)}, f32[129,128]{1,0:T(8,128)S(1)}, u32[]{:S(2)}, u32[]{:S(2)}) collective-permute-start(f32[129,128]{1,0:T(8,128)S(1)} %pad_maximum_fusion.1), channel_id=1, source_target_pairs={{0,16},{8,24},{16,0},{24,8},{1,17},{9,25},{17,1},{25,9},{2,18},{10... | collective-permute-start | bytes 198152 | tf_op jit(solution)/shard_map/ppermute | solution.py:110
  77.2 6.0 %collective-permute-start.3 = (f32[129,128]{1,0:T(8,128)S(1)}, f32[129,128]{1,0:T(8,128)S(1)}, u32[]{:S(2)}, u32[]{:S(2)}) collective-permute-start(f32[129,128]{1,0:T(8,128)S(1)} %pad_maximum_fusion.1), channel_id=1, source_target_pairs={{0,24},{8,0},{16,8},{24,16},{1,25},{9,1},{17,9},{25,17},{2,26},{10... | collective-permute-start | bytes 198152 | tf_op jit(solution)/shard_map/ppermute | solution.py:110
